TPU v7x, 256 devices: a whole 4x4x8 slice. The times are simulated.
256 devices in a mesh: seq: 64 (over y, z, core), head: 4 (over x).
Axes of the slice: x: 4, y: 4, z: 8, core: 2. Of those that a mesh axis runs over, the one named last changes fastest.
Arguments:
- tokens: bfloat16 [2, 64, 4096], P(None, None, 'seq'), may hold values from -6 to 6
- lengths: int32 [64], replicated, may hold values from 1 to 32768, as said below
- page_owner: int32 [2048], P('seq'), may hold values from -1 to 63, as said below
- page_number: int32 [2048], P('seq'), may hold values from 0 to 511, as said below
- key_pages: bfloat16 [2048, 64, 4096], P('seq', None, 'head'), may hold values from -600 to 600
- value_pages: bfloat16 [2048, 64, 4096], P('seq', None, 'head'), may hold values from -6 to 6
- alibi_slopes: float32 [32], P('head'), as said below
- norm1_gain: float32 [4096], P('seq'), may hold values from 0.1 to 1.9
- norm2_gain: float32 [4096], P('seq'), may hold values from 0.1 to 1.9
- w_qkv: bfloat16 [4096, 3, 4096], P('seq', None, 'head'), may hold values from -0.09375 to 0.09375
- w_out: bfloat16 [4096, 4096], P('seq', 'head'), may hold values from -0.09375 to 0.09375
- w_up: bfloat16 [4096, 16384], P('seq', 'head'), may hold values from -0.09375 to 0.09375
- w_down: bfloat16 [4096, 16384], P('seq', 'head'), may hold values from -0.046875 to 0.046875
Outputs:
- layer_out: bfloat16 [2, 64, 4096], P(None, None, 'seq')
Inputs may be any that keep to these rules, and one draw needn't show every extreme that they name: Exactly one request holds 32768 tokens; request r's cache fills page_number 0 .. ceil(lengths[r] / 64) - 1. `page_owner`: -1 marks a free slot; every page of every request stands in exactly one slot; on some indices of seq all 32 slots are used. `page_number`: 0 for free slots. `alibi_slopes`: Positive.
All inputs are finite; a program needn't handle non-finite values.
Results may differ from a plain program's by a relative error of at most 0.011.
Values may be sent and summed in bfloat16 or wider, within the bound.
No kernel may reach another device: no remote copies, remote signals or barrier semaphores. Data moves between devices by JAX's collectives and lax.ppermute only.
A program may use at most 128 MiB of HBM per device.

v0:
```python
import jax
import jax.numpy as jnp
from jax import lax
from jax.sharding import PartitionSpec as P

D = 4096
BLK = 8


eps_norm = 1e-05
floor_score = -1e30
highest = lax.Precision.HIGHEST


def normalize(token_rows, gain_share, totals, width_all):
    row_sum, row_squares = totals
    mean_value = row_sum / width_all
    variance = row_squares / width_all - mean_value * mean_value
    return (
        (token_rows.astype(jnp.float32) - mean_value[:, None])
        * lax.rsqrt(variance + eps_norm)[:, None]
        * gain_share[None, :]
    ).astype(jnp.bfloat16)


def page_block(
    carry_state, owners, number, key_block, value_block, queries, slopes, lengths, token_step
):
    run_max, run_sum, run_out = carry_state
    nblock, page_len, width_all = key_block.shape
    nheads = slopes.shape[0]
    head_size = width_all // nheads
    requests = queries.shape[0]
    safe_owner = jnp.clip(owners, 0, requests - 1)
    page_query = jnp.take(queries, safe_owner, axis=0)
    key_heads = key_block.reshape(nblock, page_len, nheads, head_size)
    value_heads = value_block.reshape(nblock, page_len, nheads, head_size)
    scores = jnp.einsum(
        "bhe,bthe->bth", page_query, key_heads, preferred_element_type=jnp.float32
    ) * head_size ** (-0.5)
    positions = number[:, None] * page_len + jnp.arange(page_len, dtype=jnp.int32)[None, :]
    own_length = jnp.take(lengths, safe_owner)
    distance = (own_length[:, None] + token_step - positions).astype(jnp.float32)
    scores = scores - distance[:, :, None] * slopes[None, None, :]
    valid_mask = (owners[:, None] >= 0) & (positions < own_length[:, None])
    masked = jnp.where(valid_mask[:, :, None], scores, floor_score)
    page_max = jnp.max(masked, axis=1)
    member = owners[None, :] == jnp.arange(requests, dtype=jnp.int32)[:, None]
    block_max = jnp.max(jnp.where(member[:, :, None], page_max[None, :, :], floor_score), axis=1)
    next_max = jnp.maximum(run_max, block_max)
    owner_max = jnp.take(next_max, safe_owner, axis=0)
    expon = jnp.where(valid_mask[:, :, None], jnp.exp(masked - owner_max[:, None, :]), 0.0)
    page_sum = jnp.sum(expon, axis=1)
    weights = expon.astype(jnp.bfloat16)
    page_out = jnp.einsum("bth,bthe->bhe", weights, value_heads, preferred_element_type=jnp.float32)
    member_float = member.astype(jnp.float32)
    rescale = jnp.exp(run_max - next_max)
    next_sum = run_sum * rescale + jnp.dot(member_float, page_sum, precision=highest)
    added = jnp.dot(member_float, page_out.reshape(nblock, nheads * head_size), precision=highest)
    next_out = run_out * rescale[:, :, None] + added.reshape(requests, nheads, head_size)
    return (next_max, next_sum, next_out)


def attend_new(carry_state, queries, new_keys, new_values, slopes, token_step):
    run_max, run_sum, run_out = carry_state
    head_size = queries.shape[2]
    for earlier in range(token_step + 1):
        scores = jnp.sum(
            queries.astype(jnp.float32) * new_keys[earlier].astype(jnp.float32), axis=2
        ) * head_size ** (-0.5)
        scores = scores - slopes[None, :] * float(token_step - earlier)
        next_max = jnp.maximum(run_max, scores)
        rescale = jnp.exp(run_max - next_max)
        expon = jnp.exp(scores - next_max)
        weights = lax.optimization_barrier(expon.astype(jnp.bfloat16)).astype(jnp.float32)
        run_sum = run_sum * rescale + expon
        run_out = run_out * rescale[:, :, None] + weights[:, :, None] * new_values[earlier].astype(
            jnp.float32
        )
        run_max = next_max
    attended = (run_out / run_sum[:, :, None]).astype(jnp.bfloat16)
    return attended.reshape(attended.shape[0], -1)


def on_device(
    tokens,
    lengths,
    page_owner,
    page_number,
    key_pages,
    value_pages,
    alibi_slopes,
    norm1_gain,
    norm2_gain,
    w_qkv,
    w_out,
    w_up,
    w_down,
):
    nsteps, requests, local_width = tokens.shape
    nheads = alibi_slopes.shape[0]
    head_width = key_pages.shape[2]
    head_size = head_width // nheads
    nblocks = key_pages.shape[0] // BLK
    qkv_width = w_qkv.shape[1] * w_qkv.shape[2]
    new_keys = []
    new_values = []
    outputs = []
    for token_step in range(nsteps):
        token_rows = tokens[token_step]
        token_float = token_rows.astype(jnp.float32)
        totals = lax.psum(
            (jnp.sum(token_float, axis=1), jnp.sum(token_float * token_float, axis=1)), "seq"
        )
        normed = normalize(token_rows, norm1_gain, totals, D)
        partial_qkv = jnp.dot(
            normed, w_qkv.reshape(local_width, qkv_width), preferred_element_type=jnp.float32
        )
        joined = lax.psum(partial_qkv, "seq").astype(jnp.bfloat16)
        queries = joined[:, :head_width].reshape(requests, nheads, head_size)
        new_keys.append(joined[:, head_width : 2 * head_width].reshape(requests, nheads, head_size))
        new_values.append(joined[:, 2 * head_width :].reshape(requests, nheads, head_size))
        carry_state = (
            jnp.full((requests, nheads), floor_score, jnp.float32),
            jnp.zeros((requests, nheads), jnp.float32),
            jnp.zeros((requests, nheads, head_size), jnp.float32),
        )

        def visit(turn_index, state_in):
            first_page = (turn_index * BLK).astype(jnp.int32)
            owners = lax.dynamic_slice_in_dim(page_owner, first_page, BLK, 0)
            number = lax.dynamic_slice_in_dim(page_number, first_page, BLK, 0)
            key_block = lax.dynamic_slice_in_dim(key_pages, first_page, BLK, 0)
            value_block = lax.dynamic_slice_in_dim(value_pages, first_page, BLK, 0)

            def compute(state_given):
                return page_block(
                    state_given,
                    owners,
                    number,
                    key_block,
                    value_block,
                    queries,
                    alibi_slopes,
                    lengths,
                    token_step,
                )

            def keep_state(state_given):
                return state_given

            return lax.cond(jnp.any(owners >= 0), compute, keep_state, state_in)

        carry_state = lax.fori_loop(0, nblocks, visit, carry_state)
        run_max, run_sum, run_out = carry_state
        top_max = lax.pmax(run_max, "seq")
        rescale = jnp.exp(run_max - top_max)
        run_sum, run_out = lax.psum((run_sum * rescale, run_out * rescale[:, :, None]), "seq")
        run_max = top_max
        attended = attend_new(
            (run_max, run_sum, run_out), queries, new_keys, new_values, alibi_slopes, token_step
        )
        projected = lax.psum(
            lax.dot_general(
                attended, w_out, (((1,), (1,)), ((), ())), preferred_element_type=jnp.float32
            ),
            "head",
        )
        hidden_in = (token_float + projected).astype(jnp.bfloat16)
        hidden_float = hidden_in.astype(jnp.float32)
        totals_two = lax.psum(
            (jnp.sum(hidden_float, axis=1), jnp.sum(hidden_float * hidden_float, axis=1)), "seq"
        )
        normed_two = normalize(hidden_in, norm2_gain, totals_two, D)
        up_proj = jnp.dot(normed_two, w_up, preferred_element_type=jnp.float32)
        up_share = lax.psum_scatter(up_proj, "seq", scatter_dimension=1, tiled=True)
        hidden_share = jax.nn.gelu(up_share, approximate=False).astype(jnp.bfloat16)
        down_part = lax.dot_general(
            lax.all_gather(hidden_share, "seq", axis=1, tiled=True),
            w_down,
            (((1,), (1,)), ((), ())),
            preferred_element_type=jnp.float32,
        )
        down_proj = lax.psum(down_part, "head")
        outputs.append((hidden_float + down_proj).astype(jnp.bfloat16))
    return jnp.stack(outputs)


def solution(mesh):
    placed = (
        P(None, None, "seq"),
        P(),
        P("seq"),
        P("seq"),
        P("seq", None, "head"),
        P("seq", None, "head"),
        P("head"),
        P("seq"),
        P("seq"),
        P("seq", None, "head"),
        P("seq", "head"),
        P("seq", "head"),
        P("seq", "head"),
    )
    return jax.shard_map(
        on_device, mesh=mesh, in_specs=placed, out_specs=P(None, None, "seq"), check_vma=False
    )
```

profile of v0, /device:TPU:4, one launch (start us, length us, event | category | flops | bytes accessed | tf_op | source)
XLA Modules:
  0.0 1269.4 jit_solution(11729159161762872882)
XLA Ops:
  6.6 0.9 fusion.62
  7.5 0.9 convert_reduce_fusion.3
  8.4 1.0 copy.122
  9.4 131.8 %all-reduce.3 = (f32[64]{0:T(128)S(1)}, f32[64]{0:T(128)S(1)}, f32[64]{0:T(128)S(1)}, f32[64]{0:T(128)S(1)}) all-reduce(f32[64]{0:T(128)S(1)} %get-tuple-element.600, f32[64]{0:T(128)S(1)} %get-tuple-element.598, f32[64]{0:T(128)S(1)} %get-tuple-element.599, f32[64]{0:T(128)S(1)} %get-tuple-element.597), channel_id=1, replica_groups=mesh['seq'=64,'head'=4] {'seq'}, use_global_device_ids=true, to_apply=%region_27.31 | all-reduce | flops 256 | bytes 2048 | tf_op jit(solution)/shard_map/psum | solution.py:112
  141.2 1.0 fusion.105
  142.2 1.0 fusion.108
  143.3 260.9 %all-reduce.12 = (bf16[64,3072]{1,0:T(8,128)(2,1)S(1)}, bf16[64,3072]{1,0:T(8,128)(2,1)S(1)}) all-reduce(f32[64,3072]{1,0:T(8,128)S(1)} %fusion.105, f32[64,3072]{1,0:T(8,128)S(1)} %fusion.108), channel_id=1, replica_groups=mesh['seq'=64,'head'=4] {'seq'}, use_global_device_ids=true, to_apply=%region_28.32 | all-reduce | flops 393216 | bytes 2359296 | tf_op jit(solution)/shard_map/psum | solution.py:119
  404.2 0.7 convert_bitcast_fusion.2
  405.6 0.8 convert_bitcast_fusion
  406.5 18.2 %while.35 = (s32[]{:T(128)}, f32[64,8]{0,1:T(8,128)S(1)}, f32[64,8]{0,1:T(8,128)S(1)}, f32[64,8,128]{2,0,1:T(8,128)S(1)}, s32[32]{0:T(128)S(1)}, /*index=5*/s32[...) while((s32[]{:T(128)}, f32[64,8]{0,1:T(8,128)S(1)}, ...), condition=%wide.region_36.40_spmd, body=%wide.region_29.39_spmd.sunk | while | flops 8645702 | bytes 7067565 | solution.py:154
  406.5 0.8 compare_reduce_fusion.5
  407.9 6.2 conditional.5
  407.9 1.8 dynamic-slice_bitcast_fusion.2
  414.2 0.8 compare_reduce_fusion.5
  415.6 6.2 conditional.5
  415.6 1.8 dynamic-slice_bitcast_fusion.2
  421.9 0.8 compare_reduce_fusion.5
  423.3 0.8 compare_reduce_fusion.5
  425.4 19.9 %while.34 = (s32[]{:T(128)}, f32[64,8]{0,1:T(8,128)S(1)}, f32[64,8]{0,1:T(8,128)S(1)}, f32[64,8,128]{2,0,1:T(8,128)S(1)}, s32[32]{0:T(128)S(1)}, /*index=5*/s32[...) while((s32[]{:T(128)}, f32[64,8]{0,1:T(8,128)S(1)}, ...), condition=%wide.region_12.16_spmd, body=%wide.region_5.15_spmd.sunk | while | flops 8645694 | bytes 7067533 | solution.py:154
  425.4 0.7 compare_reduce_fusion.4
  426.8 7.1 conditional.4
  426.8 1.8 dynamic-slice_bitcast_fusion
  428.6 1.5 gather_fusion.1
  433.9 0.7 compare_reduce_fusion.4
  435.3 7.1 conditional.4
  435.3 1.8 dynamic-slice_bitcast_fusion
  437.1 1.5 gather_fusion.1
  442.5 0.7 compare_reduce_fusion.4
  443.9 0.7 compare_reduce_fusion.4
  445.3 147.1 %all-reduce.5 = (f32[64,8]{0,1:T(8,128)S(1)}, f32[64,8]{0,1:T(8,128)S(1)}) all-reduce(f32[64,8]{0,1:T(8,128)S(1)} %get-tuple-element.592, f32[64,8]{0,1:T(8,128)S(1)} %get-tuple-element.589), channel_id=1, replica_groups=mesh['seq'=64,'head'=4] {'seq'}, use_global_device_ids=true, to_apply=%region_37.41 | all-reduce | flops 1024 | bytes 8192 | tf_op jit(solution)/shard_map/pmax | solution.py:156
  592.5 0.9 broadcast_multiply_fusion
  593.3 0.8 broadcast_multiply_fusion.1
  594.3 1.0 copy.128
  595.3 1.3 multiply_reduce_fusion
  596.8 126.5 %all-reduce.1 = (f32[64,8]{0,1:T(8,128)S(1)}, f32[64,8]{0,1:T(8,128)S(1)}) all-reduce(f32[64,8]{0,1:T(8,128)S(1)} %get-tuple-element.689, f32[64,8]{0,1:T(8,128)S(1)} %get-tuple-element.687), channel_id=1, replica_groups=mesh['seq'=64,'head'=4] {'seq'}, use_global_device_ids=true, to_apply=%region_41.45 | all-reduce | flops 1024 | bytes 8192 | tf_op jit(solution)/shard_map/psum | solution.py:158
  723.4 48.1 %all-reduce.11.cloned.1.call-done = (f32[64,8,128]{2,0,1:T(8,128)}, f32[64,8,128]{2,0,1:T(8,128)}) async-done(((f32[64,8,128]{2,0,1:T(8,128)}, f32[64,8,128]{2,0,1:T(8,128)}), (f32[64,8,128]{2,0,1:T(8,128)}, f32[64,8,128]{2,0,1:T(8,128)})) %all-reduce.11.cloned.1.call-update) | async-done | bytes 524304 | tf_op jit(solution)/shard_map/psum | solution.py:158
  771.5 1.8 fusion.54
  773.6 16.0 %all-reduce.7 = (f32[64,64]{1,0:T(8,128)S(1)}, f32[64,64]{1,0:T(8,128)S(1)}) all-reduce(f32[64,64]{1,0:T(8,128)S(1)} %fusion.48, f32[64,64]{1,0:T(8,128)S(1)} %fusion.51), channel_id=1, replica_groups=mesh['seq'=64,'head'=4] {'head'}, use_global_device_ids=true, to_apply=%region_42.46 | all-reduce | flops 8192 | bytes 65536 | tf_op jit(solution)/shard_map/psum | solution.py:163
  789.8 124.1 %all-reduce = (f32[64]{0:T(128)S(1)}, f32[64]{0:T(128)S(1)}, f32[64]{0:T(128)S(1)}, f32[64]{0:T(128)S(1)}) all-reduce(f32[64]{0:T(128)S(1)} %get-tuple-element.712, f32[64]{0:T(128)S(1)} %get-tuple-element.713, f32[64]{0:T(128)S(1)} %get-tuple-element.602, f32[64]{0:T(128)S(1)} %get-tuple-element.601), channel_id=1, replica_groups=mesh['seq'=64,'head'=4] {'seq'}, use_global_device_ids=true, to_apply=%region_46.50 | all-reduce | flops 256 | bytes 2048 | tf_op jit(solution)/shard_map/psum | solution.py:171
  913.9 1.9 convolution_bitcast_fusion
  915.9 1.9 convolution_bitcast_fusion.1
  917.8 133.4 %reduce-scatter.9.cloned.1.call-done = f32[64,64]{1,0:T(8,128)} async-done(((f32[4096,64]{1,0:T(8,128)}), f32[64,64]{1,0:T(8,128)}) %reduce-scatter.9.cloned.1.call-update) | async-done | bytes 16400
  1051.2 0.8 copy.113
  1052.2 49.1 %all_gather.7 = bf16[64,4096]{0,1:T(8,128)(2,1)S(1)} all-gather(bf16[64,64]{0,1:T(8,128)(2,1)S(1)} %copy.97), channel_id=1, replica_groups=mesh['seq'=64,'head'=4] {'seq'}, dimensions={1}, use_global_device_ids=true | all-gather | bytes 532480 | tf_op jit(solution)/shard_map/all_gather | solution.py:179
  1101.3 93.8 %reduce-scatter.7.cloned.1.call-done = f32[64,64]{1,0:T(8,128)} async-done(((f32[4096,64]{1,0:T(8,128)}), f32[64,64]{1,0:T(8,128)}) %reduce-scatter.7.cloned.1.call-update) | async-done | bytes 16400
  1195.1 0.8 copy.111
  1196.1 49.3 %all_gather.6 = bf16[64,4096]{0,1:T(8,128)(2,1)S(1)} all-gather(bf16[64,64]{0,1:T(8,128)(2,1)S(1)} %copy.91), channel_id=1, replica_groups=mesh['seq'=64,'head'=4] {'seq'}, dimensions={1}, use_global_device_ids=true | all-gather | bytes 532480 | tf_op jit(solution)/shard_map/all_gather | solution.py:179
  1246.3 16.0 %all-reduce.6 = (f32[64,64]{1,0:T(8,128)S(1)}, f32[64,64]{1,0:T(8,128)S(1)}) all-reduce(f32[64,64]{1,0:T(8,128)S(1)} %fusion.138, f32[64,64]{1,0:T(8,128)S(1)} %fusion.137), channel_id=1, replica_groups=mesh['seq'=64,'head'=4] {'head'}, use_global_device_ids=true, to_apply=%region_48.52 | all-reduce | flops 8192 | bytes 65536 | tf_op jit(solution)/shard_map/psum | solution.py:184
  (142 shorter events, 20.8 us)
Async XLA Ops:
  6.5 907.3 %copy-start = (bf16[64,4096]{1,0:T(8,128)(2,1)S(1)}, bf16[64,4096]{1,0:T(8,128)(2,1)}, u32[]{:S(2)}) copy-start(bf16[64,4096]{1,0:T(8,128)(2,1)} %param.38) | copy-start | bytes 1572868
  6.5 399.9 %copy-start.6 = (f32[8]{0:T(128)S(1)}, f32[8]{0:T(128)}, u32[]{:S(2)}) copy-start(f32[8]{0:T(128)} %param.33) | copy-start | bytes 100
  6.5 399.9 %copy-start.8 = (s32[32]{0:T(128)S(1)}, s32[32]{0:T(128)}, u32[]{:S(2)}) copy-start(s32[32]{0:T(128)} %param.29) | copy-start | bytes 388
  6.5 399.9 %copy-start.7 = (s32[32]{0:T(128)S(1)}, s32[32]{0:T(128)}, u32[]{:S(2)}) copy-start(s32[32]{0:T(128)} %param.30) | copy-start | bytes 388
  6.5 400.0 %copy-start.1 = (s32[64]{0:T(128)S(1)}, s32[64]{0:T(128)}, u32[]{:S(2)}) copy-start(s32[64]{0:T(128)} %param.28) | copy-start | bytes 772
  6.5 764.9 %all-reduce.11.cloned.1.call-start = ((), (), s32[]{:S(2)}) async-start(), calls=%async_computation.4 | async-start | bytes 1048576 | tf_op jit(solution)/shard_map/psum | solution.py:158
  424.7 0.7 copy-start.3
  445.3 328.0 %copy-start.5 = (bf16[64,1024]{1,0:T(8,128)(2,1)S(1)}, bf16[64,1024]{1,0:T(8,128)(2,1)}, u32[]{:S(2)}) copy-start(bf16[64,1024]{1,0:T(8,128)(2,1)} %param.37) | copy-start | bytes 393220
  445.3 344.3 %copy-start.4 = (bf16[2,64,64]{2,1,0:T(8,128)(2,1)S(1)}, bf16[2,64,64]{2,1,0:T(8,128)(2,1)}, u32[]{:S(2)}) copy-start(bf16[2,64,64]{2,1,0:T(8,128)(2,1)} %param.27) | copy-start | bytes 49156
  445.3 468.5 %copy-start.9 = (f32[64]{0:T(128)S(1)}, f32[64]{0:T(128)}, u32[]{:S(2)}) copy-start(f32[64]{0:T(128)} %param.35) | copy-start | bytes 772
  594.2 457.0 %reduce-scatter.9.cloned.1.call-start = ((), (), s32[]{:S(2)}) async-start(), calls=%async_computation.3 | async-start | bytes 2129920
  915.8 329.6 %copy-start.2 = (bf16[64,4096]{1,0:T(8,128)(2,1)S(1)}, bf16[64,4096]{1,0:T(8,128)(2,1)}, u32[]{:S(2)}) copy-start(bf16[64,4096]{1,0:T(8,128)(2,1)} %param.39) | copy-start | bytes 1572868
  915.8 279.2 %reduce-scatter.7.cloned.1.call-start = ((), (), s32[]{:S(2)}) async-start(), calls=%async_computation.2 | async-start | bytes 2129920
Sparse Core Ops, SparseCore 0:
  594.3 177.1 all-reduce.10
  915.9 135.1 reduce-scatter.8
  1055.2 139.7 reduce-scatter.6
where the time goes:
time: 1270 us
  blocking collectives  921 us (73%)
  waiting for transfers between devices  275 us (22%)
  local copies, waits for them, and re-layouts  21.9 us (2%)
  other arithmetic  18.8 us (1%)
  matrix products  13.6 us (1%)
  between operations  13.5 us (1%)
    psum x1, blocking collectives, on_device(): joined = lax.psum(partial_qkv, 'seq').astype(jnp.bfloat16)  261 us
    unnamed x5, waiting for transfers between devices  227 us
    pmax x1, blocking collectives, on_device(): top_max = lax.pmax(run_max, 'seq')  147 us
    psum x1, blocking collectives, on_device(): lax.psum((jnp.sum(token_float, axis=1), jnp.sum(token_float * token_float...  132 us
    psum x1, blocking collectives, on_device(): lax.psum((run_sum * rescale, run_out * rescale[:, :, None]), 'seq')  126 us
    psum x1, blocking collectives, on_device(): lax.psum((jnp.sum(hidden_float, axis=1), jnp.sum(hidden_float * hidden_fl...  124 us
    all_gather x2, blocking collectives, on_device(): lax.all_gather(hidden_share, 'seq', axis=1, tiled=True)  98.4 us
    psum x1, waiting for transfers between devices, on_device(): lax.psum((run_sum * rescale, run_out * rescale[:, :, None]), 'seq')  48.1 us
  transfers between devices with their start and end apart: 3, of which 3 were waited for; matrix products, arithmetic and copies ran while one was open for 0% of the time, Pallas kernels for 0%

commit v1 on v0

--- a/solution.py
+++ b/solution.py
@@ -1,3 +1,5 @@
+import functools
+
 import jax
 import jax.numpy as jnp
 from jax import lax
@@ -82,6 +84,35 @@
     return attended.reshape(attended.shape[0], -1)
 
 
+def gather_cols(part, axis_name):
+    return lax.all_gather(part, axis_name, axis=1, tiled=True)
+
+
+def full_normalize(rows, gain_full):
+    row_float = rows.astype(jnp.float32)
+    totals = (jnp.sum(row_float, axis=1), jnp.sum(row_float * row_float, axis=1))
+    return normalize(rows, gain_full, totals, rows.shape[1])
+
+
+def butterfly_combine(state, nseq):
+    my_index = lax.axis_index("seq")
+    stride = 1
+    while stride < nseq:
+        pairs = [(i, i ^ stride) for i in range(nseq)]
+        other = lax.ppermute(state, "seq", pairs)
+        low = (my_index & stride) == 0
+        first = tuple(jnp.where(low, a, b) for a, b in zip(state, other))
+        second = tuple(jnp.where(low, b, a) for a, b in zip(state, other))
+        top = jnp.maximum(first[0], second[0])
+        scale_a = jnp.exp(first[0] - top)
+        scale_b = jnp.exp(second[0] - top)
+        total = first[1] * scale_a + second[1] * scale_b
+        out = first[2] * scale_a[:, :, None] + second[2] * scale_b[:, :, None]
+        state = (top, total, out)
+        stride *= 2
+    return state
+
+
 def on_device(
     tokens,
     lengths,
@@ -96,6 +127,7 @@
     w_out,
     w_up,
     w_down,
+    nseq,
 ):
     nsteps, requests, local_width = tokens.shape
     nheads = alibi_slopes.shape[0]
@@ -103,23 +135,24 @@
     head_size = head_width // nheads
     nblocks = key_pages.shape[0] // BLK
     qkv_width = w_qkv.shape[1] * w_qkv.shape[2]
-    new_keys = []
-    new_values = []
-    outputs = []
+    rows = nsteps * requests
+
+    qkv_cols = lax.all_to_all(w_qkv.reshape(local_width, qkv_width), "seq", 1, 0, tiled=True)
+    up_cols = lax.all_to_all(w_up, "seq", 1, 0, tiled=True)
+    gains = lax.all_gather(jnp.stack([norm1_gain, norm2_gain]), "seq", axis=1, tiled=True)
+
+    token_rows = tokens.reshape(rows, local_width)
+    token_float = token_rows.astype(jnp.float32)
+    normed = full_normalize(gather_cols(token_rows, "seq"), gains[0])
+    qkv_part = jnp.dot(normed, qkv_cols, preferred_element_type=jnp.float32).astype(jnp.bfloat16)
+    joined = gather_cols(qkv_part, "seq")
+    all_queries = joined[:, :head_width].reshape(nsteps, requests, nheads, head_size)
+    new_keys = joined[:, head_width : 2 * head_width].reshape(nsteps, requests, nheads, head_size)
+    new_values = joined[:, 2 * head_width :].reshape(nsteps, requests, nheads, head_size)
+
+    states = []
     for token_step in range(nsteps):
-        token_rows = tokens[token_step]
-        token_float = token_rows.astype(jnp.float32)
-        totals = lax.psum(
-            (jnp.sum(token_float, axis=1), jnp.sum(token_float * token_float, axis=1)), "seq"
-        )
-        normed = normalize(token_rows, norm1_gain, totals, D)
-        partial_qkv = jnp.dot(
-            normed, w_qkv.reshape(local_width, qkv_width), preferred_element_type=jnp.float32
-        )
-        joined = lax.psum(partial_qkv, "seq").astype(jnp.bfloat16)
-        queries = joined[:, :head_width].reshape(requests, nheads, head_size)
-        new_keys.append(joined[:, head_width : 2 * head_width].reshape(requests, nheads, head_size))
-        new_values.append(joined[:, 2 * head_width :].reshape(requests, nheads, head_size))
+        queries = all_queries[token_step]
         carry_state = (
             jnp.full((requests, nheads), floor_score, jnp.float32),
             jnp.zeros((requests, nheads), jnp.float32),
@@ -151,39 +184,41 @@
 
             return lax.cond(jnp.any(owners >= 0), compute, keep_state, state_in)
 
-        carry_state = lax.fori_loop(0, nblocks, visit, carry_state)
-        run_max, run_sum, run_out = carry_state
-        top_max = lax.pmax(run_max, "seq")
-        rescale = jnp.exp(run_max - top_max)
-        run_sum, run_out = lax.psum((run_sum * rescale, run_out * rescale[:, :, None]), "seq")
-        run_max = top_max
-        attended = attend_new(
-            (run_max, run_sum, run_out), queries, new_keys, new_values, alibi_slopes, token_step
+        states.append(lax.fori_loop(0, nblocks, visit, carry_state))
+
+    joined_state = tuple(jnp.concatenate(parts, axis=0) for parts in zip(*states))
+    run_max, run_sum, run_out = butterfly_combine(joined_state, nseq)
+    attended = []
+    for token_step in range(nsteps):
+        picked = slice(token_step * requests, (token_step + 1) * requests)
+        attended.append(
+            attend_new(
+                (run_max[picked], run_sum[picked], run_out[picked]),
+                all_queries[token_step],
+                new_keys,
+                new_values,
+                alibi_slopes,
+                token_step,
+            )
         )
-        projected = lax.psum(
-            lax.dot_general(
-                attended, w_out, (((1,), (1,)), ((), ())), preferred_element_type=jnp.float32
-            ),
-            "head",
-        )
-        hidden_in = (token_float + projected).astype(jnp.bfloat16)
-        hidden_float = hidden_in.astype(jnp.float32)
-        totals_two = lax.psum(
-            (jnp.sum(hidden_float, axis=1), jnp.sum(hidden_float * hidden_float, axis=1)), "seq"
-        )
-        normed_two = normalize(hidden_in, norm2_gain, totals_two, D)
-        up_proj = jnp.dot(normed_two, w_up, preferred_element_type=jnp.float32)
-        up_share = lax.psum_scatter(up_proj, "seq", scatter_dimension=1, tiled=True)
-        hidden_share = jax.nn.gelu(up_share, approximate=False).astype(jnp.bfloat16)
-        down_part = lax.dot_general(
-            lax.all_gather(hidden_share, "seq", axis=1, tiled=True),
-            w_down,
-            (((1,), (1,)), ((), ())),
-            preferred_element_type=jnp.float32,
-        )
-        down_proj = lax.psum(down_part, "head")
-        outputs.append((hidden_float + down_proj).astype(jnp.bfloat16))
-    return jnp.stack(outputs)
+    attended = jnp.concatenate(attended, axis=0)
+    projected = lax.psum(
+        lax.dot_general(attended, w_out, (((1,), (1,)), ((), ())), preferred_element_type=jnp.float32),
+        "head",
+    )
+    hidden_in = (token_float + projected).astype(jnp.bfloat16)
+    hidden_float = hidden_in.astype(jnp.float32)
+    normed_two = full_normalize(gather_cols(hidden_in, "seq"), gains[1])
+    up_share = jnp.dot(normed_two, up_cols, preferred_element_type=jnp.float32)
+    hidden_share = jax.nn.gelu(up_share, approximate=False).astype(jnp.bfloat16)
+    down_part = lax.dot_general(
+        gather_cols(hidden_share, "seq"),
+        w_down,
+        (((1,), (1,)), ((), ())),
+        preferred_element_type=jnp.float32,
+    )
+    down_proj = lax.psum(down_part, "head")
+    return (hidden_float + down_proj).astype(jnp.bfloat16).reshape(nsteps, requests, local_width)
 
 
 def solution(mesh):
@@ -202,6 +237,7 @@
         P("seq", "head"),
         P("seq", "head"),
     )
+    nseq = mesh.shape["seq"]
     return jax.shard_map(
-        on_device, mesh=mesh, in_specs=placed, out_specs=P(None, None, "seq"), check_vma=False
-    )
+        functools.partial(on_device, nseq=nseq), mesh=mesh, in_specs=placed, out_specs=P(None, None, "seq"), check_vma=False
+    )

time: 1270 us -> 522 us (0.41)
  blocking collectives: 921 us -> 152 us
  starting transfers between devices: 0.12 us -> 67.5 us
  waiting for transfers between devices: 275 us -> 213 us
    psum x4 -> x0, blocking collectives: 643 us -> none  [the longest x1 261 us: on_device(): joined = lax.psum(partial_qkv, 'seq').astype(jnp.bfloat16)]
    unnamed x5 -> x3, waiting for transfers between devices: 227 us -> 0.05 us
    pmax x1 -> x0, blocking collectives: 147 us -> none  [on_device(): top_max = lax.pmax(run_max, 'seq')]
    all_gather x0 -> x3, waiting for transfers between devices: none -> 140 us  [gather_cols(): return lax.all_gather(part, axis_name, axis=1, tiled=True)]
    ppermute x0 -> x18, waiting for transfers between devices: none -> 72.8 us  [butterfly_combine(): other = lax.ppermute(state, 'seq', pairs)]
    ppermute x0 -> x18, starting transfers between devices: none -> 55.1 us  [butterfly_combine(): other = lax.ppermute(state, 'seq', pairs)]
    psum x1 -> x0, waiting for transfers between devices: 48.1 us -> none  [on_device(): lax.psum((run_sum * rescale, run_out * rescale[:, :, None]), 'seq')]
    all_to_all x0 -> x1, blocking collectives: none -> 25 us  [on_device(): up_cols = lax.all_to_all(w_up, 'seq', 1, 0, tiled=True)]
  transfers between devices with their start and end apart: 3 -> 22, of which waited for: 3 -> 11; matrix products, arithmetic and copies ran while one was open for 0% -> 1% of each run, Pallas kernels for 0% -> 0%
where the time goes in v1:
time: 522 us; the launch traced here: 520 us
  waiting for transfers between devices  213 us (41%)
  blocking collectives  152 us (29%)
  starting transfers between devices  67.5 us (13%)
  local copies, waits for them, and re-layouts  34.1 us (7%)
  other arithmetic  21.4 us (4%)
  between operations  13.6 us (3%)
  matrix products  12.9 us (2%)
  loops' own time  5.68 us (1%)
    all_gather x3, waiting for transfers between devices, gather_cols(): return lax.all_gather(part, axis_name, axis=1, tiled=True)  140 us
    ppermute x18, waiting for transfers between devices, butterfly_combine(): other = lax.ppermute(state, 'seq', pairs)  72.8 us
    ppermute x18, starting transfers between devices, butterfly_combine(): other = lax.ppermute(state, 'seq', pairs)  55.1 us
    all_gather x1, blocking collectives, gather_cols(): return lax.all_gather(part, axis_name, axis=1, tiled=True)  49.2 us
    all_gather x1, blocking collectives, on_device(): lax.all_gather(jnp.stack([norm1_gain, norm2_gain]), 'seq', axis=1, tiled=...  47 us
    all_to_all x1, blocking collectives, on_device(): up_cols = lax.all_to_all(w_up, 'seq', 1, 0, tiled=True)  25 us
    psum x1, blocking collectives, on_device(): down_proj = lax.psum(down_part, 'head')  15.5 us
    psum x1, blocking collectives, on_device(): lax.psum(lax.dot_general(attended, w_out, (((1,), (1,)), ((), ())), prefe...  15.4 us
  transfers between devices with their start and end apart: 22, of which 11 were waited for; matrix products, arithmetic and copies ran while one was open for 1% of the time, Pallas kernels for 0%

profile of v1, /device:TPU:4, one launch (start us, length us, event | category | flops | bytes accessed | tf_op | source)
XLA Modules:
  0.0 520.3 jit_solution(8866509199030743355)
XLA Ops:
  6.5 1.5 copy.88
  8.1 1.4 copy.64
  9.5 1.2 reshape.450
  10.7 12.1 %all-to-all-start = ((bf16[64,2,1536]{2,1,0:T(2,128)(2,1)}), bf16[64,2,1536]{2,1,0:T(2,128)(2,1)S(1)}, u32[]{:S(2)}, u32[]{:S(2)}) async-start(bf16[64,2,1536]{2,1,0:T(2,128)(2,1)} %reshape.450), calls=%async_computation | async-start | bytes 786432 | tf_op jit(solution)/shard_map/all_to_all | solution.py:140
  22.9 47.0 %all-gather = f32[64,64,2]{1,2,0:T(2,128)S(1)} all-gather(f32[1,64,2]{1,2,0:T(2,128)S(1)} %maximum_bitcast_fusion), channel_id=1, replica_groups=mesh['seq'=64,'head'=4] {'seq'}, dimensions={0}, use_global_device_ids=true | all-gather | bytes 33280 | tf_op jit(solution)/shard_map/all_gather | solution.py:142
  71.4 18.6 %all-gather.5.cloned.1.call-done = bf16[128,4096]{0,1:T(8,128)(2,1)} async-done(((bf16[128,64]{0,1:T(8,128)(2,1)}), bf16[128,4096]{0,1:T(8,128)(2,1)}) %all-gather.5.cloned.1.call-update) | async-done | bytes 1048592 | tf_op jit(solution)/shard_map/all_gather | solution.py:88
  90.0 1.8 convert_reduce_fusion.1
  91.7 2.0 convolution_convert_fusion
  93.8 49.2 %all_gather.17 = bf16[128,3072]{0,1:T(8,128)(2,1)S(1)} all-gather(bf16[128,48]{0,1:T(8,128)(2,1)S(1)} %convolution_convert_fusion), channel_id=1, replica_groups=mesh['seq'=64,'head'=4] {'seq'}, dimensions={1}, use_global_device_ids=true | all-gather | bytes 798720 | tf_op jit(solution)/shard_map/all_gather | solution.py:88
  144.9 19.9 %while.35 = (s32[]{:T(128)}, f32[64,8]{0,1:T(8,128)S(1)}, f32[64,8]{0,1:T(8,128)S(1)}, f32[64,8,128]{2,0,1:T(8,128)S(1)}, s32[32]{0:T(128)S(1)}, /*index=5*/s32[...) while((s32[]{:T(128)}, f32[64,8]{0,1:T(8,128)S(1)}, ...), condition=%wide.region_17.21_spmd, body=%wide.region_10.20_spmd.sunk | while | flops 8645702 | bytes 7067557 | solution.py:187
  146.3 7.1 %conditional.5 = ((f32[64,8]{0,1:T(8,128)S(1)}, f32[64,8]{0,1:T(8,128)S(1)}, f32[64,8,128]{2,0,1:T(8,128)S(1)})) conditional(s32[]{:T(128)} %convert_element_type.230, (f32[64,8]{0,1:T(8,128)S(1)}, f32[64,8]{0,1:T(8,128)S(1)}, f32[64,8,128]{2,0,1:T(8,128)S(1)}) %tuple.149, (s32[8]{0:T(128)S(1)}, s32[32]{0:T(128)S(1)}, s32[]{:T(128)}, ...), branch_computations={%region_12.15_spmd, %region_13.19_spmd} | conditional | flops 8645680 | bytes 7067184 | solution.py:185
  146.4 1.5 gather_fusion.4
  148.8 1.8 dynamic-slice_bitcast_fusion.2
  154.8 7.1 %conditional.5 = ((f32[64,8]{0,1:T(8,128)S(1)}, f32[64,8]{0,1:T(8,128)S(1)}, f32[64,8,128]{2,0,1:T(8,128)S(1)})) conditional(s32[]{:T(128)} %convert_element_type.230, (f32[64,8]{0,1:T(8,128)S(1)}, f32[64,8]{0,1:T(8,128)S(1)}, f32[64,8,128]{2,0,1:T(8,128)S(1)}) %tuple.149, (s32[8]{0:T(128)S(1)}, s32[32]{0:T(128)S(1)}, s32[]{:T(128)}, ...), branch_computations={%region_12.15_spmd, %region_13.19_spmd} | conditional | flops 8645680 | bytes 7067184 | solution.py:185
  154.9 1.5 gather_fusion.4
  157.3 1.8 dynamic-slice_bitcast_fusion.2
  165.6 19.9 %while.34 = (s32[]{:T(128)}, f32[64,8]{0,1:T(8,128)S(1)}, f32[64,8]{0,1:T(8,128)S(1)}, f32[64,8,128]{2,0,1:T(8,128)S(1)}, s32[32]{0:T(128)S(1)}, /*index=5*/s32[...) while((s32[]{:T(128)}, f32[64,8]{0,1:T(8,128)S(1)}, ...), condition=%wide.region_9.13_spmd, body=%wide.region_2.12_spmd.sunk | while | flops 8645694 | bytes 7067525 | solution.py:187
  167.0 7.1 %conditional.4 = ((f32[64,8]{0,1:T(8,128)S(1)}, f32[64,8]{0,1:T(8,128)S(1)}, f32[64,8,128]{2,0,1:T(8,128)S(1)})) conditional(s32[]{:T(128)} %convert_element_type.229, (f32[64,8]{0,1:T(8,128)S(1)}, f32[64,8]{0,1:T(8,128)S(1)}, f32[64,8,128]{2,0,1:T(8,128)S(1)}) %tuple.145, (s32[8]{0:T(128)S(1)}, s32[32]{0:T(128)S(1)}, s32[]{:T(128)}, ...), branch_computations={%region_4.0_spmd, %region_5.11_spmd} | conditional | flops 8645672 | bytes 7067152 | solution.py:185
  167.1 1.5 gather_fusion.1
  169.6 1.8 dynamic-slice_bitcast_fusion
  175.5 7.1 %conditional.4 = ((f32[64,8]{0,1:T(8,128)S(1)}, f32[64,8]{0,1:T(8,128)S(1)}, f32[64,8,128]{2,0,1:T(8,128)S(1)})) conditional(s32[]{:T(128)} %convert_element_type.229, (f32[64,8]{0,1:T(8,128)S(1)}, f32[64,8]{0,1:T(8,128)S(1)}, f32[64,8,128]{2,0,1:T(8,128)S(1)}) %tuple.145, (s32[8]{0:T(128)S(1)}, s32[32]{0:T(128)S(1)}, s32[]{:T(128)}, ...), branch_computations={%region_4.0_spmd, %region_5.11_spmd} | conditional | flops 8645672 | bytes 7067152 | solution.py:185
  175.7 1.5 gather_fusion.1
  178.1 1.8 dynamic-slice_bitcast_fusion
  188.5 1.4 multiply_add_fusion.5
  190.9 1.2 collective-permute-start.13
  192.9 11.4 %collective-permute-done.13 = f32[128,8]{0,1:T(8,128)S(1)} collective-permute-done((f32[128,8]{0,1:T(8,128)S(1)}, f32[128,8]{0,1:T(8,128)S(1)}, u32[]{:S(2)}, u32[]{:S(2)}) %collective-permute-start.13) | collective-permute-done | bytes 4128 | tf_op jit(solution)/shard_map/ppermute | solution.py:102
  205.2 1.4 multiply_add_fusion.4
  206.6 30.1 %collective-permute-start.4 = (f32[128,8,128]{2,0,1:T(8,128)S(1)}, f32[128,8,128]{2,0,1:T(8,128)S(1)}, u32[]{:S(2)}, u32[]{:S(2)}) collective-permute-start(f32[128,8,128]{2,0,1:T(8,128)S(1)} %multiply_add_fusion.4), channel_id=1, source_target_pairs={{0,16},{4,20},{8,24},{12,28},{16,0},{20,4},{24,8},{28,12},{32,48},... | collective-permute-start | bytes 1572872 | tf_op jit(solution)/shard_map/ppermute | solution.py:102
  236.8 2.8 collective-permute-start.5
  239.6 20.3 %collective-permute-done.14 = f32[128,8]{0,1:T(8,128)S(1)} collective-permute-done((f32[128,8]{0,1:T(8,128)S(1)}, f32[128,8]{0,1:T(8,128)S(1)}, u32[]{:S(2)}, u32[]{:S(2)}) %collective-permute-start.14) | collective-permute-done | bytes 4128 | tf_op jit(solution)/shard_map/ppermute | solution.py:102
  260.8 1.4 multiply_add_fusion.3
  262.3 5.9 %collective-permute-start.15 = (f32[128,8]{0,1:T(8,128)S(1)}, f32[128,8]{0,1:T(8,128)S(1)}, u32[]{:S(2)}, u32[]{:S(2)}) collective-permute-start(f32[128,8]{0,1:T(8,128)S(1)} %get-tuple-element.765), channel_id=1, source_target_pairs={{0,32},{4,36},{8,40},{12,44},{16,48},{20,52},{24,56},{28,60},{32,0... | collective-permute-start | bytes 12296 | tf_op jit(solution)/shard_map/ppermute | solution.py:102
  268.3 19.9 %collective-permute-done.15 = f32[128,8]{0,1:T(8,128)S(1)} collective-permute-done((f32[128,8]{0,1:T(8,128)S(1)}, f32[128,8]{0,1:T(8,128)S(1)}, u32[]{:S(2)}, u32[]{:S(2)}) %collective-permute-start.15) | collective-permute-done | bytes 4128 | tf_op jit(solution)/shard_map/ppermute | solution.py:102
  289.0 1.4 multiply_add_fusion.2
  290.4 2.0 collective-permute-start.8
  292.6 1.9 collective-permute-start.9
  295.1 9.6 %collective-permute-done.16 = f32[128,8]{0,1:T(8,128)S(1)} collective-permute-done((f32[128,8]{0,1:T(8,128)S(1)}, f32[128,8]{0,1:T(8,128)S(1)}, u32[]{:S(2)}, u32[]{:S(2)}) %collective-permute-start.16) | collective-permute-done | bytes 4128 | tf_op jit(solution)/shard_map/ppermute | solution.py:102
  304.8 4.3 collective-permute-start.17
  309.6 3.5 collective-permute-start.10
  314.5 9.4 %collective-permute-done.10 = f32[128,8,128]{2,0,1:T(8,128)S(1)} collective-permute-done((f32[128,8,128]{2,0,1:T(8,128)S(1)}, f32[128,8,128]{2,0,1:T(8,128)S(1)}, u32[]{:S(2)}, u32[]{:S(2)}) %collective-permute-start.10) | collective-permute-done | bytes 524320 | tf_op jit(solution)/shard_map/ppermute | solution.py:102
  325.2 15.4 %psum.14 = f32[128,64]{0,1:T(8,128)S(1)} all-reduce(f32[128,64]{0,1:T(8,128)S(1)} %fusion.64), channel_id=1, replica_groups=mesh['seq'=64,'head'=4] {'head'}, use_global_device_ids=true, to_apply=%region_21.25 | all-reduce | flops 8192 | bytes 65536 | tf_op jit(solution)/shard_map/psum | solution.py:205
  342.7 25.0 %all_to_all.38 = bf16[64,2,2048]{2,1,0:T(2,128)(2,1)S(1)} all-to-all(bf16[64,2,2048]{2,1,0:T(2,128)(2,1)S(1)} %reshape.452), channel_id=1, replica_groups=mesh['seq'=64,'head'=4] {'seq'}, dimensions={0} | all-to-all | bytes 1048576 | tf_op jit(solution)/shard_map/all_to_all | solution.py:141
  370.0 46.8 %all-gather.7.cloned.1.call-done = bf16[128,4096]{0,1:T(8,128)(2,1)} async-done(((bf16[128,64]{0,1:T(8,128)(2,1)}), bf16[128,4096]{0,1:T(8,128)(2,1)}) %all-gather.7.cloned.1.call-update) | async-done | bytes 1048592 | tf_op jit(solution)/shard_map/all_gather | solution.py:88
  416.8 1.8 convert_reduce_fusion
  418.6 2.7 fusion.74
  421.3 74.7 %all-gather.9.cloned.1.call-done = bf16[128,4096]{0,1:T(8,128)(2,1)} async-done(((bf16[128,64]{0,1:T(8,128)(2,1)}), bf16[128,4096]{0,1:T(8,128)(2,1)}) %all-gather.9.cloned.1.call-update) | async-done | bytes 1048592 | tf_op jit(solution)/shard_map/all_gather | solution.py:88
  496.0 1.5 fusion.107
  497.6 15.5 %psum.15 = f32[128,64]{0,1:T(8,128)S(1)} all-reduce(f32[128,64]{0,1:T(8,128)S(1)} %fusion.107), channel_id=1, replica_groups=mesh['seq'=64,'head'=4] {'head'}, use_global_device_ids=true, to_apply=%region_24.28 | all-reduce | flops 8192 | bytes 65536 | tf_op jit(solution)/shard_map/psum | solution.py:220
  (202 shorter events, 42.0 us)
Async XLA Ops:
  6.5 489.5 %copy-start = (bf16[64,4096]{1,0:T(8,128)(2,1)S(1)}, bf16[64,4096]{1,0:T(8,128)(2,1)}, u32[]{:S(2)}) copy-start(bf16[64,4096]{1,0:T(8,128)(2,1)} %param.39) | copy-start | bytes 1572868
  6.5 16.3 %copy-start.13 = (f32[64]{0:T(128)S(1)}, f32[64]{0:T(128)}, u32[]{:S(2)}) copy-start(f32[64]{0:T(128)} %param.35) | copy-start | bytes 772
  6.5 16.3 %copy-start.14 = (f32[64]{0:T(128)S(1)}, f32[64]{0:T(128)}, u32[]{:S(2)}) copy-start(f32[64]{0:T(128)} %param.34) | copy-start | bytes 772
  6.5 83.4 %all-gather.5.cloned.1.call-start = ((), (), s32[]{:S(2)}) async-start(), calls=%async_computation.2 | async-start | bytes 1064960 | tf_op jit(solution)/shard_map/all_gather | solution.py:88
  10.7 59.3 %all-to-all-start = ((bf16[64,2,1536]{2,1,0:T(2,128)(2,1)}), bf16[64,2,1536]{2,1,0:T(2,128)(2,1)S(1)}, u32[]{:S(2)}, u32[]{:S(2)}) async-start(bf16[64,2,1536]{2,1,0:T(2,128)(2,1)} %reshape.450), calls=%async_computation | async-start | bytes 786432 | tf_op jit(solution)/shard_map/all_to_all | solution.py:140
  22.8 394.0 %all-gather.7.cloned.1.call-start = ((), (), s32[]{:S(2)}) async-start(), calls=%async_computation.3 | async-start | bytes 1064960 | tf_op jit(solution)/shard_map/all_gather | solution.py:88
  93.7 51.1 %copy-start.1 = (s32[64]{0:T(128)S(1)}, s32[64]{0:T(128)}, u32[]{:S(2)}) copy-start(s32[64]{0:T(128)} %param.28) | copy-start | bytes 772
  93.7 51.1 %copy-start.8 = (f32[8]{0:T(128)S(1)}, f32[8]{0:T(128)}, u32[]{:S(2)}) copy-start(f32[8]{0:T(128)} %param.33) | copy-start | bytes 100
  93.8 51.1 %copy-start.11 = (s32[32]{0:T(128)S(1)}, s32[32]{0:T(128)}, u32[]{:S(2)}) copy-start(s32[32]{0:T(128)} %param.30) | copy-start | bytes 388
  93.8 51.1 %copy-start.12 = (s32[32]{0:T(128)S(1)}, s32[32]{0:T(128)}, u32[]{:S(2)}) copy-start(s32[32]{0:T(128)} %param.29) | copy-start | bytes 388
  185.6 2.2 collective-permute-start
  186.1 1.5 collective-permute-start.12
  186.3 1.3 collective-permute-start.1
  187.7 0.8 copy-start.4
  189.9 14.4 %collective-permute-start.2 = (f32[128,8,128]{2,0,1:T(8,128)S(1)}, f32[128,8,128]{2,0,1:T(8,128)S(1)}, u32[]{:S(2)}, u32[]{:S(2)}) collective-permute-start(f32[128,8,128]{2,0,1:T(8,128)S(1)} %multiply_add_fusion.5), channel_id=1, source_target_pairs={{0,8},{4,12},{8,0},{12,4},{16,24},{20,28},{24,16},{28,20},{32,40},... | collective-permute-start | bytes 1572872 | tf_op jit(solution)/shard_map/ppermute | solution.py:102
  190.9 13.4 %collective-permute-start.13 = (f32[128,8]{0,1:T(8,128)S(1)}, f32[128,8]{0,1:T(8,128)S(1)}, u32[]{:S(2)}, u32[]{:S(2)}) collective-permute-start(f32[128,8]{0,1:T(8,128)S(1)} %get-tuple-element.773), channel_id=1, source_target_pairs={{0,8},{4,12},{8,0},{12,4},{16,24},{20,28},{24,16},{28,20},{32,40},... | collective-permute-start | bytes 12296 | tf_op jit(solution)/shard_map/ppermute | solution.py:102
  192.0 12.3 %collective-permute-start.3 = (f32[128,8]{0,1:T(8,128)S(1)}, f32[128,8]{0,1:T(8,128)S(1)}, u32[]{:S(2)}, u32[]{:S(2)}) collective-permute-start(f32[128,8]{0,1:T(8,128)S(1)} %get-tuple-element.776), channel_id=1, source_target_pairs={{0,8},{4,12},{8,0},{12,4},{16,24},{20,28},{24,16},{28,20},{32,40},... | collective-permute-start | bytes 12296 | tf_op jit(solution)/shard_map/ppermute | solution.py:102
  204.4 0.8 copy-start.6
  205.2 89.4 %copy-start.2 = (bf16[64,1024]{0,1:T(8,128)(2,1)S(1)}, bf16[64,1024]{0,1:T(8,128)(2,1)}, u32[]{:S(2)}) copy-start(bf16[64,1024]{0,1:T(8,128)(2,1)} %get-tuple-element.794) | copy-start | bytes 393220
  206.6 53.3 %collective-permute-start.4 = (f32[128,8,128]{2,0,1:T(8,128)S(1)}, f32[128,8,128]{2,0,1:T(8,128)S(1)}, u32[]{:S(2)}, u32[]{:S(2)}) collective-permute-start(f32[128,8,128]{2,0,1:T(8,128)S(1)} %multiply_add_fusion.4), channel_id=1, source_target_pairs={{0,16},{4,20},{8,24},{12,28},{16,0},{20,4},{24,8},{28,12},{32,48},... | collective-permute-start | bytes 1572872 | tf_op jit(solution)/shard_map/ppermute | solution.py:102
  236.7 23.2 %collective-permute-start.14 = (f32[128,8]{0,1:T(8,128)S(1)}, f32[128,8]{0,1:T(8,128)S(1)}, u32[]{:S(2)}, u32[]{:S(2)}) collective-permute-start(f32[128,8]{0,1:T(8,128)S(1)} %get-tuple-element.769), channel_id=1, source_target_pairs={{0,16},{4,20},{8,24},{12,28},{16,0},{20,4},{24,8},{28,12},{32,48},... | collective-permute-start | bytes 12296 | tf_op jit(solution)/shard_map/ppermute | solution.py:102
  236.8 23.1 %collective-permute-start.5 = (f32[128,8]{0,1:T(8,128)S(1)}, f32[128,8]{0,1:T(8,128)S(1)}, u32[]{:S(2)}, u32[]{:S(2)}) collective-permute-start(f32[128,8]{0,1:T(8,128)S(1)} %get-tuple-element.772), channel_id=1, source_target_pairs={{0,16},{4,20},{8,24},{12,28},{16,0},{20,4},{24,8},{28,12},{32,48},... | collective-permute-start | bytes 12296 | tf_op jit(solution)/shard_map/ppermute | solution.py:102
  259.9 0.8 copy-start.7
  262.2 26.1 %collective-permute-start.6 = (f32[128,8,128]{2,0,1:T(8,128)S(1)}, f32[128,8,128]{2,0,1:T(8,128)S(1)}, u32[]{:S(2)}, u32[]{:S(2)}) collective-permute-start(f32[128,8,128]{2,0,1:T(8,128)S(1)} %multiply_add_fusion.3), channel_id=1, source_target_pairs={{0,32},{4,36},{8,40},{12,44},{16,48},{20,52},{24,56},{28,60},{32,0... | collective-permute-start | bytes 1572872 | tf_op jit(solution)/shard_map/ppermute | solution.py:102
  262.3 25.9 %collective-permute-start.15 = (f32[128,8]{0,1:T(8,128)S(1)}, f32[128,8]{0,1:T(8,128)S(1)}, u32[]{:S(2)}, u32[]{:S(2)}) collective-permute-start(f32[128,8]{0,1:T(8,128)S(1)} %get-tuple-element.765), channel_id=1, source_target_pairs={{0,32},{4,36},{8,40},{12,44},{16,48},{20,52},{24,56},{28,60},{32,0... | collective-permute-start | bytes 12296 | tf_op jit(solution)/shard_map/ppermute | solution.py:102
  268.2 20.0 %collective-permute-start.7 = (f32[128,8]{0,1:T(8,128)S(1)}, f32[128,8]{0,1:T(8,128)S(1)}, u32[]{:S(2)}, u32[]{:S(2)}) collective-permute-start(f32[128,8]{0,1:T(8,128)S(1)} %get-tuple-element.768), channel_id=1, source_target_pairs={{0,32},{4,36},{8,40},{12,44},{16,48},{20,52},{24,56},{28,60},{32,0... | collective-permute-start | bytes 12296 | tf_op jit(solution)/shard_map/ppermute | solution.py:102
  288.2 0.8 copy-start.5
  290.4 18.7 %collective-permute-start.8 = (f32[128,8,128]{2,0,1:T(8,128)S(1)}, f32[128,8,128]{2,0,1:T(8,128)S(1)}, u32[]{:S(2)}, u32[]{:S(2)}) collective-permute-start(f32[128,8,128]{2,0,1:T(8,128)S(1)} %multiply_add_fusion.2), channel_id=1, source_target_pairs={{0,64},{4,68},{8,72},{12,76},{16,80},{20,84},{24,88},{28,92},{32,9... | collective-permute-start | bytes 1572872 | tf_op jit(solution)/shard_map/ppermute | solution.py:102
  292.5 12.2 %collective-permute-start.16 = (f32[128,8]{0,1:T(8,128)S(1)}, f32[128,8]{0,1:T(8,128)S(1)}, u32[]{:S(2)}, u32[]{:S(2)}) collective-permute-start(f32[128,8]{0,1:T(8,128)S(1)} %get-tuple-element.761), channel_id=1, source_target_pairs={{0,64},{4,68},{8,72},{12,76},{16,80},{20,84},{24,88},{28,92},{32,9... | collective-permute-start | bytes 12296 | tf_op jit(solution)/shard_map/ppermute | solution.py:102
  292.6 12.2 %collective-permute-start.9 = (f32[128,8]{0,1:T(8,128)S(1)}, f32[128,8]{0,1:T(8,128)S(1)}, u32[]{:S(2)}, u32[]{:S(2)}) collective-permute-start(f32[128,8]{0,1:T(8,128)S(1)} %get-tuple-element.764), channel_id=1, source_target_pairs={{0,64},{4,68},{8,72},{12,76},{16,80},{20,84},{24,88},{28,92},{32,9... | collective-permute-start | bytes 12296 | tf_op jit(solution)/shard_map/ppermute | solution.py:102
  304.8 8.3 %collective-permute-start.17 = (f32[128,8]{0,1:T(8,128)S(1)}, f32[128,8]{0,1:T(8,128)S(1)}, u32[]{:S(2)}, u32[]{:S(2)}) collective-permute-start(f32[128,8]{0,1:T(8,128)S(1)} %get-tuple-element.757), channel_id=1, source_target_pairs={{0,128},{4,132},{8,136},{12,140},{16,144},{20,148},{24,152},{28,15... | collective-permute-start | bytes 12296 | tf_op jit(solution)/shard_map/ppermute | solution.py:102
  309.1 5.2 collective-permute-start.11
  309.5 15.4 %copy-start.15 = (bf16[64,1024]{1,0:T(8,128)(2,1)S(1)}, bf16[64,1024]{1,0:T(8,128)(2,1)}, u32[]{:S(2)}) copy-start(bf16[64,1024]{1,0:T(8,128)(2,1)} %param.37) | copy-start | bytes 393220
  309.6 14.3 %collective-permute-start.10 = (f32[128,8,128]{2,0,1:T(8,128)S(1)}, f32[128,8,128]{2,0,1:T(8,128)S(1)}, u32[]{:S(2)}, u32[]{:S(2)}) collective-permute-start(f32[128,8,128]{2,0,1:T(8,128)S(1)} %multiply_add_fusion.1), channel_id=1, source_target_pairs={{0,128},{4,132},{8,136},{12,140},{16,144},{20,148},{24,152},{28,15... | collective-permute-start | bytes 1572872 | tf_op jit(solution)/shard_map/ppermute | solution.py:102
  314.2 26.4 %copy-start.9 = (bf16[128,64]{0,1:T(8,128)(2,1)S(1)}, bf16[128,64]{0,1:T(8,128)(2,1)}, u32[]{:S(2)}) copy-start(bf16[128,64]{0,1:T(8,128)(2,1)} %copy.88) | copy-start | bytes 49156
  314.4 27.1 %copy-start.3 = (bf16[64,4096]{1,0:T(8,128)(2,1)S(1)}, bf16[64,4096]{1,0:T(8,128)(2,1)}, u32[]{:S(2)}) copy-start(bf16[64,4096]{1,0:T(8,128)(2,1)} %param.38) | copy-start | bytes 1572868
  341.2 154.8 %all-gather.9.cloned.1.call-start = ((), (), s32[]{:S(2)}) async-start(), calls=%async_computation.4 | async-start | bytes 1064960 | tf_op jit(solution)/shard_map/all_gather | solution.py:88
  418.5 94.5 %copy-start.10 = (bf16[128,64]{0,1:T(8,128)(2,1)S(1)}, bf16[128,64]{0,1:T(8,128)(2,1)}, u32[]{:S(2)}) copy-start(bf16[128,64]{0,1:T(8,128)(2,1)} %add_convert_fusion.1) | copy-start | bytes 49156
Sparse Core Ops, SparseCore 0:
  10.1 79.7 all-gather.4
  341.4 75.3 all-gather.6
  421.4 74.5 all-gather.8

commit v2 on v1

--- a/solution.py
+++ b/solution.py
@@ -113,6 +113,30 @@
     return state
 
 
+def attend_rows(carry_state, queries, new_keys, new_values, slopes, token_step):
+    run_max, run_sum, run_out = carry_state
+    head_size = queries.shape[2]
+    for earlier in range(len(new_keys)):
+        active = earlier <= token_step
+        scores = jnp.sum(
+            queries.astype(jnp.float32) * new_keys[earlier].astype(jnp.float32), axis=2
+        ) * head_size ** (-0.5)
+        scores = scores - slopes[None, :] * (token_step - earlier).astype(jnp.float32)
+        next_max = jnp.maximum(run_max, scores)
+        rescale = jnp.exp(run_max - next_max)
+        expon = jnp.exp(scores - next_max)
+        weights = lax.optimization_barrier(expon.astype(jnp.bfloat16)).astype(jnp.float32)
+        next_sum = run_sum * rescale + expon
+        next_out = run_out * rescale[:, :, None] + weights[:, :, None] * new_values[earlier].astype(
+            jnp.float32
+        )
+        run_sum = jnp.where(active, next_sum, run_sum)
+        run_out = jnp.where(active, next_out, run_out)
+        run_max = jnp.where(active, next_max, run_max)
+    attended = (run_out / run_sum[:, :, None]).astype(jnp.bfloat16)
+    return attended.reshape(attended.shape[0], -1)
+
+
 def on_device(
     tokens,
     lengths,
@@ -137,8 +161,18 @@
     qkv_width = w_qkv.shape[1] * w_qkv.shape[2]
     rows = nsteps * requests
 
-    qkv_cols = lax.all_to_all(w_qkv.reshape(local_width, qkv_width), "seq", 1, 0, tiled=True)
-    up_cols = lax.all_to_all(w_up, "seq", 1, 0, tiled=True)
+    qkv_chunk = qkv_width // nseq
+    up_chunk = w_up.shape[1] // nseq
+    both = jnp.concatenate(
+        [
+            w_qkv.reshape(local_width, nseq, qkv_chunk),
+            w_up.reshape(local_width, nseq, up_chunk),
+        ],
+        axis=2,
+    )
+    both = lax.all_to_all(both, "seq", 1, 0, tiled=True).reshape(nseq * local_width, qkv_chunk + up_chunk)
+    qkv_cols = both[:, :qkv_chunk]
+    up_cols = both[:, qkv_chunk:]
     gains = lax.all_gather(jnp.stack([norm1_gain, norm2_gain]), "seq", axis=1, tiled=True)
 
     token_rows = tokens.reshape(rows, local_width)
@@ -186,22 +220,33 @@
 
         states.append(lax.fori_loop(0, nblocks, visit, carry_state))
 
-    joined_state = tuple(jnp.concatenate(parts, axis=0) for parts in zip(*states))
-    run_max, run_sum, run_out = butterfly_combine(joined_state, nseq)
-    attended = []
-    for token_step in range(nsteps):
-        picked = slice(token_step * requests, (token_step + 1) * requests)
-        attended.append(
-            attend_new(
-                (run_max[picked], run_sum[picked], run_out[picked]),
-                all_queries[token_step],
-                new_keys,
-                new_values,
-                alibi_slopes,
-                token_step,
-            )
-        )
-    attended = jnp.concatenate(attended, axis=0)
+    run_max, run_sum, run_out = (jnp.concatenate(parts, axis=0) for parts in zip(*states))
+    packed = jnp.concatenate([run_out, run_max[:, :, None], run_sum[:, :, None]], axis=2)
+    own_rows = rows // nseq
+    packed = lax.all_to_all(
+        packed.reshape(nseq, own_rows, nheads, head_size + 2), "seq", 0, 0, tiled=True
+    )
+    part_out = packed[:, :, :, :head_size]
+    part_max = packed[:, :, :, head_size]
+    part_sum = packed[:, :, :, head_size + 1]
+    top_max = jnp.max(part_max, axis=0)
+    rescale = jnp.exp(part_max - top_max[None])
+    top_sum = jnp.sum(part_sum * rescale, axis=0)
+    top_out = jnp.sum(part_out * rescale[:, :, :, None], axis=0)
+    first_row = lax.axis_index("seq") * own_rows
+    my_step = first_row // requests
+    pick = lambda a: lax.dynamic_slice_in_dim(a.reshape(rows, nheads, head_size), first_row, own_rows, 0)
+    my_queries = pick(all_queries)
+    my_keys = []
+    my_values = []
+    for earlier in range(nsteps):
+        shifted = first_row - (my_step - earlier) * requests
+        my_keys.append(lax.dynamic_slice_in_dim(new_keys.reshape(rows, nheads, head_size), shifted, own_rows, 0))
+        my_values.append(lax.dynamic_slice_in_dim(new_values.reshape(rows, nheads, head_size), shifted, own_rows, 0))
+    mine = attend_rows(
+        (top_max, top_sum, top_out), my_queries, my_keys, my_values, alibi_slopes, my_step
+    )
+    attended = lax.all_gather(mine, "seq", axis=0, tiled=True)
     projected = lax.psum(
         lax.dot_general(attended, w_out, (((1,), (1,)), ((), ())), preferred_element_type=jnp.float32),
         "head",

time: 522 us -> 487 us (0.933)
  waiting for transfers between devices: 213 us -> 180 us
  blocking collectives: 152 us -> 184 us
  starting transfers between devices: 67.5 us -> 44.4 us
  local copies, waits for them, and re-layouts: 34.1 us -> 25.7 us
    ppermute x18 -> x0, waiting for transfers between devices: 72.8 us -> none  [butterfly_combine(): other = lax.ppermute(state, 'seq', pairs)]
    ppermute x18 -> x0, starting transfers between devices: 55.1 us -> none  [butterfly_combine(): other = lax.ppermute(state, 'seq', pairs)]
    all_gather x0 -> x1, blocking collectives: none -> 42.5 us  [on_device(): attended = lax.all_gather(mine, 'seq', axis=0, tiled=True)]
    all_to_all x1 -> x2, starting transfers between devices: 12.1 us -> 44.3 us  [the longest x1 32.2 us: on_device(): lax.all_to_all(packed.reshape(nseq, own_rows, nheads, head_size + 2), 'se...]
    all_to_all x1 -> x2, waiting for transfers between devices: 0.01 us -> 27 us  [the longest x1 27 us: on_device(): lax.all_to_all(packed.reshape(nseq, own_rows, nheads, head_size + 2), 'se...]
    all_to_all x1 -> x0, blocking collectives: 25 us -> none  [on_device(): up_cols = lax.all_to_all(w_up, 'seq', 1, 0, tiled=True)]
    all_gather x1, blocking collectives: 47 us -> 61.5 us  [on_device(): lax.all_gather(jnp.stack([norm1_gain, norm2_gain]), 'seq', axis=1, tiled=...]
    all_gather x3, waiting for transfers between devices: 140 us -> 153 us  [gather_cols(): return lax.all_gather(part, axis_name, axis=1, tiled=True)]
  transfers between devices with their start and end apart: 22 -> 5, of which waited for: 11 -> 4; matrix products, arithmetic and copies ran while one was open for 1% -> 2% of each run, Pallas kernels for 0% -> 0%
where the time goes in v2:
time: 487 us; the launch traced here: 486 us
  blocking collectives  184 us (38%)
  waiting for transfers between devices  180 us (37%)
  starting transfers between devices  44.4 us (9%)
  local copies, waits for them, and re-layouts  25.7 us (5%)
  other arithmetic  18.2 us (4%)
  matrix products  13.9 us (3%)
  between operations  13.6 us (3%)
  loops' own time  5.96 us (1%)
    all_gather x3, waiting for transfers between devices, gather_cols(): return lax.all_gather(part, axis_name, axis=1, tiled=True)  153 us
    all_gather x1, blocking collectives, on_device(): lax.all_gather(jnp.stack([norm1_gain, norm2_gain]), 'seq', axis=1, tiled=...  61.5 us
    all_gather x1, blocking collectives, gather_cols(): return lax.all_gather(part, axis_name, axis=1, tiled=True)  49.4 us
    all_gather x1, blocking collectives, on_device(): attended = lax.all_gather(mine, 'seq', axis=0, tiled=True)  42.5 us
    all_to_all x1, starting transfers between devices, on_device(): lax.all_to_all(packed.reshape(nseq, own_rows, nheads, head_size + 2), 'se...  32.2 us
    all_to_all x1, waiting for transfers between devices, on_device(): lax.all_to_all(packed.reshape(nseq, own_rows, nheads, head_size + 2), 'se...  27 us
    psum x1, blocking collectives, on_device(): down_proj = lax.psum(down_part, 'head')  15.5 us
    psum x1, blocking collectives, on_device(): lax.psum(lax.dot_general(attended, w_out, (((1,), (1,)), ((), ())), prefe...  15.5 us
  transfers between devices with their start and end apart: 5, of which 4 were waited for; matrix products, arithmetic and copies ran while one was open for 2% of the time, Pallas kernels for 0%

profile of v2, /device:TPU:4, one launch (start us, length us, event | category | flops | bytes accessed | tf_op | source)
XLA Modules:
  0.0 485.6 jit_solution(7923873284231080723)
XLA Ops:
  6.5 1.5 copy.241
  8.1 2.1 reshape.423
  10.2 0.7 copy.211
  11.2 0.6 copy.210
  11.9 1.6 pad_maximum_fusion
  13.5 12.1 %all-to-all-start = ((bf16[64,64,112]{2,0,1:T(8,128)(2,1)}), bf16[64,64,112]{2,0,1:T(8,128)(2,1)S(1)}, u32[]{:S(2)}, u32[]{:S(2)}) async-start(bf16[64,64,112]{2,0,1:T(8,128)(2,1)} %pad_maximum_fusion), calls=%async_computation | async-start | bytes 2097152 | tf_op jit(solution)/shard_map/all_to_all | solution.py:173
  25.6 61.5 %all-gather = f32[64,64,2]{1,2,0:T(2,128)S(1)} all-gather(f32[1,64,2]{1,2,0:T(2,128)S(1)} %maximum_bitcast_fusion), channel_id=1, replica_groups=mesh['seq'=64,'head'=4] {'seq'}, dimensions={0}, use_global_device_ids=true | all-gather | bytes 33280 | tf_op jit(solution)/shard_map/all_gather | solution.py:176
  87.2 3.3 all-gather.6.cloned.1.call-done
  90.5 1.8 convert_reduce_fusion.1
  92.3 1.0 copy-done.2
  93.3 2.3 convolution_convert_fusion
  95.6 49.4 %all_gather.20 = bf16[128,3072]{0,1:T(8,128)(2,1)S(1)} all-gather(bf16[128,48]{0,1:T(8,128)(2,1)S(1)} %convolution_convert_fusion), channel_id=1, replica_groups=mesh['seq'=64,'head'=4] {'seq'}, dimensions={1}, use_global_device_ids=true | all-gather | bytes 798720 | tf_op jit(solution)/shard_map/all_gather | solution.py:88
  145.4 18.3 %while.34 = (s32[]{:T(128)}, f32[64,8]{0,1:T(8,128)S(1)}, f32[64,8]{0,1:T(8,128)S(1)}, f32[64,8,128]{2,0,1:T(8,128)S(1)}, s32[32]{0:T(128)S(1)}, /*index=5*/s32[...) while((s32[]{:T(128)}, f32[64,8]{0,1:T(8,128)S(1)}, ...), condition=%wide.region_9.13_spmd, body=%wide.region_2.12_spmd.sunk | while | flops 8645694 | bytes 7067525 | solution.py:221
  145.4 0.8 compare_reduce_fusion.4
  146.9 6.2 %conditional.4 = ((f32[64,8]{0,1:T(8,128)S(1)}, f32[64,8]{0,1:T(8,128)S(1)}, f32[64,8,128]{2,0,1:T(8,128)S(1)})) conditional(s32[]{:T(128)} %convert_element_type.196, (f32[64,8]{0,1:T(8,128)S(1)}, f32[64,8]{0,1:T(8,128)S(1)}, f32[64,8,128]{2,0,1:T(8,128)S(1)}) %tuple.133, (s32[8]{0:T(128)S(1)}, s32[32]{0:T(128)S(1)}, s32[]{:T(128)}, ...), branch_computations={%region_4.0_spmd, %region_5.11_spmd} | conditional | flops 8645672 | bytes 7067152 | solution.py:219
  146.9 0.6 gather_fusion
  148.5 1.8 dynamic-slice_bitcast_fusion
  153.1 0.8 compare_reduce_fusion.4
  154.6 6.2 %conditional.4 = ((f32[64,8]{0,1:T(8,128)S(1)}, f32[64,8]{0,1:T(8,128)S(1)}, f32[64,8,128]{2,0,1:T(8,128)S(1)})) conditional(s32[]{:T(128)} %convert_element_type.196, (f32[64,8]{0,1:T(8,128)S(1)}, f32[64,8]{0,1:T(8,128)S(1)}, f32[64,8,128]{2,0,1:T(8,128)S(1)}) %tuple.133, (s32[8]{0:T(128)S(1)}, s32[32]{0:T(128)S(1)}, s32[]{:T(128)}, ...), branch_computations={%region_4.0_spmd, %region_5.11_spmd} | conditional | flops 8645672 | bytes 7067152 | solution.py:219
  154.6 0.6 gather_fusion
  156.1 1.8 dynamic-slice_bitcast_fusion
  160.7 0.8 compare_reduce_fusion.4
  162.3 0.8 compare_reduce_fusion.4
  164.0 18.3 %while.35 = (s32[]{:T(128)}, f32[64,8]{0,1:T(8,128)S(1)}, f32[64,8]{0,1:T(8,128)S(1)}, f32[64,8,128]{2,0,1:T(8,128)S(1)}, s32[32]{0:T(128)S(1)}, /*index=5*/s32[...) while((s32[]{:T(128)}, f32[64,8]{0,1:T(8,128)S(1)}, ...), condition=%wide.region_17.21_spmd, body=%wide.region_10.20_spmd.sunk | while | flops 8645702 | bytes 7067557 | solution.py:221
  164.0 0.8 compare_reduce_fusion.5
  165.5 6.2 %conditional.5 = ((f32[64,8]{0,1:T(8,128)S(1)}, f32[64,8]{0,1:T(8,128)S(1)}, f32[64,8,128]{2,0,1:T(8,128)S(1)})) conditional(s32[]{:T(128)} %convert_element_type.197, (f32[64,8]{0,1:T(8,128)S(1)}, f32[64,8]{0,1:T(8,128)S(1)}, f32[64,8,128]{2,0,1:T(8,128)S(1)}) %tuple.137, (s32[8]{0:T(128)S(1)}, s32[32]{0:T(128)S(1)}, s32[]{:T(128)}, ...), branch_computations={%region_12.15_spmd, %region_13.19_spmd} | conditional | flops 8645680 | bytes 7067184 | solution.py:219
  165.5 0.6 gather_fusion.3
  167.0 1.8 dynamic-slice_bitcast_fusion.2
  171.6 0.8 compare_reduce_fusion.5
  173.1 6.2 %conditional.5 = ((f32[64,8]{0,1:T(8,128)S(1)}, f32[64,8]{0,1:T(8,128)S(1)}, f32[64,8,128]{2,0,1:T(8,128)S(1)})) conditional(s32[]{:T(128)} %convert_element_type.197, (f32[64,8]{0,1:T(8,128)S(1)}, f32[64,8]{0,1:T(8,128)S(1)}, f32[64,8,128]{2,0,1:T(8,128)S(1)}) %tuple.137, (s32[8]{0:T(128)S(1)}, s32[32]{0:T(128)S(1)}, s32[]{:T(128)}, ...), branch_computations={%region_12.15_spmd, %region_13.19_spmd} | conditional | flops 8645680 | bytes 7067184 | solution.py:219
  173.2 0.6 gather_fusion.3
  174.7 1.8 dynamic-slice_bitcast_fusion.2
  179.3 0.8 compare_reduce_fusion.5
  180.8 0.8 compare_reduce_fusion.5
  182.5 0.8 copy.218
  183.4 0.8 copy.219
  184.6 1.3 pad_maximum_fusion.1
  185.9 32.2 %all-to-all-start.1 = ((f32[64,2,8,130]{3,2,1,0:T(8,128)}), f32[64,2,8,130]{3,2,1,0:T(8,128)S(1)}, u32[]{:S(2)}, u32[]{:S(2)}) async-start(f32[64,2,8,130]{3,2,1,0:T(8,128)} %pad_maximum_fusion.1), calls=%async_computation.1 | async-start | bytes 2097152 | tf_op jit(solution)/shard_map/all_to_all | solution.py:226
  219.2 27.0 %all-to-all-done.1 = f32[64,2,8,130]{3,2,1,0:T(8,128)S(1)} async-done(((f32[64,2,8,130]{3,2,1,0:T(8,128)}), f32[64,2,8,130]{3,2,1,0:T(8,128)S(1)}, u32[]{:S(2)}, u32[]{:S(2)}) %all-to-all-start.1) | async-done | bytes 532512 | tf_op jit(solution)/shard_map/all_to_all | solution.py:226
  247.7 42.5 %all-gather.1 = bf16[64,2,1024]{2,1,0:T(2,128)(2,1)S(1)} all-gather(bf16[1,2,1024]{2,1,0:T(2,128)(2,1)S(1)} %reshape.483), channel_id=1, replica_groups=mesh['seq'=64,'head'=4] {'seq'}, dimensions={0}, use_global_device_ids=true | all-gather | bytes 266240 | tf_op jit(solution)/shard_map/all_gather | solution.py:249
  290.5 15.5 %psum.14 = f32[128,64]{0,1:T(8,128)S(1)} all-reduce(f32[128,64]{0,1:T(8,128)S(1)} %fusion.87), channel_id=1, replica_groups=mesh['seq'=64,'head'=4] {'head'}, use_global_device_ids=true, to_apply=%region_23.27 | all-reduce | flops 8192 | bytes 65536 | tf_op jit(solution)/shard_map/psum | solution.py:250
  306.7 74.6 %all-gather.8.cloned.1.call-done = bf16[128,4096]{0,1:T(8,128)(2,1)} async-done(((bf16[128,64]{0,1:T(8,128)(2,1)}), bf16[128,4096]{0,1:T(8,128)(2,1)}) %all-gather.8.cloned.1.call-update) | async-done | bytes 1048592 | tf_op jit(solution)/shard_map/all_gather | solution.py:88
  381.3 1.8 convert_reduce_fusion
  383.1 3.5 fusion.62
  386.6 74.7 %all-gather.10.cloned.1.call-done = bf16[128,4096]{0,1:T(8,128)(2,1)} async-done(((bf16[128,64]{0,1:T(8,128)(2,1)}), bf16[128,4096]{0,1:T(8,128)(2,1)}) %all-gather.10.cloned.1.call-update) | async-done | bytes 1048592 | tf_op jit(solution)/shard_map/all_gather | solution.py:88
  461.3 1.5 fusion.88
  462.8 15.5 %psum.15 = f32[128,64]{0,1:T(8,128)S(1)} all-reduce(f32[128,64]{0,1:T(8,128)S(1)} %fusion.88), channel_id=1, replica_groups=mesh['seq'=64,'head'=4] {'head'}, use_global_device_ids=true, to_apply=%region_26.30 | all-reduce | flops 8192 | bytes 65536 | tf_op jit(solution)/shard_map/psum | solution.py:265
  478.3 0.7 copy.242
  (158 shorter events, 20.2 us)
Async XLA Ops:
  6.5 454.8 %copy-start = (bf16[64,4096]{1,0:T(8,128)(2,1)S(1)}, bf16[64,4096]{1,0:T(8,128)(2,1)}, u32[]{:S(2)}) copy-start(bf16[64,4096]{1,0:T(8,128)(2,1)} %param.39) | copy-start | bytes 1572868
  6.5 4.3 copy-start.4
  6.5 84.0 %all-gather.6.cloned.1.call-start = ((), (), s32[]{:S(2)}) async-start(), calls=%async_computation.2 | async-start | bytes 1064960 | tf_op jit(solution)/shard_map/all_gather | solution.py:88
  11.9 13.7 %copy-start.11 = (f32[64]{0:T(128)S(1)}, f32[64]{0:T(128)}, u32[]{:S(2)}) copy-start(f32[64]{0:T(128)} %param.35) | copy-start | bytes 772
  11.9 13.7 %copy-start.12 = (f32[64]{0:T(128)S(1)}, f32[64]{0:T(128)}, u32[]{:S(2)}) copy-start(f32[64]{0:T(128)} %param.34) | copy-start | bytes 772
  13.5 78.8 %all-to-all-start = ((bf16[64,64,112]{2,0,1:T(8,128)(2,1)}), bf16[64,64,112]{2,0,1:T(8,128)(2,1)S(1)}, u32[]{:S(2)}, u32[]{:S(2)}) async-start(bf16[64,64,112]{2,0,1:T(8,128)(2,1)} %pad_maximum_fusion), calls=%async_computation | async-start | bytes 2097152 | tf_op jit(solution)/shard_map/all_to_all | solution.py:173
  92.3 1.0 copy-start.2
  95.6 49.8 %copy-start.1 = (s32[64]{0:T(128)S(1)}, s32[64]{0:T(128)}, u32[]{:S(2)}) copy-start(s32[64]{0:T(128)} %param.28) | copy-start | bytes 772
  95.6 49.8 %copy-start.5 = (f32[8]{0:T(128)S(1)}, f32[8]{0:T(128)}, u32[]{:S(2)}) copy-start(f32[8]{0:T(128)} %param.33) | copy-start | bytes 100
  95.6 49.8 %copy-start.9 = (s32[32]{0:T(128)S(1)}, s32[32]{0:T(128)}, u32[]{:S(2)}) copy-start(s32[32]{0:T(128)} %param.30) | copy-start | bytes 388
  95.6 49.8 %copy-start.10 = (s32[32]{0:T(128)S(1)}, s32[32]{0:T(128)}, u32[]{:S(2)}) copy-start(s32[32]{0:T(128)} %param.29) | copy-start | bytes 388
  185.9 60.3 %all-to-all-start.1 = ((f32[64,2,8,130]{3,2,1,0:T(8,128)}), f32[64,2,8,130]{3,2,1,0:T(8,128)S(1)}, u32[]{:S(2)}, u32[]{:S(2)}) async-start(f32[64,2,8,130]{3,2,1,0:T(8,128)} %pad_maximum_fusion.1), calls=%async_computation.1 | async-start | bytes 2097152 | tf_op jit(solution)/shard_map/all_to_all | solution.py:226
  218.1 163.2 %all-gather.8.cloned.1.call-start = ((), (), s32[]{:S(2)}) async-start(), calls=%async_computation.3 | async-start | bytes 1064960 | tf_op jit(solution)/shard_map/all_gather | solution.py:88
  219.2 71.1 %copy-start.8 = (bf16[64,1024]{1,0:T(8,128)(2,1)S(1)}, bf16[64,1024]{1,0:T(8,128)(2,1)}, u32[]{:S(2)}) copy-start(bf16[64,1024]{1,0:T(8,128)(2,1)} %param.37) | copy-start | bytes 393220
  219.2 86.8 %copy-start.6 = (bf16[128,64]{0,1:T(8,128)(2,1)S(1)}, bf16[128,64]{0,1:T(8,128)(2,1)}, u32[]{:S(2)}) copy-start(bf16[128,64]{0,1:T(8,128)(2,1)} %copy.241) | copy-start | bytes 49156
  247.0 136.1 %copy-start.3 = (bf16[64,64,112]{2,0,1:T(8,128)(2,1)S(1)}, bf16[64,64,112]{2,0,1:T(8,128)(2,1)}, u32[]{:S(2)}) copy-start(bf16[64,64,112]{2,0,1:T(8,128)(2,1)} %copy-done.2) | copy-start | bytes 2752516
  306.6 154.6 %all-gather.10.cloned.1.call-start = ((), (), s32[]{:S(2)}) async-start(), calls=%async_computation.4 | async-start | bytes 1064960 | tf_op jit(solution)/shard_map/all_gather | solution.py:88
  383.1 95.3 %copy-start.7 = (bf16[128,64]{0,1:T(8,128)(2,1)S(1)}, bf16[128,64]{0,1:T(8,128)(2,1)}, u32[]{:S(2)}) copy-start(bf16[128,64]{0,1:T(8,128)(2,1)} %add_convert_fusion.1) | copy-start | bytes 49156
Sparse Core Ops, SparseCore 0:
  10.1 80.3 all-gather.5
  306.8 74.4 all-gather.7
  386.7 74.5 all-gather.9

commit v3 on v2

--- a/solution.py
+++ b/solution.py
@@ -84,8 +84,25 @@
     return attended.reshape(attended.shape[0], -1)
 
 
-def gather_cols(part, axis_name):
-    return lax.all_gather(part, axis_name, axis=1, tiled=True)
+def gather_rows(part, nseq):
+    copies = jnp.broadcast_to(part[None], (nseq,) + part.shape)
+    return lax.all_to_all(copies, "seq", 0, 0, tiled=True)
+
+
+def gather_cols(part, nseq):
+    got = gather_rows(part, nseq)
+    return jnp.moveaxis(got, 0, -2).reshape(part.shape[:-1] + (nseq * part.shape[-1],))
+
+
+def head_sum(part, nhead):
+    my_index = lax.axis_index("head")
+    stride = 1
+    while stride < nhead:
+        other = lax.ppermute(part, "head", [(i, i ^ stride) for i in range(nhead)])
+        low = (my_index & stride) == 0
+        part = jnp.where(low, part + other, other + part)
+        stride *= 2
+    return part
 
 
 def full_normalize(rows, gain_full):
@@ -152,6 +169,7 @@
     w_up,
     w_down,
     nseq,
+    nhead,
 ):
     nsteps, requests, local_width = tokens.shape
     nheads = alibi_slopes.shape[0]
@@ -173,13 +191,13 @@
     both = lax.all_to_all(both, "seq", 1, 0, tiled=True).reshape(nseq * local_width, qkv_chunk + up_chunk)
     qkv_cols = both[:, :qkv_chunk]
     up_cols = both[:, qkv_chunk:]
-    gains = lax.all_gather(jnp.stack([norm1_gain, norm2_gain]), "seq", axis=1, tiled=True)
+    gains = gather_cols(jnp.stack([norm1_gain, norm2_gain]), nseq)
 
     token_rows = tokens.reshape(rows, local_width)
     token_float = token_rows.astype(jnp.float32)
-    normed = full_normalize(gather_cols(token_rows, "seq"), gains[0])
+    normed = full_normalize(gather_cols(token_rows, nseq), gains[0])
     qkv_part = jnp.dot(normed, qkv_cols, preferred_element_type=jnp.float32).astype(jnp.bfloat16)
-    joined = gather_cols(qkv_part, "seq")
+    joined = gather_cols(qkv_part, nseq)
     all_queries = joined[:, :head_width].reshape(nsteps, requests, nheads, head_size)
     new_keys = joined[:, head_width : 2 * head_width].reshape(nsteps, requests, nheads, head_size)
     new_values = joined[:, 2 * head_width :].reshape(nsteps, requests, nheads, head_size)
@@ -246,23 +264,23 @@
     mine = attend_rows(
         (top_max, top_sum, top_out), my_queries, my_keys, my_values, alibi_slopes, my_step
     )
-    attended = lax.all_gather(mine, "seq", axis=0, tiled=True)
-    projected = lax.psum(
+    attended = gather_rows(mine, nseq).reshape(rows, -1)
+    projected = head_sum(
         lax.dot_general(attended, w_out, (((1,), (1,)), ((), ())), preferred_element_type=jnp.float32),
-        "head",
+        nhead,
     )
     hidden_in = (token_float + projected).astype(jnp.bfloat16)
     hidden_float = hidden_in.astype(jnp.float32)
-    normed_two = full_normalize(gather_cols(hidden_in, "seq"), gains[1])
+    normed_two = full_normalize(gather_cols(hidden_in, nseq), gains[1])
     up_share = jnp.dot(normed_two, up_cols, preferred_element_type=jnp.float32)
     hidden_share = jax.nn.gelu(up_share, approximate=False).astype(jnp.bfloat16)
     down_part = lax.dot_general(
-        gather_cols(hidden_share, "seq"),
+        gather_cols(hidden_share, nseq),
         w_down,
         (((1,), (1,)), ((), ())),
         preferred_element_type=jnp.float32,
     )
-    down_proj = lax.psum(down_part, "head")
+    down_proj = head_sum(down_part, nhead)
     return (hidden_float + down_proj).astype(jnp.bfloat16).reshape(nsteps, requests, local_width)
 
 
@@ -284,5 +302,5 @@
     )
     nseq = mesh.shape["seq"]
     return jax.shard_map(
-        functools.partial(on_device, nseq=nseq), mesh=mesh, in_specs=placed, out_specs=P(None, None, "seq"), check_vma=False
-    )
+        functools.partial(on_device, nseq=nseq, nhead=mesh.shape["head"]), mesh=mesh, in_specs=placed, out_specs=P(None, None, "seq"), check_vma=False
+    )

time: 487 us -> 343 us (0.70)
  blocking collectives: 184 us -> 52.9 us
  waiting for transfers between devices: 180 us -> 145 us
  starting transfers between devices: 44.4 us -> 71.1 us
  between operations: 13.6 us -> 0.55 us
  local copies, waits for them, and re-layouts: 25.7 us -> 33.1 us
    all_gather x3 -> x0, blocking collectives: 153 us -> none  [the longest x1 61.5 us: on_device(): lax.all_gather(jnp.stack([norm1_gain, norm2_gain]), 'seq', axis=1, tiled=...]
    all_gather x3 -> x0, waiting for transfers between devices: 153 us -> none  [gather_cols(): return lax.all_gather(part, axis_name, axis=1, tiled=True)]
    all_to_all x0 -> x4, waiting for transfers between devices: none -> 78.8 us  [gather_rows(): return lax.all_to_all(copies, 'seq', 0, 0, tiled=True)]
    all_to_all x0 -> x2, blocking collectives: none -> 52.9 us  [gather_rows(): return lax.all_to_all(copies, 'seq', 0, 0, tiled=True)]
    psum x2 -> x0, blocking collectives: 30.9 us -> none  [the longest x1 15.5 us: on_device(): down_proj = lax.psum(down_part, 'head')]
    all_to_all x0 -> x4, starting transfers between devices: none -> 29.8 us  [gather_rows(): return lax.all_to_all(copies, 'seq', 0, 0, tiled=True)]
    all_to_all x1, waiting for transfers between devices: 0.01 us -> 23.8 us  [on_device(): lax.all_to_all(both, 'seq', 1, 0, tiled=True)]
    ppermute x0 -> x4, waiting for transfers between devices: none -> 15.2 us  [head_sum(): other = lax.ppermute(part, 'head', [(i, i ^ stride) for i in range(nhead)])]
  transfers between devices with their start and end apart: 5 -> 10, of which waited for: 4 -> 10; matrix products, arithmetic and copies ran while one was open for 2% -> 4% of each run, Pallas kernels for 0% -> 0%
where the time goes in v3:
time: 343 us; the launch traced here: 341 us
  waiting for transfers between devices  145 us (42%)
  starting transfers between devices  71.1 us (21%)
  blocking collectives  52.9 us (15%)
  local copies, waits for them, and re-layouts  33.1 us (10%)
  other arithmetic  22.7 us (7%)
  matrix products  10.2 us (3%)
  loops' own time  6 us (2%)
    all_to_all x4, waiting for transfers between devices, gather_rows(): return lax.all_to_all(copies, 'seq', 0, 0, tiled=True)  78.8 us
    all_to_all x2, blocking collectives, gather_rows(): return lax.all_to_all(copies, 'seq', 0, 0, tiled=True)  52.9 us
    all_to_all x1, starting transfers between devices, on_device(): lax.all_to_all(packed.reshape(nseq, own_rows, nheads, head_size + 2), 'se...  31.2 us
    all_to_all x4, starting transfers between devices, gather_rows(): return lax.all_to_all(copies, 'seq', 0, 0, tiled=True)  29.8 us
    all_to_all x1, waiting for transfers between devices, on_device(): lax.all_to_all(packed.reshape(nseq, own_rows, nheads, head_size + 2), 'se...  27 us
    all_to_all x1, waiting for transfers between devices, on_device(): lax.all_to_all(both, 'seq', 1, 0, tiled=True)  23.8 us
    ppermute x4, waiting for transfers between devices, head_sum(): other = lax.ppermute(part, 'head', [(i, i ^ stride) for i in range(nhead)])  15.2 us
    reduce_or x8, other arithmetic, visit(): return lax.cond(jnp.any(owners >= 0), compute, keep_state, state_in)  8.88 us
  transfers between devices with their start and end apart: 10, of which 10 were waited for; matrix products, arithmetic and copies ran while one was open for 4% of the time, Pallas kernels for 0%

profile of v3, /device:TPU:4, one launch (start us, length us, event | category | flops | bytes accessed | tf_op | source)
XLA Modules:
  0.0 341.5 jit_solution(5034365910217816239)
XLA Ops:
  1.5 12.1 %all-to-all-start.1 = ((f32[64,1,128]{2,1,0:T(1,128)}), f32[64,1,128]{2,1,0:T(1,128)S(1)}, u32[]{:S(2)}, u32[]{:S(2)}) async-start(f32[64,1,128]{2,1,0:T(1,128)} %reshape.542), calls=%async_computation.1 | async-start | bytes 65536 | tf_op jit(solution)/shard_map/all_to_all | solution.py:89
  13.6 0.8 copy.235
  14.5 8.6 %all-to-all-done.1 = f32[64,1,128]{2,1,0:T(1,128)S(1)} async-done(((f32[64,1,128]{2,1,0:T(1,128)}), f32[64,1,128]{2,1,0:T(1,128)S(1)}, u32[]{:S(2)}, u32[]{:S(2)}) %all-to-all-start.1) | async-done | bytes 32800 | tf_op jit(solution)/shard_map/all_to_all | solution.py:89
  23.1 1.2 broadcast_in_dim.195
  24.3 4.7 %all-to-all-start = ((bf16[64,128,64]{1,2,0:T(8,128)(2,1)}), bf16[64,128,64]{1,2,0:T(8,128)(2,1)S(1)}, u32[]{:S(2)}, u32[]{:S(2)}) async-start(bf16[64,128,64]{1,2,0:T(8,128)(2,1)} %broadcast_in_dim.195), calls=%async_computation | async-start | bytes 2097152 | tf_op jit(solution)/shard_map/all_to_all | solution.py:89
  29.0 1.1 reshape.446
  30.1 1.7 copy.206
  31.8 1.2 copy.204
  33.0 1.6 copy.205
  34.6 2.8 pad_maximum_fusion
  37.4 19.7 %all-to-all-done = bf16[64,128,64]{1,2,0:T(8,128)(2,1)S(1)} async-done(((bf16[64,128,64]{1,2,0:T(8,128)(2,1)}), bf16[64,128,64]{1,2,0:T(8,128)(2,1)S(1)}, u32[]{:S(2)}, u32[]{:S(2)}) %all-to-all-start) | async-done | bytes 1048608 | tf_op jit(solution)/shard_map/all_to_all | solution.py:89
  57.1 6.6 %all-to-all-start.2 = ((bf16[64,64,112]{2,0,1:T(8,128)(2,1)}), bf16[64,64,112]{2,0,1:T(8,128)(2,1)S(1)}, u32[]{:S(2)}, u32[]{:S(2)}) async-start(bf16[64,64,112]{2,0,1:T(8,128)(2,1)} %pad_maximum_fusion), calls=%async_computation.2 | async-start | bytes 2097152 | tf_op jit(solution)/shard_map/all_to_all | solution.py:191
  66.5 1.5 fusion.43
  68.0 23.8 %all-to-all-done.2 = bf16[64,64,112]{2,0,1:T(8,128)(2,1)S(1)} async-done(((bf16[64,64,112]{2,0,1:T(8,128)(2,1)}), bf16[64,64,112]{2,0,1:T(8,128)(2,1)S(1)}, u32[]{:S(2)}, u32[]{:S(2)}) %all-to-all-start.2) | async-done | bytes 917536 | tf_op jit(solution)/shard_map/all_to_all | solution.py:191
  91.9 2.1 convolution_convert_fusion
  94.0 1.0 broadcast_in_dim.197
  95.0 6.8 %all-to-all-start.3 = ((bf16[64,128,48]{1,2,0:T(8,128)(2,1)}), bf16[64,128,48]{1,2,0:T(8,128)(2,1)S(1)}, u32[]{:S(2)}, u32[]{:S(2)}) async-start(bf16[64,128,48]{1,2,0:T(8,128)(2,1)} %broadcast_in_dim.197), calls=%async_computation.3 | async-start | bytes 1572864 | tf_op jit(solution)/shard_map/all_to_all | solution.py:89
  101.8 22.7 %all-to-all-done.3 = bf16[64,128,48]{1,2,0:T(8,128)(2,1)S(1)} async-done(((bf16[64,128,48]{1,2,0:T(8,128)(2,1)}), bf16[64,128,48]{1,2,0:T(8,128)(2,1)S(1)}, u32[]{:S(2)}, u32[]{:S(2)}) %all-to-all-start.3) | async-done | bytes 786464 | tf_op jit(solution)/shard_map/all_to_all | solution.py:89
  125.4 18.5 %while.35 = (s32[]{:T(128)}, f32[64,8]{0,1:T(8,128)S(1)}, f32[64,8]{0,1:T(8,128)S(1)}, f32[64,8,128]{2,0,1:T(8,128)S(1)}, s32[32]{0:T(128)S(1)}, /*index=5*/s32[...) while((s32[]{:T(128)}, f32[64,8]{0,1:T(8,128)S(1)}, ...), condition=%wide.region_17.21_spmd, body=%wide.region_10.20_spmd.sunk | while | flops 8645702 | bytes 7067565 | solution.py:239
  126.8 6.3 %conditional.5 = ((f32[64,8]{0,1:T(8,128)S(1)}, f32[64,8]{0,1:T(8,128)S(1)}, f32[64,8,128]{2,0,1:T(8,128)S(1)})) conditional(s32[]{:T(128)} %convert_element_type.211, (f32[64,8]{0,1:T(8,128)S(1)}, f32[64,8]{0,1:T(8,128)S(1)}, f32[64,8,128]{2,0,1:T(8,128)S(1)}) %tuple.135, (s32[8]{0:T(128)S(1)}, s32[32]{0:T(128)S(1)}, s32[]{:T(128)}, ...), branch_computations={%region_12.15_spmd, %region_13.19_spmd} | conditional | flops 8645680 | bytes 7067184 | solution.py:237
  126.8 1.8 dynamic-slice_bitcast_fusion.2
  134.6 6.3 %conditional.5 = ((f32[64,8]{0,1:T(8,128)S(1)}, f32[64,8]{0,1:T(8,128)S(1)}, f32[64,8,128]{2,0,1:T(8,128)S(1)})) conditional(s32[]{:T(128)} %convert_element_type.211, (f32[64,8]{0,1:T(8,128)S(1)}, f32[64,8]{0,1:T(8,128)S(1)}, f32[64,8,128]{2,0,1:T(8,128)S(1)}) %tuple.135, (s32[8]{0:T(128)S(1)}, s32[32]{0:T(128)S(1)}, s32[]{:T(128)}, ...), branch_computations={%region_12.15_spmd, %region_13.19_spmd} | conditional | flops 8645680 | bytes 7067184 | solution.py:237
  134.6 1.8 dynamic-slice_bitcast_fusion.2
  144.5 21.2 %while.34 = (s32[]{:T(128)}, f32[64,8]{0,1:T(8,128)S(1)}, f32[64,8]{0,1:T(8,128)S(1)}, f32[64,8,128]{2,0,1:T(8,128)S(1)}, s32[32]{0:T(128)}, /*index=5*/s32[32]{...) while((s32[]{:T(128)}, f32[64,8]{0,1:T(8,128)S(1)}, ...), condition=%wide.region_9.13_spmd, body=%wide.region_2.12_spmd.sunk | while | flops 8645694 | bytes 7067533 | solution.py:239
  144.5 1.4 compare_reduce_fusion.4
  146.7 6.3 %conditional.4 = ((f32[64,8]{0,1:T(8,128)S(1)}, f32[64,8]{0,1:T(8,128)S(1)}, f32[64,8,128]{2,0,1:T(8,128)S(1)})) conditional(s32[]{:T(128)} %convert_element_type.210, (f32[64,8]{0,1:T(8,128)S(1)}, f32[64,8]{0,1:T(8,128)S(1)}, f32[64,8,128]{2,0,1:T(8,128)S(1)}) %tuple.131, (s32[8]{0:T(128)S(1)}, s32[32]{0:T(128)S(1)}, s32[]{:T(128)}, ...), branch_computations={%region_4.0_spmd, %region_5.11_spmd} | conditional | flops 8645672 | bytes 7067152 | solution.py:237
  146.7 1.8 dynamic-slice_bitcast_fusion
  153.0 1.4 compare_reduce_fusion.4
  155.1 6.3 %conditional.4 = ((f32[64,8]{0,1:T(8,128)S(1)}, f32[64,8]{0,1:T(8,128)S(1)}, f32[64,8,128]{2,0,1:T(8,128)S(1)})) conditional(s32[]{:T(128)} %convert_element_type.210, (f32[64,8]{0,1:T(8,128)S(1)}, f32[64,8]{0,1:T(8,128)S(1)}, f32[64,8,128]{2,0,1:T(8,128)S(1)}) %tuple.131, (s32[8]{0:T(128)S(1)}, s32[32]{0:T(128)S(1)}, s32[]{:T(128)}, ...), branch_computations={%region_4.0_spmd, %region_5.11_spmd} | conditional | flops 8645672 | bytes 7067152 | solution.py:237
  155.1 1.8 dynamic-slice_bitcast_fusion
  161.4 1.4 compare_reduce_fusion.4
  163.5 1.4 compare_reduce_fusion.4
  166.8 0.8 copy.213
  168.0 1.3 pad_maximum_fusion.1
  169.3 31.2 %all-to-all-start.4 = ((f32[64,2,8,130]{3,2,1,0:T(8,128)}), f32[64,2,8,130]{3,2,1,0:T(8,128)S(1)}, u32[]{:S(2)}, u32[]{:S(2)}) async-start(f32[64,2,8,130]{3,2,1,0:T(8,128)} %pad_maximum_fusion.1), calls=%async_computation.4 | async-start | bytes 2097152 | tf_op jit(solution)/shard_map/all_to_all | solution.py:244
  201.5 27.0 %all-to-all-done.4 = f32[64,2,8,130]{3,2,1,0:T(8,128)S(1)} async-done(((f32[64,2,8,130]{3,2,1,0:T(8,128)}), f32[64,2,8,130]{3,2,1,0:T(8,128)S(1)}, u32[]{:S(2)}, u32[]{:S(2)}) %all-to-all-start.4) | async-done | bytes 532512 | tf_op jit(solution)/shard_map/all_to_all | solution.py:244
  230.3 18.3 %all_to_all.50 = bf16[64,2,1024]{2,1,0:T(2,128)(2,1)S(1)} all-to-all(bf16[64,2,1024]{2,1,0:T(2,128)(2,1)S(1)} %broadcast_in_dim.199), channel_id=1, replica_groups=mesh['seq'=64,'head'=4] {'seq'}, dimensions={0} | all-to-all | bytes 524288 | tf_op jit(solution)/shard_map/all_to_all | solution.py:89
  248.9 1.3 collective-permute-start
  250.2 2.7 collective-permute-done
  253.5 4.9 %collective-permute-done.1 = f32[128,64]{0,1:T(8,128)S(1)} collective-permute-done((f32[128,64]{0,1:T(8,128)S(1)}, f32[128,64]{0,1:T(8,128)S(1)}, u32[]{:S(2)}, u32[]{:S(2)}) %collective-permute-start.1) | collective-permute-done | bytes 32800 | tf_op jit(solution)/shard_map/ppermute | solution.py:101
  258.4 1.3 broadcast_in_dim.200
  259.7 6.2 %all-to-all-start.6 = ((bf16[64,128,64]{1,2,0:T(8,128)(2,1)}), bf16[64,128,64]{1,2,0:T(8,128)(2,1)S(1)}, u32[]{:S(2)}, u32[]{:S(2)}) async-start(bf16[64,128,64]{1,2,0:T(8,128)(2,1)} %broadcast_in_dim.200), calls=%async_computation.6 | async-start | bytes 2097152 | tf_op jit(solution)/shard_map/all_to_all | solution.py:89
  266.0 27.8 %all-to-all-done.6 = bf16[64,128,64]{1,2,0:T(8,128)(2,1)S(1)} async-done(((bf16[64,128,64]{1,2,0:T(8,128)(2,1)}), bf16[64,128,64]{1,2,0:T(8,128)(2,1)S(1)}, u32[]{:S(2)}, u32[]{:S(2)}) %all-to-all-start.6) | async-done | bytes 1048608 | tf_op jit(solution)/shard_map/all_to_all | solution.py:89
  295.1 1.1 fusion.52
  296.5 34.5 %all_to_all.51 = bf16[64,128,64]{1,2,0:T(8,128)(2,1)S(1)} all-to-all(bf16[64,128,64]{1,2,0:T(8,128)(2,1)S(1)} %broadcast_in_dim.201), channel_id=1, replica_groups=mesh['seq'=64,'head'=4] {'seq'}, dimensions={0} | all-to-all | bytes 2097152 | tf_op jit(solution)/shard_map/all_to_all | solution.py:89
  331.3 1.3 collective-permute-start.2
  332.6 2.7 collective-permute-done.2
  335.8 4.9 %collective-permute-done.3 = f32[128,64]{0,1:T(8,128)S(1)} collective-permute-done((f32[128,64]{0,1:T(8,128)S(1)}, f32[128,64]{0,1:T(8,128)S(1)}, u32[]{:S(2)}, u32[]{:S(2)}) %collective-permute-start.3) | collective-permute-done | bytes 32800 | tf_op jit(solution)/shard_map/ppermute | solution.py:101
  (188 shorter events, 34.7 us)
Async XLA Ops:
  0.0 331.0 %copy-start = (bf16[64,4096]{1,0:T(8,128)(2,1)S(1)}, bf16[64,4096]{1,0:T(8,128)(2,1)}, u32[]{:S(2)}) copy-start(bf16[64,4096]{1,0:T(8,128)(2,1)} %param.39) | copy-start | bytes 1572868
  0.0 29.0 %copy-start.6 = (bf16[64,4096]{1,0:T(8,128)(2,1)S(1)}, bf16[64,4096]{1,0:T(8,128)(2,1)}, u32[]{:S(2)}) copy-start(bf16[64,4096]{1,0:T(8,128)(2,1)} %param.38) | copy-start | bytes 1572868
  1.5 21.6 %all-to-all-start.1 = ((f32[64,1,128]{2,1,0:T(1,128)}), f32[64,1,128]{2,1,0:T(1,128)S(1)}, u32[]{:S(2)}, u32[]{:S(2)}) async-start(f32[64,1,128]{2,1,0:T(1,128)} %reshape.542), calls=%async_computation.1 | async-start | bytes 65536 | tf_op jit(solution)/shard_map/all_to_all | solution.py:89
  14.5 9.8 %copy-start.9 = (bf16[128,64]{0,1:T(8,128)(2,1)}, bf16[128,64]{0,1:T(8,128)(2,1)S(1)}, u32[]{:S(2)}) copy-start(bf16[128,64]{0,1:T(8,128)(2,1)S(1)} %copy.235) | copy-start | bytes 49156
  23.1 1.2 copy-start.12
  24.3 32.8 %all-to-all-start = ((bf16[64,128,64]{1,2,0:T(8,128)(2,1)}), bf16[64,128,64]{1,2,0:T(8,128)(2,1)S(1)}, u32[]{:S(2)}, u32[]{:S(2)}) async-start(bf16[64,128,64]{1,2,0:T(8,128)(2,1)} %broadcast_in_dim.195), calls=%async_computation | async-start | bytes 2097152 | tf_op jit(solution)/shard_map/all_to_all | solution.py:89
  29.0 2.8 copy-start.7
  34.6 29.7 %copy-start.13 = (f32[64,1,128]{2,1,0:T(1,128)S(1)}, f32[64,1,128]{2,1,0:T(1,128)}, u32[]{:S(2)}) copy-start(f32[64,1,128]{2,1,0:T(1,128)} %copy-done.12) | copy-start | bytes 98308
  57.1 34.7 %all-to-all-start.2 = ((bf16[64,64,112]{2,0,1:T(8,128)(2,1)}), bf16[64,64,112]{2,0,1:T(8,128)(2,1)S(1)}, u32[]{:S(2)}, u32[]{:S(2)}) async-start(bf16[64,64,112]{2,0,1:T(8,128)(2,1)} %pad_maximum_fusion), calls=%async_computation.2 | async-start | bytes 2097152 | tf_op jit(solution)/shard_map/all_to_all | solution.py:191
  91.9 3.2 copy-start.4
  94.0 30.9 %copy-start.1 = (s32[64]{0:T(128)S(1)}, s32[64]{0:T(128)}, u32[]{:S(2)}) copy-start(s32[64]{0:T(128)} %param.28) | copy-start | bytes 772
  94.0 30.9 %copy-start.8 = (f32[8]{0:T(128)S(1)}, f32[8]{0:T(128)}, u32[]{:S(2)}) copy-start(f32[8]{0:T(128)} %param.33) | copy-start | bytes 100
  94.0 30.9 %copy-start.15 = (s32[32]{0:T(128)S(1)}, s32[32]{0:T(128)}, u32[]{:S(2)}) copy-start(s32[32]{0:T(128)} %param.30) | copy-start | bytes 388
  94.0 30.9 %copy-start.16 = (s32[32]{0:T(128)S(1)}, s32[32]{0:T(128)}, u32[]{:S(2)}) copy-start(s32[32]{0:T(128)} %param.29) | copy-start | bytes 388
  95.0 29.5 %all-to-all-start.3 = ((bf16[64,128,48]{1,2,0:T(8,128)(2,1)}), bf16[64,128,48]{1,2,0:T(8,128)(2,1)S(1)}, u32[]{:S(2)}, u32[]{:S(2)}) async-start(bf16[64,128,48]{1,2,0:T(8,128)(2,1)} %broadcast_in_dim.197), calls=%async_computation.3 | async-start | bytes 1572864 | tf_op jit(solution)/shard_map/all_to_all | solution.py:89
  124.5 0.9 copy-start.2
  143.9 0.6 copy-start.17
  144.5 21.2 %copy-start.18 = (f32[64,8]{0,1:T(8,128)S(1)}, f32[64,8]{0,1:T(8,128)}, u32[]{:S(2)}) copy-start(f32[64,8]{0,1:T(8,128)} %copy-done.17) | copy-start | bytes 6148
  168.0 32.5 %copy-start.3 = (bf16[64,128,48]{1,2,0:T(8,128)(2,1)S(1)}, bf16[64,128,48]{1,2,0:T(8,128)(2,1)}, u32[]{:S(2)}) copy-start(bf16[64,128,48]{1,2,0:T(8,128)(2,1)} %copy-done.2) | copy-start | bytes 2359300
  169.3 59.3 %all-to-all-start.4 = ((f32[64,2,8,130]{3,2,1,0:T(8,128)}), f32[64,2,8,130]{3,2,1,0:T(8,128)S(1)}, u32[]{:S(2)}, u32[]{:S(2)}) async-start(f32[64,2,8,130]{3,2,1,0:T(8,128)} %pad_maximum_fusion.1), calls=%async_computation.4 | async-start | bytes 2097152 | tf_op jit(solution)/shard_map/all_to_all | solution.py:244
  228.8 19.9 %copy-start.11 = (bf16[64,1024]{1,0:T(8,128)(2,1)S(1)}, bf16[64,1024]{1,0:T(8,128)(2,1)}, u32[]{:S(2)}) copy-start(bf16[64,1024]{1,0:T(8,128)(2,1)} %param.37) | copy-start | bytes 393220
  228.9 29.5 %copy-start.10 = (bf16[128,64]{0,1:T(8,128)(2,1)S(1)}, bf16[128,64]{0,1:T(8,128)(2,1)}, u32[]{:S(2)}) copy-start(bf16[128,64]{0,1:T(8,128)(2,1)} %copy-done.9) | copy-start | bytes 49156
  248.6 17.3 %copy-start.14 = (f32[64,64]{1,0:T(8,128)S(1)}, f32[64,64]{1,0:T(8,128)}, u32[]{:S(2)}) copy-start(f32[64,64]{1,0:T(8,128)} %get-tuple-element.776) | copy-start | bytes 49156
  248.9 4.0 %collective-permute-start = (f32[128,64]{0,1:T(8,128)S(1)}, f32[128,64]{0,1:T(8,128)S(1)}, u32[]{:S(2)}, u32[]{:S(2)}) collective-permute-start(f32[128,64]{0,1:T(8,128)S(1)} %fusion.74), channel_id=1, source_target_pairs={{0,1},{1,0},{2,3},{3,2},{4,5},{5,4},{6,7},{7,6},{8,9},{9,8},{10,11... | collective-permute-start | bytes 98312 | tf_op jit(solution)/shard_map/ppermute | solution.py:101
  252.9 5.4 %collective-permute-start.1 = (f32[128,64]{0,1:T(8,128)S(1)}, f32[128,64]{0,1:T(8,128)S(1)}, u32[]{:S(2)}, u32[]{:S(2)}) collective-permute-start(f32[128,64]{0,1:T(8,128)S(1)} %add.210), channel_id=1, source_target_pairs={{0,2},{1,3},{2,0},{3,1},{4,6},{5,7},{6,4},{7,5},{8,10},{9,11},{10,... | collective-permute-start | bytes 98312 | tf_op jit(solution)/shard_map/ppermute | solution.py:101
  259.7 34.2 %all-to-all-start.6 = ((bf16[64,128,64]{1,2,0:T(8,128)(2,1)}), bf16[64,128,64]{1,2,0:T(8,128)(2,1)S(1)}, u32[]{:S(2)}, u32[]{:S(2)}) async-start(bf16[64,128,64]{1,2,0:T(8,128)(2,1)} %broadcast_in_dim.200), calls=%async_computation.6 | async-start | bytes 2097152 | tf_op jit(solution)/shard_map/all_to_all | solution.py:89
  265.9 29.2 %copy-start.5 = (bf16[64,64,112]{2,0,1:T(8,128)(2,1)S(1)}, bf16[64,64,112]{2,0,1:T(8,128)(2,1)}, u32[]{:S(2)}) copy-start(bf16[64,64,112]{2,0,1:T(8,128)(2,1)} %copy-done.4) | copy-start | bytes 2752516
  331.3 4.0 %collective-permute-start.2 = (f32[128,64]{0,1:T(8,128)S(1)}, f32[128,64]{0,1:T(8,128)S(1)}, u32[]{:S(2)}, u32[]{:S(2)}) collective-permute-start(f32[128,64]{0,1:T(8,128)S(1)} %fusion.75), channel_id=1, source_target_pairs={{0,1},{1,0},{2,3},{3,2},{4,5},{5,4},{6,7},{7,6},{8,9},{9,8},{10,11... | collective-permute-start | bytes 98312 | tf_op jit(solution)/shard_map/ppermute | solution.py:101
  335.3 5.4 %collective-permute-start.3 = (f32[128,64]{0,1:T(8,128)S(1)}, f32[128,64]{0,1:T(8,128)S(1)}, u32[]{:S(2)}, u32[]{:S(2)}) collective-permute-start(f32[128,64]{0,1:T(8,128)S(1)} %add.214), channel_id=1, source_target_pairs={{0,2},{1,3},{2,0},{3,1},{4,6},{5,7},{6,4},{7,5},{8,10},{9,11},{10,... | collective-permute-start | bytes 98312 | tf_op jit(solution)/shard_map/ppermute | solution.py:101

commit v4 on v3

--- a/solution.py
+++ b/solution.py
@@ -181,23 +181,27 @@
 
     qkv_chunk = qkv_width // nseq
     up_chunk = w_up.shape[1] // nseq
-    both = jnp.concatenate(
-        [
-            w_qkv.reshape(local_width, nseq, qkv_chunk),
-            w_up.reshape(local_width, nseq, up_chunk),
-        ],
-        axis=2,
-    )
-    both = lax.all_to_all(both, "seq", 1, 0, tiled=True).reshape(nseq * local_width, qkv_chunk + up_chunk)
-    qkv_cols = both[:, :qkv_chunk]
-    up_cols = both[:, qkv_chunk:]
-    gains = gather_cols(jnp.stack([norm1_gain, norm2_gain]), nseq)
+    gain_pair = jnp.stack([norm1_gain, norm2_gain])
+    gain_parts = []
+    for _ in range(3):
+        piece = lax.optimization_barrier(gain_pair.astype(jnp.bfloat16))
+        gain_parts.append(piece)
+        gain_pair = gain_pair - piece.astype(jnp.float32)
 
     token_rows = tokens.reshape(rows, local_width)
     token_float = token_rows.astype(jnp.float32)
-    normed = full_normalize(gather_cols(token_rows, nseq), gains[0])
+    gathered = gather_cols(jnp.concatenate([token_rows] + gain_parts, axis=0), nseq)
+    qkv_in, gathered = lax.optimization_barrier(
+        (w_qkv.reshape(local_width, nseq, qkv_chunk), gathered)
+    )
+    qkv_cols = lax.all_to_all(qkv_in, "seq", 1, 0, tiled=True).reshape(nseq * local_width, qkv_chunk)
+    pieces = gathered[rows:].astype(jnp.float32)
+    gains = (pieces[0:2] + pieces[2:4]) + pieces[4:6]
+    normed = full_normalize(gathered[:rows], gains[0])
     qkv_part = jnp.dot(normed, qkv_cols, preferred_element_type=jnp.float32).astype(jnp.bfloat16)
     joined = gather_cols(qkv_part, nseq)
+    up_in, joined = lax.optimization_barrier((w_up.reshape(local_width, nseq, up_chunk), joined))
+    up_cols = lax.all_to_all(up_in, "seq", 1, 0, tiled=True).reshape(nseq * local_width, up_chunk)
     all_queries = joined[:, :head_width].reshape(nsteps, requests, nheads, head_size)
     new_keys = joined[:, head_width : 2 * head_width].reshape(nsteps, requests, nheads, head_size)
     new_values = joined[:, 2 * head_width :].reshape(nsteps, requests, nheads, head_size)
@@ -238,15 +242,24 @@
 
         states.append(lax.fori_loop(0, nblocks, visit, carry_state))
 
-    run_max, run_sum, run_out = (jnp.concatenate(parts, axis=0) for parts in zip(*states))
-    packed = jnp.concatenate([run_out, run_max[:, :, None], run_sum[:, :, None]], axis=2)
+    joined_state = tuple(jnp.concatenate(parts, axis=0) for parts in zip(*states))
+    up_cols, (run_max, run_sum, run_out) = lax.optimization_barrier((up_cols, joined_state))
     own_rows = rows // nseq
-    packed = lax.all_to_all(
-        packed.reshape(nseq, own_rows, nheads, head_size + 2), "seq", 0, 0, tiled=True
-    )
-    part_out = packed[:, :, :, :head_size]
-    part_max = packed[:, :, :, head_size]
-    part_sum = packed[:, :, :, head_size + 1]
+    stats = jnp.concatenate(
+        [
+            jnp.swapaxes(run_max.reshape(nseq, own_rows, nheads), 1, 2),
+            jnp.swapaxes(run_sum.reshape(nseq, own_rows, nheads), 1, 2),
+            jnp.zeros((nseq, nheads, head_size - 2 * own_rows), jnp.float32),
+        ],
+        axis=2,
+    )
+    packed = jnp.concatenate(
+        [run_out.reshape(nseq, own_rows, nheads, head_size), stats[:, None]], axis=1
+    )
+    packed = lax.all_to_all(packed, "seq", 0, 0, tiled=True)
+    part_out = packed[:, :own_rows]
+    part_max = jnp.swapaxes(packed[:, own_rows, :, :own_rows], 1, 2)
+    part_sum = jnp.swapaxes(packed[:, own_rows, :, own_rows : 2 * own_rows], 1, 2)
     top_max = jnp.max(part_max, axis=0)
     rescale = jnp.exp(part_max - top_max[None])
     top_sum = jnp.sum(part_sum * rescale, axis=0)

time: 343 us -> 368 us (1.073)
  blocking collectives: 52.9 us -> 86.5 us
  waiting for transfers between devices: 145 us -> 123 us
  local copies, waits for them, and re-layouts: 33.1 us -> 42 us
    all_to_all x2 -> x3, blocking collectives: 52.9 us -> 86.5 us  [gather_rows(): return lax.all_to_all(copies, 'seq', 0, 0, tiled=True)]
    all_to_all x2 -> x3, starting transfers between devices: 37.7 us -> 52.3 us  [the longest x1 40 us: on_device(): packed = lax.all_to_all(packed, 'seq', 0, 0, tiled=True)]
    all_to_all x2 -> x3, waiting for transfers between devices: 50.8 us -> 36.4 us  [the longest x1 21.9 us: on_device(): packed = lax.all_to_all(packed, 'seq', 0, 0, tiled=True)]
    all_to_all x4 -> x2, starting transfers between devices: 29.8 us -> 18.5 us  [gather_rows(): return lax.all_to_all(copies, 'seq', 0, 0, tiled=True)]
    all_to_all x4 -> x2, waiting for transfers between devices: 78.8 us -> 71.7 us  [gather_rows(): return lax.all_to_all(copies, 'seq', 0, 0, tiled=True)]
    unnamed x46 -> x32, local copies, waits for them, and re-layouts: 3.85 us -> 7.65 us
  transfers between devices with their start and end apart: 10 -> 9, of which waited for: 10 -> 8; matrix products, arithmetic and copies ran while one was open for 4% -> 13% of each run, Pallas kernels for 0% -> 0%
where the time goes in v4:
time: 368 us; the launch traced here: 367 us
  waiting for transfers between devices  123 us (33%)
  blocking collectives  86.5 us (24%)
  starting transfers between devices  74.4 us (20%)
  local copies, waits for them, and re-layouts  42 us (11%)
  other arithmetic  24.4 us (7%)
  matrix products  10.5 us (3%)
  loops' own time  5.16 us (1%)
    all_to_all x3, blocking collectives, gather_rows(): return lax.all_to_all(copies, 'seq', 0, 0, tiled=True)  86.5 us
    all_to_all x2, waiting for transfers between devices, gather_rows(): return lax.all_to_all(copies, 'seq', 0, 0, tiled=True)  71.7 us
    all_to_all x1, starting transfers between devices, on_device(): packed = lax.all_to_all(packed, 'seq', 0, 0, tiled=True)  40 us
    all_to_all x1, waiting for transfers between devices, on_device(): packed = lax.all_to_all(packed, 'seq', 0, 0, tiled=True)  21.9 us
    all_to_all x2, starting transfers between devices, gather_rows(): return lax.all_to_all(copies, 'seq', 0, 0, tiled=True)  18.5 us
    ppermute x4, waiting for transfers between devices, head_sum(): other = lax.ppermute(part, 'head', [(i, i ^ stride) for i in range(nhead)])  15.3 us
    all_to_all x1, waiting for transfers between devices, on_device(): lax.all_to_all(qkv_in, 'seq', 1, 0, tiled=True)  14.4 us
    reduce_or x8, other arithmetic, visit(): return lax.cond(jnp.any(owners >= 0), compute, keep_state, state_in)  11.1 us
  transfers between devices with their start and end apart: 9, of which 8 were waited for; matrix products, arithmetic and copies ran while one was open for 13% of the time, Pallas kernels for 0%

profile of v4, /device:TPU:4, one launch (start us, length us, event | category | flops | bytes accessed | tf_op | source)
XLA Modules:
  0.0 366.9 jit_solution(6210114702318891265)
XLA Ops:
  3.4 1.6 broadcast_in_dim.194
  5.0 12.2 %all-to-all-start = ((bf16[64,134,64]{1,2,0:T(8,128)(2,1)}), bf16[64,134,64]{1,2,0:T(8,128)(2,1)S(1)}, u32[]{:S(2)}, u32[]{:S(2)}) async-start(bf16[64,134,64]{1,2,0:T(8,128)(2,1)} %broadcast_in_dim.194), calls=%async_computation | async-start | bytes 4194304 | tf_op jit(solution)/shard_map/all_to_all | solution.py:89
  18.4 50.0 %all-to-all-done = bf16[64,134,64]{1,2,0:T(8,128)(2,1)S(1)} async-done(((bf16[64,134,64]{1,2,0:T(8,128)(2,1)}), bf16[64,134,64]{1,2,0:T(8,128)(2,1)S(1)}, u32[]{:S(2)}, u32[]{:S(2)}) %all-to-all-start) | async-done | bytes 1097760 | tf_op jit(solution)/shard_map/all_to_all | solution.py:89
  68.4 2.6 copy.160
  71.0 1.6 convert_reduce_fusion
  73.5 2.7 reshape.536
  76.1 5.9 %all-to-all-start.1 = ((bf16[64,2,1536]{2,1,0:T(2,128)(2,1)}), bf16[64,2,1536]{2,1,0:T(2,128)(2,1)S(1)}, u32[]{:S(2)}, u32[]{:S(2)}) async-start(bf16[64,2,1536]{2,1,0:T(2,128)(2,1)} %reshape.536), calls=%async_computation.1 | async-start | bytes 786432 | tf_op jit(solution)/shard_map/all_to_all | solution.py:197
  82.1 14.4 %all-to-all-done.1 = bf16[64,2,1536]{2,1,0:T(2,128)(2,1)S(1)} async-done(((bf16[64,2,1536]{2,1,0:T(2,128)(2,1)}), bf16[64,2,1536]{2,1,0:T(2,128)(2,1)S(1)}, u32[]{:S(2)}, u32[]{:S(2)}) %all-to-all-start.1) | async-done | bytes 393248 | tf_op jit(solution)/shard_map/all_to_all | solution.py:197
  99.8 6.3 %all-to-all-start.2 = ((bf16[64,128,48]{1,2,0:T(8,128)(2,1)}), bf16[64,128,48]{1,2,0:T(8,128)(2,1)S(1)}, u32[]{:S(2)}, u32[]{:S(2)}) async-start(bf16[64,128,48]{1,2,0:T(8,128)(2,1)} %broadcast_in_dim.195), calls=%async_computation.2 | async-start | bytes 1572864 | tf_op jit(solution)/shard_map/all_to_all | solution.py:89
  107.2 21.7 %all-to-all-done.2 = bf16[64,128,48]{1,2,0:T(8,128)(2,1)S(1)} async-done(((bf16[64,128,48]{1,2,0:T(8,128)(2,1)}), bf16[64,128,48]{1,2,0:T(8,128)(2,1)S(1)}, u32[]{:S(2)}, u32[]{:S(2)}) %all-to-all-start.2) | async-done | bytes 786464 | tf_op jit(solution)/shard_map/all_to_all | solution.py:89
  130.8 1.6 reshape.538
  132.3 6.5 %all-to-all-start.3 = ((bf16[64,2,2048]{2,1,0:T(2,128)(2,1)}), bf16[64,2,2048]{2,1,0:T(2,128)(2,1)S(1)}, u32[]{:S(2)}, u32[]{:S(2)}) async-start(bf16[64,2,2048]{2,1,0:T(2,128)(2,1)} %reshape.538), calls=%async_computation.3 | async-start | bytes 1048576 | tf_op jit(solution)/shard_map/all_to_all | solution.py:204
  138.9 21.9 %while.34 = (s32[]{:T(128)}, f32[64,8]{0,1:T(8,128)S(1)}, f32[64,8]{0,1:T(8,128)S(1)}, f32[64,8,128]{2,0,1:T(8,128)S(1)}, s32[32]{0:T(128)}, /*index=5*/s32[32]{...) while((s32[]{:T(128)}, f32[64,8]{0,1:T(8,128)S(1)}, ...), condition=%wide.region_9.13_spmd, body=%wide.region_2.12_spmd.sunk | while | flops 8645694 | bytes 7067525 | solution.py:243
  138.9 1.3 compare_reduce_fusion.4
  140.8 7.1 %conditional.4 = ((f32[64,8]{0,1:T(8,128)S(1)}, f32[64,8]{0,1:T(8,128)S(1)}, f32[64,8,128]{2,0,1:T(8,128)S(1)})) conditional(s32[]{:T(128)} %convert_element_type.242, (f32[64,8]{0,1:T(8,128)S(1)}, f32[64,8]{0,1:T(8,128)S(1)}, f32[64,8,128]{2,0,1:T(8,128)S(1)}) %tuple.130, (s32[8]{0:T(128)S(1)}, s32[32]{0:T(128)S(1)}, s32[]{:T(128)}, ...), branch_computations={%region_4.0_spmd, %region_5.11_spmd} | conditional | flops 8645672 | bytes 7067152 | solution.py:241
  141.7 1.5 gather_fusion.1
  143.3 1.8 dynamic-slice_bitcast_fusion
  147.9 1.4 compare_reduce_fusion.4
  149.8 7.1 %conditional.4 = ((f32[64,8]{0,1:T(8,128)S(1)}, f32[64,8]{0,1:T(8,128)S(1)}, f32[64,8,128]{2,0,1:T(8,128)S(1)})) conditional(s32[]{:T(128)} %convert_element_type.242, (f32[64,8]{0,1:T(8,128)S(1)}, f32[64,8]{0,1:T(8,128)S(1)}, f32[64,8,128]{2,0,1:T(8,128)S(1)}) %tuple.130, (s32[8]{0:T(128)S(1)}, s32[32]{0:T(128)S(1)}, s32[]{:T(128)}, ...), branch_computations={%region_4.0_spmd, %region_5.11_spmd} | conditional | flops 8645672 | bytes 7067152 | solution.py:241
  150.7 1.5 gather_fusion.1
  152.3 1.8 dynamic-slice_bitcast_fusion
  156.9 1.4 compare_reduce_fusion.4
  158.9 1.3 compare_reduce_fusion.4
  161.4 25.1 %while.35 = (s32[]{:T(128)}, f32[64,8]{0,1:T(8,128)S(1)}, f32[64,8]{0,1:T(8,128)}, f32[64,8,128]{2,0,1:T(8,128)S(1)}, s32[32]{0:T(128)}, /*index=5*/s32[32]{0:T(...) while((s32[]{:T(128)}, f32[64,8]{0,1:T(8,128)S(1)}, ...), condition=%wide.region_17.21_spmd, body=%wide.region_10.20_spmd.sunk | while | flops 8645702 | bytes 7067557 | solution.py:243
  161.4 1.4 compare_reduce_fusion.5
  163.5 8.4 %conditional.5 = ((f32[64,8]{0,1:T(8,128)S(1)}, f32[64,8]{0,1:T(8,128)}, f32[64,8,128]{2,0,1:T(8,128)S(1)})) conditional(s32[]{:T(128)} %convert_element_type.243, (f32[64,8]{0,1:T(8,128)S(1)}, f32[64,8]{0,1:T(8,128)}, f32[64,8,128]{2,0,1:T(8,128)S(1)}) %tuple.134, (s32[8]{0:T(128)S(1)}, s32[32]{0:T(128)S(1)}, s32[]{:T(128)}, s32[64]{0:T(128)S(1)}, ...), branch_computations={%region_12.15_spmd, %region_13.19_spmd} | conditional | flops 8645680 | bytes 7067184 | solution.py:241
  164.4 1.5 gather_fusion.4
  166.0 1.8 dynamic-slice_bitcast_fusion.2
  170.4 1.5 convolution_add_fusion.3
  171.9 1.4 compare_reduce_fusion.5
  173.9 8.4 %conditional.5 = ((f32[64,8]{0,1:T(8,128)S(1)}, f32[64,8]{0,1:T(8,128)}, f32[64,8,128]{2,0,1:T(8,128)S(1)})) conditional(s32[]{:T(128)} %convert_element_type.243, (f32[64,8]{0,1:T(8,128)S(1)}, f32[64,8]{0,1:T(8,128)}, f32[64,8,128]{2,0,1:T(8,128)S(1)}) %tuple.134, (s32[8]{0:T(128)S(1)}, s32[32]{0:T(128)S(1)}, s32[]{:T(128)}, s32[64]{0:T(128)S(1)}, ...), branch_computations={%region_12.15_spmd, %region_13.19_spmd} | conditional | flops 8645680 | bytes 7067184 | solution.py:241
  174.8 1.5 gather_fusion.4
  176.4 1.8 dynamic-slice_bitcast_fusion.2
  180.8 1.5 convolution_add_fusion.3
  182.3 1.4 compare_reduce_fusion.5
  184.4 1.4 compare_reduce_fusion.5
  189.6 1.6 reshape.452
  193.7 40.0 %all-to-all-start.4 = ((f32[64,3,8,128]{3,2,1,0:T(8,128)}), f32[64,3,8,128]{3,2,1,0:T(8,128)S(1)}, u32[]{:S(2)}, u32[]{:S(2)}) async-start(f32[64,3,8,128]{3,2,1,0:T(8,128)} %pad_maximum_fusion), calls=%async_computation.4 | async-start | bytes 1572864 | tf_op jit(solution)/shard_map/all_to_all | solution.py:259
  234.6 21.9 %all-to-all-done.4 = f32[64,3,8,128]{3,2,1,0:T(8,128)S(1)} async-done(((f32[64,3,8,128]{3,2,1,0:T(8,128)}), f32[64,3,8,128]{3,2,1,0:T(8,128)S(1)}, u32[]{:S(2)}, u32[]{:S(2)}) %all-to-all-start.4) | async-done | bytes 786464 | tf_op jit(solution)/shard_map/all_to_all | solution.py:259
  257.9 18.1 %all_to_all.60 = bf16[64,2,1024]{2,1,0:T(2,128)(2,1)S(1)} all-to-all(bf16[64,2,1024]{2,1,0:T(2,128)(2,1)S(1)} %broadcast_in_dim.199), channel_id=1, replica_groups=mesh['seq'=64,'head'=4] {'seq'}, dimensions={0} | all-to-all | bytes 524288 | tf_op jit(solution)/shard_map/all_to_all | solution.py:89
  276.3 1.3 collective-permute-start
  277.5 2.7 collective-permute-done
  280.8 4.9 %collective-permute-done.1 = f32[128,64]{0,1:T(8,128)S(1)} collective-permute-done((f32[128,64]{0,1:T(8,128)S(1)}, f32[128,64]{0,1:T(8,128)S(1)}, u32[]{:S(2)}, u32[]{:S(2)}) %collective-permute-start.1) | collective-permute-done | bytes 32800 | tf_op jit(solution)/shard_map/ppermute | solution.py:101
  285.9 34.0 %all_to_all.61 = bf16[64,128,64]{1,2,0:T(8,128)(2,1)S(1)} all-to-all(bf16[64,128,64]{1,2,0:T(8,128)(2,1)S(1)} %broadcast_in_dim.200), channel_id=1, replica_groups=mesh['seq'=64,'head'=4] {'seq'}, dimensions={0} | all-to-all | bytes 2097152 | tf_op jit(solution)/shard_map/all_to_all | solution.py:89
  321.9 34.5 %all_to_all.62 = bf16[64,128,64]{1,2,0:T(8,128)(2,1)S(1)} all-to-all(bf16[64,128,64]{1,2,0:T(8,128)(2,1)S(1)} %broadcast_in_dim.201), channel_id=1, replica_groups=mesh['seq'=64,'head'=4] {'seq'}, dimensions={0} | all-to-all | bytes 2097152 | tf_op jit(solution)/shard_map/all_to_all | solution.py:89
  356.7 1.3 collective-permute-start.2
  358.0 2.7 collective-permute-done.2
  361.2 4.9 %collective-permute-done.3 = f32[128,64]{0,1:T(8,128)S(1)} collective-permute-done((f32[128,64]{0,1:T(8,128)S(1)}, f32[128,64]{0,1:T(8,128)S(1)}, u32[]{:S(2)}, u32[]{:S(2)}) %collective-permute-start.3) | collective-permute-done | bytes 32800 | tf_op jit(solution)/shard_map/ppermute | solution.py:101
  (178 shorter events, 39.3 us)
Async XLA Ops:
  0.0 356.4 %copy-start = (bf16[64,4096]{1,0:T(8,128)(2,1)S(1)}, bf16[64,4096]{1,0:T(8,128)(2,1)}, u32[]{:S(2)}) copy-start(bf16[64,4096]{1,0:T(8,128)(2,1)} %param.39) | copy-start | bytes 1572868
  5.0 12.3 %copy-start.6 = (bf16[64,3,1024]{2,0,1:T(8,128)(2,1)S(1)}, bf16[64,3,1024]{2,0,1:T(8,128)(2,1)}, u32[]{:S(2)}) copy-start(bf16[64,3,1024]{2,0,1:T(8,128)(2,1)} %param.36) | copy-start | bytes 1179652
  5.0 63.4 %all-to-all-start = ((bf16[64,134,64]{1,2,0:T(8,128)(2,1)}), bf16[64,134,64]{1,2,0:T(8,128)(2,1)S(1)}, u32[]{:S(2)}, u32[]{:S(2)}) async-start(bf16[64,134,64]{1,2,0:T(8,128)(2,1)} %broadcast_in_dim.194), calls=%async_computation | async-start | bytes 4194304 | tf_op jit(solution)/shard_map/all_to_all | solution.py:89
  76.1 20.4 %all-to-all-start.1 = ((bf16[64,2,1536]{2,1,0:T(2,128)(2,1)}), bf16[64,2,1536]{2,1,0:T(2,128)(2,1)S(1)}, u32[]{:S(2)}, u32[]{:S(2)}) async-start(bf16[64,2,1536]{2,1,0:T(2,128)(2,1)} %reshape.536), calls=%async_computation.1 | async-start | bytes 786432 | tf_op jit(solution)/shard_map/all_to_all | solution.py:197
  97.0 1.3 copy-start.2
  98.3 7.9 %copy-start.4 = (bf16[64,4096]{1,0:T(8,128)(2,1)S(1)}, bf16[64,4096]{1,0:T(8,128)(2,1)}, u32[]{:S(2)}) copy-start(bf16[64,4096]{1,0:T(8,128)(2,1)} %param.38) | copy-start | bytes 1572868
  99.8 29.2 %all-to-all-start.2 = ((bf16[64,128,48]{1,2,0:T(8,128)(2,1)}), bf16[64,128,48]{1,2,0:T(8,128)(2,1)S(1)}, u32[]{:S(2)}, u32[]{:S(2)}) async-start(bf16[64,128,48]{1,2,0:T(8,128)(2,1)} %broadcast_in_dim.195), calls=%async_computation.2 | async-start | bytes 1572864 | tf_op jit(solution)/shard_map/all_to_all | solution.py:89
  129.1 9.7 %copy-start.1 = (s32[64]{0:T(128)S(1)}, s32[64]{0:T(128)}, u32[]{:S(2)}) copy-start(s32[64]{0:T(128)} %param.28) | copy-start | bytes 772
  129.1 9.7 %copy-start.7 = (f32[8]{0:T(128)S(1)}, f32[8]{0:T(128)}, u32[]{:S(2)}) copy-start(f32[8]{0:T(128)} %param.33) | copy-start | bytes 100
  129.1 9.7 %copy-start.9 = (s32[32]{0:T(128)S(1)}, s32[32]{0:T(128)}, u32[]{:S(2)}) copy-start(s32[32]{0:T(128)} %param.30) | copy-start | bytes 388
  132.3 55.8 %all-to-all-start.3 = ((bf16[64,2,2048]{2,1,0:T(2,128)(2,1)}), bf16[64,2,2048]{2,1,0:T(2,128)(2,1)S(1)}, u32[]{:S(2)}, u32[]{:S(2)}) async-start(bf16[64,2,2048]{2,1,0:T(2,128)(2,1)} %reshape.538), calls=%async_computation.3 | async-start | bytes 1048576 | tf_op jit(solution)/shard_map/all_to_all | solution.py:204
  160.8 0.6 copy-start.10
  188.9 3.4 copy-start.3
  189.6 3.1 copy-start.11
  193.7 62.8 %all-to-all-start.4 = ((f32[64,3,8,128]{3,2,1,0:T(8,128)}), f32[64,3,8,128]{3,2,1,0:T(8,128)S(1)}, u32[]{:S(2)}, u32[]{:S(2)}) async-start(f32[64,3,8,128]{3,2,1,0:T(8,128)} %pad_maximum_fusion), calls=%async_computation.4 | async-start | bytes 1572864 | tf_op jit(solution)/shard_map/all_to_all | solution.py:259
  234.3 41.8 %copy-start.8 = (bf16[64,1024]{1,0:T(8,128)(2,1)S(1)}, bf16[64,1024]{1,0:T(8,128)(2,1)}, u32[]{:S(2)}) copy-start(bf16[64,1024]{1,0:T(8,128)(2,1)} %param.37) | copy-start | bytes 393220
  276.3 4.0 %collective-permute-start = (f32[128,64]{0,1:T(8,128)S(1)}, f32[128,64]{0,1:T(8,128)S(1)}, u32[]{:S(2)}, u32[]{:S(2)}) collective-permute-start(f32[128,64]{0,1:T(8,128)S(1)} %fusion.81), channel_id=1, source_target_pairs={{0,1},{1,0},{2,3},{3,2},{4,5},{5,4},{6,7},{7,6},{8,9},{9,8},{10,11... | collective-permute-start | bytes 98312 | tf_op jit(solution)/shard_map/ppermute | solution.py:101
  280.3 5.4 %collective-permute-start.1 = (f32[128,64]{0,1:T(8,128)S(1)}, f32[128,64]{0,1:T(8,128)S(1)}, u32[]{:S(2)}, u32[]{:S(2)}) collective-permute-start(f32[128,64]{0,1:T(8,128)S(1)} %add.218), channel_id=1, source_target_pairs={{0,2},{1,3},{2,0},{3,1},{4,6},{5,7},{6,4},{7,5},{8,10},{9,11},{10,... | collective-permute-start | bytes 98312 | tf_op jit(solution)/shard_map/ppermute | solution.py:101
  319.9 1.3 copy-start.5
  356.7 4.0 %collective-permute-start.2 = (f32[128,64]{0,1:T(8,128)S(1)}, f32[128,64]{0,1:T(8,128)S(1)}, u32[]{:S(2)}, u32[]{:S(2)}) collective-permute-start(f32[128,64]{0,1:T(8,128)S(1)} %fusion.82), channel_id=1, source_target_pairs={{0,1},{1,0},{2,3},{3,2},{4,5},{5,4},{6,7},{7,6},{8,9},{9,8},{10,11... | collective-permute-start | bytes 98312 | tf_op jit(solution)/shard_map/ppermute | solution.py:101
  360.7 5.4 %collective-permute-start.3 = (f32[128,64]{0,1:T(8,128)S(1)}, f32[128,64]{0,1:T(8,128)S(1)}, u32[]{:S(2)}, u32[]{:S(2)}) collective-permute-start(f32[128,64]{0,1:T(8,128)S(1)} %add.222), channel_id=1, source_target_pairs={{0,2},{1,3},{2,0},{3,1},{4,6},{5,7},{6,4},{7,5},{8,10},{9,11},{10,... | collective-permute-start | bytes 98312 | tf_op jit(solution)/shard_map/ppermute | solution.py:101

commit v5 on v4

--- a/solution.py
+++ b/solution.py
@@ -25,41 +25,53 @@
     ).astype(jnp.bfloat16)
 
 
-def page_block(
-    carry_state, owners, number, key_block, value_block, queries, slopes, lengths, token_step
-):
+def page_block(carry_state, owners, number, key_block, value_block, queries, slopes, lengths):
     run_max, run_sum, run_out = carry_state
     nblock, page_len, width_all = key_block.shape
     nheads = slopes.shape[0]
     head_size = width_all // nheads
-    requests = queries.shape[0]
+    nsteps, requests = queries.shape[0], queries.shape[1]
     safe_owner = jnp.clip(owners, 0, requests - 1)
-    page_query = jnp.take(queries, safe_owner, axis=0)
+    page_query = jnp.take(queries, safe_owner, axis=1)
     key_heads = key_block.reshape(nblock, page_len, nheads, head_size)
     value_heads = value_block.reshape(nblock, page_len, nheads, head_size)
     scores = jnp.einsum(
-        "bhe,bthe->bth", page_query, key_heads, preferred_element_type=jnp.float32
+        "sbhe,bthe->sbth", page_query, key_heads, preferred_element_type=jnp.float32
     ) * head_size ** (-0.5)
     positions = number[:, None] * page_len + jnp.arange(page_len, dtype=jnp.int32)[None, :]
     own_length = jnp.take(lengths, safe_owner)
-    distance = (own_length[:, None] + token_step - positions).astype(jnp.float32)
-    scores = scores - distance[:, :, None] * slopes[None, None, :]
+    step_ids = jnp.arange(nsteps, dtype=jnp.int32)
+    distance = (
+        own_length[None, :, None] + step_ids[:, None, None] - positions[None]
+    ).astype(jnp.float32)
+    scores = scores - distance[..., None] * slopes
     valid_mask = (owners[:, None] >= 0) & (positions < own_length[:, None])
-    masked = jnp.where(valid_mask[:, :, None], scores, floor_score)
-    page_max = jnp.max(masked, axis=1)
+    masked = jnp.where(valid_mask[None, :, :, None], scores, floor_score)
+    page_max = jnp.max(masked, axis=2)
     member = owners[None, :] == jnp.arange(requests, dtype=jnp.int32)[:, None]
-    block_max = jnp.max(jnp.where(member[:, :, None], page_max[None, :, :], floor_score), axis=1)
+    block_max = jnp.max(
+        jnp.where(member[None, :, :, None], page_max[:, None, :, :], floor_score), axis=2
+    )
     next_max = jnp.maximum(run_max, block_max)
-    owner_max = jnp.take(next_max, safe_owner, axis=0)
-    expon = jnp.where(valid_mask[:, :, None], jnp.exp(masked - owner_max[:, None, :]), 0.0)
-    page_sum = jnp.sum(expon, axis=1)
+    owner_max = jnp.take(next_max, safe_owner, axis=1)
+    expon = jnp.where(
+        valid_mask[None, :, :, None], jnp.exp(masked - owner_max[:, :, None, :]), 0.0
+    )
+    page_sum = jnp.sum(expon, axis=2)
     weights = expon.astype(jnp.bfloat16)
-    page_out = jnp.einsum("bth,bthe->bhe", weights, value_heads, preferred_element_type=jnp.float32)
+    page_out = jnp.einsum(
+        "sbth,bthe->sbhe", weights, value_heads, preferred_element_type=jnp.float32
+    )
     member_float = member.astype(jnp.float32)
     rescale = jnp.exp(run_max - next_max)
-    next_sum = run_sum * rescale + jnp.dot(member_float, page_sum, precision=highest)
-    added = jnp.dot(member_float, page_out.reshape(nblock, nheads * head_size), precision=highest)
-    next_out = run_out * rescale[:, :, None] + added.reshape(requests, nheads, head_size)
+    next_sum = run_sum * rescale + jnp.einsum(
+        "rb,sbh->srh", member_float, page_sum, precision=highest
+    )
+    added = jnp.einsum(
+        "rb,sbx->srx", member_float, page_out.reshape(nsteps, nblock, nheads * head_size),
+        precision=highest,
+    )
+    next_out = run_out * rescale[..., None] + added.reshape(nsteps, requests, nheads, head_size)
     return (next_max, next_sum, next_out)
 
 
@@ -206,43 +218,32 @@
     new_keys = joined[:, head_width : 2 * head_width].reshape(nsteps, requests, nheads, head_size)
     new_values = joined[:, 2 * head_width :].reshape(nsteps, requests, nheads, head_size)
 
-    states = []
-    for token_step in range(nsteps):
-        queries = all_queries[token_step]
-        carry_state = (
-            jnp.full((requests, nheads), floor_score, jnp.float32),
-            jnp.zeros((requests, nheads), jnp.float32),
-            jnp.zeros((requests, nheads, head_size), jnp.float32),
-        )
-
-        def visit(turn_index, state_in):
-            first_page = (turn_index * BLK).astype(jnp.int32)
-            owners = lax.dynamic_slice_in_dim(page_owner, first_page, BLK, 0)
-            number = lax.dynamic_slice_in_dim(page_number, first_page, BLK, 0)
-            key_block = lax.dynamic_slice_in_dim(key_pages, first_page, BLK, 0)
-            value_block = lax.dynamic_slice_in_dim(value_pages, first_page, BLK, 0)
-
-            def compute(state_given):
-                return page_block(
-                    state_given,
-                    owners,
-                    number,
-                    key_block,
-                    value_block,
-                    queries,
-                    alibi_slopes,
-                    lengths,
-                    token_step,
-                )
-
-            def keep_state(state_given):
-                return state_given
-
-            return lax.cond(jnp.any(owners >= 0), compute, keep_state, state_in)
-
-        states.append(lax.fori_loop(0, nblocks, visit, carry_state))
-
-    joined_state = tuple(jnp.concatenate(parts, axis=0) for parts in zip(*states))
+    carry_state = (
+        jnp.full((nsteps, requests, nheads), floor_score, jnp.float32),
+        jnp.zeros((nsteps, requests, nheads), jnp.float32),
+        jnp.zeros((nsteps, requests, nheads, head_size), jnp.float32),
+    )
+
+    def visit(turn_index, state_in):
+        first_page = (turn_index * BLK).astype(jnp.int32)
+        owners = lax.dynamic_slice_in_dim(page_owner, first_page, BLK, 0)
+        number = lax.dynamic_slice_in_dim(page_number, first_page, BLK, 0)
+        key_block = lax.dynamic_slice_in_dim(key_pages, first_page, BLK, 0)
+        value_block = lax.dynamic_slice_in_dim(value_pages, first_page, BLK, 0)
+
+        def compute(state_given):
+            return page_block(
+                state_given, owners, number, key_block, value_block, all_queries, alibi_slopes, lengths
+            )
+
+        def keep_state(state_given):
+            return state_given
+
+        return lax.cond(jnp.any(owners >= 0), compute, keep_state, state_in)
+
+    final_state = lax.fori_loop(0, nblocks, visit, carry_state)
+
+    joined_state = tuple(part.reshape((rows,) + part.shape[2:]) for part in final_state)
     up_cols, (run_max, run_sum, run_out) = lax.optimization_barrier((up_cols, joined_state))
     own_rows = rows // nseq
     stats = jnp.concatenate(

time: 368 us -> 322 us (0.88)
  starting transfers between devices: 74.4 us -> 42.4 us
  other arithmetic: 24.4 us -> 16 us
    all_to_all x1, starting transfers between devices: 40 us -> 7.69 us  [on_device(): packed = lax.all_to_all(packed, 'seq', 0, 0, tiled=True)]
    reduce_or x8 -> x4, other arithmetic: 11.1 us -> 2.92 us  [visit(): return lax.cond(jnp.any(owners >= 0), compute, keep_state, state_in)]
    unnamed x32 -> x28, local copies, waits for them, and re-layouts: 7.65 us -> 8.09 us
    cond x4 -> x8, local copies, waits for them, and re-layouts: 7.08 us -> 7.4 us
  transfers between devices with their start and end apart: 9 -> 9, of which waited for: 8 -> 8; matrix products, arithmetic and copies ran while one was open for 13% -> 11% of each run, Pallas kernels for 0% -> 0%
where the time goes in v5:
time: 322 us; the launch traced here: 320 us
  waiting for transfers between devices  124 us (39%)
  blocking collectives  86.5 us (27%)
  starting transfers between devices  42.4 us (13%)
  local copies, waits for them, and re-layouts  38.9 us (12%)
  other arithmetic  16 us (5%)
  matrix products  8.8 us (3%)
    all_to_all x3, blocking collectives, gather_rows(): return lax.all_to_all(copies, 'seq', 0, 0, tiled=True)  86.5 us
    all_to_all x2, waiting for transfers between devices, gather_rows(): return lax.all_to_all(copies, 'seq', 0, 0, tiled=True)  72.1 us
    all_to_all x1, waiting for transfers between devices, on_device(): packed = lax.all_to_all(packed, 'seq', 0, 0, tiled=True)  22 us
    all_to_all x2, starting transfers between devices, gather_rows(): return lax.all_to_all(copies, 'seq', 0, 0, tiled=True)  18.4 us
    ppermute x4, waiting for transfers between devices, head_sum(): other = lax.ppermute(part, 'head', [(i, i ^ stride) for i in range(nhead)])  15.3 us
    all_to_all x1, waiting for transfers between devices, on_device(): lax.all_to_all(qkv_in, 'seq', 1, 0, tiled=True)  14.4 us
    unnamed x28, local copies, waits for them, and re-layouts  8.09 us
    all_to_all x1, starting transfers between devices, on_device(): packed = lax.all_to_all(packed, 'seq', 0, 0, tiled=True)  7.69 us
  transfers between devices with their start and end apart: 9, of which 8 were waited for; matrix products, arithmetic and copies ran while one was open for 11% of the time, Pallas kernels for 0%

profile of v5, /device:TPU:4, one launch (start us, length us, event | category | flops | bytes accessed | tf_op | source)
XLA Modules:
  0.0 320.0 jit_solution(3965231488055648539)
XLA Ops:
  0.0 0.7 fusion.53
  2.4 0.8 copy.250
  3.4 1.6 broadcast_in_dim.158
  5.0 12.1 %all-to-all-start = ((bf16[64,134,64]{1,2,0:T(8,128)(2,1)}), bf16[64,134,64]{1,2,0:T(8,128)(2,1)S(1)}, u32[]{:S(2)}, u32[]{:S(2)}) async-start(bf16[64,134,64]{1,2,0:T(8,128)(2,1)} %broadcast_in_dim.158), calls=%async_computation | async-start | bytes 4194304 | tf_op jit(solution)/shard_map/all_to_all | solution.py:101
  17.1 1.4 copy.227
  18.5 49.8 %all-to-all-done = bf16[64,134,64]{1,2,0:T(8,128)(2,1)S(1)} async-done(((bf16[64,134,64]{1,2,0:T(8,128)(2,1)}), bf16[64,134,64]{1,2,0:T(8,128)(2,1)S(1)}, u32[]{:S(2)}, u32[]{:S(2)}) %all-to-all-start) | async-done | bytes 1097760 | tf_op jit(solution)/shard_map/all_to_all | solution.py:101
  68.3 2.6 copy.251
  70.9 1.6 convert_reduce_fusion
  72.5 0.9 slice_convert_fusion
  73.4 1.3 reshape.389
  74.6 5.9 %all-to-all-start.1 = ((bf16[64,2,1536]{2,1,0:T(2,128)(2,1)}), bf16[64,2,1536]{2,1,0:T(2,128)(2,1)S(1)}, u32[]{:S(2)}, u32[]{:S(2)}) async-start(bf16[64,2,1536]{2,1,0:T(2,128)(2,1)} %reshape.389), calls=%async_computation.1 | async-start | bytes 786432 | tf_op jit(solution)/shard_map/all_to_all | solution.py:209
  80.6 14.4 %all-to-all-done.1 = bf16[64,2,1536]{2,1,0:T(2,128)(2,1)S(1)} async-done(((bf16[64,2,1536]{2,1,0:T(2,128)(2,1)}), bf16[64,2,1536]{2,1,0:T(2,128)(2,1)S(1)}, u32[]{:S(2)}, u32[]{:S(2)}) %all-to-all-start.1) | async-done | bytes 393248 | tf_op jit(solution)/shard_map/all_to_all | solution.py:209
  97.3 1.0 broadcast_in_dim.159
  98.3 6.3 %all-to-all-start.2 = ((bf16[64,128,48]{1,2,0:T(8,128)(2,1)}), bf16[64,128,48]{1,2,0:T(8,128)(2,1)S(1)}, u32[]{:S(2)}, u32[]{:S(2)}) async-start(bf16[64,128,48]{1,2,0:T(8,128)(2,1)} %broadcast_in_dim.159), calls=%async_computation.2 | async-start | bytes 1572864 | tf_op jit(solution)/shard_map/all_to_all | solution.py:101
  105.1 22.4 %all-to-all-done.2 = bf16[64,128,48]{1,2,0:T(8,128)(2,1)S(1)} async-done(((bf16[64,128,48]{1,2,0:T(8,128)(2,1)}), bf16[64,128,48]{1,2,0:T(8,128)(2,1)S(1)}, u32[]{:S(2)}, u32[]{:S(2)}) %all-to-all-start.2) | async-done | bytes 786464 | tf_op jit(solution)/shard_map/all_to_all | solution.py:101
  127.5 1.5 reshape.391
  129.0 6.9 %all-to-all-start.3 = ((bf16[64,2,2048]{2,1,0:T(2,128)(2,1)}), bf16[64,2,2048]{2,1,0:T(2,128)(2,1)}, u32[]{:S(2)}, u32[]{:S(2)}) async-start(bf16[64,2,2048]{2,1,0:T(2,128)(2,1)} %reshape.391), calls=%async_computation.3 | async-start | bytes 1048576 | tf_op jit(solution)/shard_map/all_to_all | solution.py:216
  136.4 35.3 %while.17 = (s32[]{:T(128)}, f32[2,64,8]{1,2,0:T(8,128)S(1)}, f32[2,64,8]{1,2,0:T(8,128)S(1)}, f32[2,64,8,128]{3,2,1,0:T(8,128)S(1)}, s32[32]{0:T(128)S(1)}, /*i...) while((s32[]{:T(128)}, f32[2,64,8]{1,2,0:T(8,128)S(1)}, ...), condition=%wide.region_9.10_spmd, body=%wide.region_2.9_spmd.sunk | while | flops 17270284 | bytes 10174693 | solution.py:244
  136.4 0.7 compare_reduce_fusion.2
  137.7 7.5 %conditional.2 = ((f32[2,64,8]{1,2,0:T(8,128)S(1)}, f32[2,64,8]{1,2,0:T(8,128)S(1)}, f32[2,64,8,128]{3,2,1,0:T(8,128)S(1)})) conditional(s32[]{:T(128)} %convert_element_type.210, (f32[2,64,8]{1,2,0:T(8,128)S(1)}, f32[2,64,8]{1,2,0:T(8,128)S(1)}, f32[2,64,8,128]{3,2,1,0:T(8,128)S(1)}) %tuple.72, (s32[8]{0:T(128)S(1)}, s32[32]{0:T(128)S(1)}, ...), branch_computations={%region_4.0_spmd, %region_5.8_spmd} | conditional | flops 17270264 | bytes 10174320 | solution.py:242
  139.5 1.8 dynamic-slice_bitcast_fusion
  141.2 0.7 fusion.56
  145.2 0.7 compare_reduce_fusion.2
  146.6 7.5 %conditional.2 = ((f32[2,64,8]{1,2,0:T(8,128)S(1)}, f32[2,64,8]{1,2,0:T(8,128)S(1)}, f32[2,64,8,128]{3,2,1,0:T(8,128)S(1)})) conditional(s32[]{:T(128)} %convert_element_type.210, (f32[2,64,8]{1,2,0:T(8,128)S(1)}, f32[2,64,8]{1,2,0:T(8,128)S(1)}, f32[2,64,8,128]{3,2,1,0:T(8,128)S(1)}) %tuple.72, (s32[8]{0:T(128)S(1)}, s32[32]{0:T(128)S(1)}, ...), branch_computations={%region_4.0_spmd, %region_5.8_spmd} | conditional | flops 17270264 | bytes 10174320 | solution.py:242
  148.3 1.8 dynamic-slice_bitcast_fusion
  150.0 0.7 fusion.56
  154.0 0.7 compare_reduce_fusion.2
  155.4 7.5 %conditional.2 = ((f32[2,64,8]{1,2,0:T(8,128)S(1)}, f32[2,64,8]{1,2,0:T(8,128)S(1)}, f32[2,64,8,128]{3,2,1,0:T(8,128)S(1)})) conditional(s32[]{:T(128)} %convert_element_type.210, (f32[2,64,8]{1,2,0:T(8,128)S(1)}, f32[2,64,8]{1,2,0:T(8,128)S(1)}, f32[2,64,8,128]{3,2,1,0:T(8,128)S(1)}) %tuple.72, (s32[8]{0:T(128)S(1)}, s32[32]{0:T(128)S(1)}, ...), branch_computations={%region_4.0_spmd, %region_5.8_spmd} | conditional | flops 17270264 | bytes 10174320 | solution.py:242
  157.1 1.8 dynamic-slice_bitcast_fusion
  158.9 0.7 fusion.56
  162.8 0.7 compare_reduce_fusion.2
  164.2 7.5 %conditional.2 = ((f32[2,64,8]{1,2,0:T(8,128)S(1)}, f32[2,64,8]{1,2,0:T(8,128)S(1)}, f32[2,64,8,128]{3,2,1,0:T(8,128)S(1)})) conditional(s32[]{:T(128)} %convert_element_type.210, (f32[2,64,8]{1,2,0:T(8,128)S(1)}, f32[2,64,8]{1,2,0:T(8,128)S(1)}, f32[2,64,8,128]{3,2,1,0:T(8,128)S(1)}) %tuple.72, (s32[8]{0:T(128)S(1)}, s32[32]{0:T(128)S(1)}, ...), branch_computations={%region_4.0_spmd, %region_5.8_spmd} | conditional | flops 17270264 | bytes 10174320 | solution.py:242
  165.9 1.8 dynamic-slice_bitcast_fusion
  167.7 0.7 fusion.56
  171.8 2.3 reshape.392
  174.9 1.6 reshape.349
  177.7 0.9 pad_maximum_fusion
  178.7 7.7 %all-to-all-start.4 = ((f32[64,3,8,128]{3,2,1,0:T(8,128)}), f32[64,3,8,128]{3,2,1,0:T(8,128)S(1)}, u32[]{:S(2)}, u32[]{:S(2)}) async-start(f32[64,3,8,128]{3,2,1,0:T(8,128)} %pad_maximum_fusion), calls=%async_computation.4 | async-start | bytes 1572864 | tf_op jit(solution)/shard_map/all_to_all | solution.py:260
  187.3 22.0 %all-to-all-done.4 = f32[64,3,8,128]{3,2,1,0:T(8,128)S(1)} async-done(((f32[64,3,8,128]{3,2,1,0:T(8,128)}), f32[64,3,8,128]{3,2,1,0:T(8,128)S(1)}, u32[]{:S(2)}, u32[]{:S(2)}) %all-to-all-start.4) | async-done | bytes 786464 | tf_op jit(solution)/shard_map/all_to_all | solution.py:260
  211.0 18.1 %all_to_all.60 = bf16[64,2,1024]{2,1,0:T(2,128)(2,1)S(1)} all-to-all(bf16[64,2,1024]{2,1,0:T(2,128)(2,1)S(1)} %broadcast_in_dim.166), channel_id=1, replica_groups=mesh['seq'=64,'head'=4] {'seq'}, dimensions={0} | all-to-all | bytes 524288 | tf_op jit(solution)/shard_map/all_to_all | solution.py:101
  229.4 1.3 collective-permute-start
  230.6 2.7 collective-permute-done
  233.9 4.9 %collective-permute-done.1 = f32[128,64]{0,1:T(8,128)S(1)} collective-permute-done((f32[128,64]{0,1:T(8,128)S(1)}, f32[128,64]{0,1:T(8,128)S(1)}, u32[]{:S(2)}, u32[]{:S(2)}) %collective-permute-start.1) | collective-permute-done | bytes 32800 | tf_op jit(solution)/shard_map/ppermute | solution.py:113
  239.0 34.0 %all_to_all.61 = bf16[64,128,64]{1,2,0:T(8,128)(2,1)S(1)} all-to-all(bf16[64,128,64]{1,2,0:T(8,128)(2,1)S(1)} %broadcast_in_dim.167), channel_id=1, replica_groups=mesh['seq'=64,'head'=4] {'seq'}, dimensions={0} | all-to-all | bytes 2097152 | tf_op jit(solution)/shard_map/all_to_all | solution.py:101
  275.0 34.5 %all_to_all.62 = bf16[64,128,64]{1,2,0:T(8,128)(2,1)S(1)} all-to-all(bf16[64,128,64]{1,2,0:T(8,128)(2,1)S(1)} %broadcast_in_dim.168), channel_id=1, replica_groups=mesh['seq'=64,'head'=4] {'seq'}, dimensions={0} | all-to-all | bytes 2097152 | tf_op jit(solution)/shard_map/all_to_all | solution.py:101
  309.8 1.3 collective-permute-start.2
  311.1 2.7 collective-permute-done.2
  314.3 4.9 %collective-permute-done.3 = f32[128,64]{0,1:T(8,128)S(1)} collective-permute-done((f32[128,64]{0,1:T(8,128)S(1)}, f32[128,64]{0,1:T(8,128)S(1)}, u32[]{:S(2)}, u32[]{:S(2)}) %collective-permute-start.3) | collective-permute-done | bytes 32800 | tf_op jit(solution)/shard_map/ppermute | solution.py:113
  (200 shorter events, 33.6 us)
Async XLA Ops:
  0.0 309.5 %copy-start = (bf16[64,4096]{1,0:T(8,128)(2,1)S(1)}, bf16[64,4096]{1,0:T(8,128)(2,1)}, u32[]{:S(2)}) copy-start(bf16[64,4096]{1,0:T(8,128)(2,1)} %param.29) | copy-start | bytes 1572868
  5.0 63.3 %all-to-all-start = ((bf16[64,134,64]{1,2,0:T(8,128)(2,1)}), bf16[64,134,64]{1,2,0:T(8,128)(2,1)S(1)}, u32[]{:S(2)}, u32[]{:S(2)}) async-start(bf16[64,134,64]{1,2,0:T(8,128)(2,1)} %broadcast_in_dim.158), calls=%async_computation | async-start | bytes 4194304 | tf_op jit(solution)/shard_map/all_to_all | solution.py:101
  74.6 20.4 %all-to-all-start.1 = ((bf16[64,2,1536]{2,1,0:T(2,128)(2,1)}), bf16[64,2,1536]{2,1,0:T(2,128)(2,1)S(1)}, u32[]{:S(2)}, u32[]{:S(2)}) async-start(bf16[64,2,1536]{2,1,0:T(2,128)(2,1)} %reshape.389), calls=%async_computation.1 | async-start | bytes 786432 | tf_op jit(solution)/shard_map/all_to_all | solution.py:209
  95.5 1.3 copy-start.2
  96.8 7.9 %copy-start.3 = (bf16[64,4096]{1,0:T(8,128)(2,1)S(1)}, bf16[64,4096]{1,0:T(8,128)(2,1)}, u32[]{:S(2)}) copy-start(bf16[64,4096]{1,0:T(8,128)(2,1)} %param.28) | copy-start | bytes 1572868
  98.3 29.2 %all-to-all-start.2 = ((bf16[64,128,48]{1,2,0:T(8,128)(2,1)}), bf16[64,128,48]{1,2,0:T(8,128)(2,1)S(1)}, u32[]{:S(2)}, u32[]{:S(2)}) async-start(bf16[64,128,48]{1,2,0:T(8,128)(2,1)} %broadcast_in_dim.159), calls=%async_computation.2 | async-start | bytes 1572864 | tf_op jit(solution)/shard_map/all_to_all | solution.py:101
  129.0 7.3 %copy-start.1 = (s32[64]{0:T(128)S(1)}, s32[64]{0:T(128)}, u32[]{:S(2)}) copy-start(s32[64]{0:T(128)} %param.18) | copy-start | bytes 772
  129.0 7.3 %copy-start.6 = (s32[32]{0:T(128)S(1)}, s32[32]{0:T(128)}, u32[]{:S(2)}) copy-start(s32[32]{0:T(128)} %param.19) | copy-start | bytes 388
  129.0 7.3 %copy-start.7 = (s32[32]{0:T(128)S(1)}, s32[32]{0:T(128)}, u32[]{:S(2)}) copy-start(s32[32]{0:T(128)} %param.20) | copy-start | bytes 388
  129.0 7.3 %copy-start.8 = (f32[8]{0:T(128)S(1)}, f32[8]{0:T(128)}, u32[]{:S(2)}) copy-start(f32[8]{0:T(128)} %param.23) | copy-start | bytes 100
  129.0 42.8 %all-to-all-start.3 = ((bf16[64,2,2048]{2,1,0:T(2,128)(2,1)}), bf16[64,2,2048]{2,1,0:T(2,128)(2,1)}, u32[]{:S(2)}, u32[]{:S(2)}) async-start(bf16[64,2,2048]{2,1,0:T(2,128)(2,1)} %reshape.391), calls=%async_computation.3 | async-start | bytes 1048576 | tf_op jit(solution)/shard_map/all_to_all | solution.py:216
  178.7 30.6 %all-to-all-start.4 = ((f32[64,3,8,128]{3,2,1,0:T(8,128)}), f32[64,3,8,128]{3,2,1,0:T(8,128)S(1)}, u32[]{:S(2)}, u32[]{:S(2)}) async-start(f32[64,3,8,128]{3,2,1,0:T(8,128)} %pad_maximum_fusion), calls=%async_computation.4 | async-start | bytes 1572864 | tf_op jit(solution)/shard_map/all_to_all | solution.py:260
  186.9 42.2 %copy-start.5 = (bf16[64,1024]{1,0:T(8,128)(2,1)S(1)}, bf16[64,1024]{1,0:T(8,128)(2,1)}, u32[]{:S(2)}) copy-start(bf16[64,1024]{1,0:T(8,128)(2,1)} %param.27) | copy-start | bytes 393220
  229.4 4.0 %collective-permute-start = (f32[128,64]{0,1:T(8,128)S(1)}, f32[128,64]{0,1:T(8,128)S(1)}, u32[]{:S(2)}, u32[]{:S(2)}) collective-permute-start(f32[128,64]{0,1:T(8,128)S(1)} %fusion.59), channel_id=1, source_target_pairs={{0,1},{1,0},{2,3},{3,2},{4,5},{5,4},{6,7},{7,6},{8,9},{9,8},{10,11... | collective-permute-start | bytes 98312 | tf_op jit(solution)/shard_map/ppermute | solution.py:113
  233.4 5.4 %collective-permute-start.1 = (f32[128,64]{0,1:T(8,128)S(1)}, f32[128,64]{0,1:T(8,128)S(1)}, u32[]{:S(2)}, u32[]{:S(2)}) collective-permute-start(f32[128,64]{0,1:T(8,128)S(1)} %add.176), channel_id=1, source_target_pairs={{0,2},{1,3},{2,0},{3,1},{4,6},{5,7},{6,4},{7,5},{8,10},{9,11},{10,... | collective-permute-start | bytes 98312 | tf_op jit(solution)/shard_map/ppermute | solution.py:113
  273.0 1.3 copy-start.4
  309.8 4.0 %collective-permute-start.2 = (f32[128,64]{0,1:T(8,128)S(1)}, f32[128,64]{0,1:T(8,128)S(1)}, u32[]{:S(2)}, u32[]{:S(2)}) collective-permute-start(f32[128,64]{0,1:T(8,128)S(1)} %fusion.60), channel_id=1, source_target_pairs={{0,1},{1,0},{2,3},{3,2},{4,5},{5,4},{6,7},{7,6},{8,9},{9,8},{10,11... | collective-permute-start | bytes 98312 | tf_op jit(solution)/shard_map/ppermute | solution.py:113
  313.8 5.4 %collective-permute-start.3 = (f32[128,64]{0,1:T(8,128)S(1)}, f32[128,64]{0,1:T(8,128)S(1)}, u32[]{:S(2)}, u32[]{:S(2)}) collective-permute-start(f32[128,64]{0,1:T(8,128)S(1)} %add.180), channel_id=1, source_target_pairs={{0,2},{1,3},{2,0},{3,1},{4,6},{5,7},{6,4},{7,5},{8,10},{9,11},{10,... | collective-permute-start | bytes 98312 | tf_op jit(solution)/shard_map/ppermute | solution.py:113

commit v6 on v5

--- a/solution.py
+++ b/solution.py
@@ -187,7 +187,6 @@
     nheads = alibi_slopes.shape[0]
     head_width = key_pages.shape[2]
     head_size = head_width // nheads
-    nblocks = key_pages.shape[0] // BLK
     qkv_width = w_qkv.shape[1] * w_qkv.shape[2]
     rows = nsteps * requests
 
@@ -224,24 +223,9 @@
         jnp.zeros((nsteps, requests, nheads, head_size), jnp.float32),
     )
 
-    def visit(turn_index, state_in):
-        first_page = (turn_index * BLK).astype(jnp.int32)
-        owners = lax.dynamic_slice_in_dim(page_owner, first_page, BLK, 0)
-        number = lax.dynamic_slice_in_dim(page_number, first_page, BLK, 0)
-        key_block = lax.dynamic_slice_in_dim(key_pages, first_page, BLK, 0)
-        value_block = lax.dynamic_slice_in_dim(value_pages, first_page, BLK, 0)
-
-        def compute(state_given):
-            return page_block(
-                state_given, owners, number, key_block, value_block, all_queries, alibi_slopes, lengths
-            )
-
-        def keep_state(state_given):
-            return state_given
-
-        return lax.cond(jnp.any(owners >= 0), compute, keep_state, state_in)
-
-    final_state = lax.fori_loop(0, nblocks, visit, carry_state)
+    final_state = page_block(
+        carry_state, page_owner, page_number, key_pages, value_pages, all_queries, alibi_slopes, lengths
+    )
 
     joined_state = tuple(part.reshape((rows,) + part.shape[2:]) for part in final_state)
     up_cols, (run_max, run_sum, run_out) = lax.optimization_barrier((up_cols, joined_state))

time: 322 us -> 309 us (0.960)
  local copies, waits for them, and re-layouts: 38.9 us -> 23.2 us
  waiting for transfers between devices: 124 us -> 138 us
  other arithmetic: 16 us -> 9.71 us
    all_to_all x1, waiting for transfers between devices: 0.01 us -> 15 us  [on_device(): lax.all_to_all(up_in, 'seq', 1, 0, tiled=True)]
    cond x8 -> x0, local copies, waits for them, and re-layouts: 7.4 us -> none
    unnamed x28 -> x29, local copies, waits for them, and re-layouts: 8.09 us -> 6.58 us
  transfers between devices with their start and end apart: 9 -> 9, of which waited for: 8 -> 9; matrix products, arithmetic and copies ran while one was open for 11% -> 2% of each run, Pallas kernels for 0% -> 0%
where the time goes in v6:
time: 309 us; the launch traced here: 308 us
  waiting for transfers between devices  138 us (45%)
  blocking collectives  86.5 us (28%)
  starting transfers between devices  40.7 us (13%)
  local copies, waits for them, and re-layouts  23.2 us (8%)
  matrix products  10.1 us (3%)
  other arithmetic  9.71 us (3%)
    all_to_all x3, blocking collectives, gather_rows(): return lax.all_to_all(copies, 'seq', 0, 0, tiled=True)  86.5 us
    all_to_all x2, waiting for transfers between devices, gather_rows(): return lax.all_to_all(copies, 'seq', 0, 0, tiled=True)  70.9 us
    all_to_all x1, waiting for transfers between devices, on_device(): packed = lax.all_to_all(packed, 'seq', 0, 0, tiled=True)  22 us
    all_to_all x2, starting transfers between devices, gather_rows(): return lax.all_to_all(copies, 'seq', 0, 0, tiled=True)  18.4 us
    ppermute x4, waiting for transfers between devices, head_sum(): other = lax.ppermute(part, 'head', [(i, i ^ stride) for i in range(nhead)])  15.3 us
    all_to_all x1, waiting for transfers between devices, on_device(): lax.all_to_all(up_in, 'seq', 1, 0, tiled=True)  15 us
    all_to_all x1, waiting for transfers between devices, on_device(): lax.all_to_all(qkv_in, 'seq', 1, 0, tiled=True)  14.4 us
    unnamed x29, local copies, waits for them, and re-layouts  6.58 us
  transfers between devices with their start and end apart: 9, of which 9 were waited for; matrix products, arithmetic and copies ran while one was open for 2% of the time, Pallas kernels for 0%

profile of v6, /device:TPU:4, one launch (start us, length us, event | category | flops | bytes accessed | tf_op | source)
XLA Modules:
  0.0 308.3 jit_solution(195823948427129568)
XLA Ops:
  0.0 0.7 fusion.67
  0.7 0.7 fusion.63
  1.4 0.7 subtract_convert_fusion.1
  2.4 0.8 copy.224
  3.4 1.6 broadcast_in_dim.90
  5.0 12.1 %all-to-all-start = ((bf16[64,134,64]{1,2,0:T(8,128)(2,1)}), bf16[64,134,64]{1,2,0:T(8,128)(2,1)S(1)}, u32[]{:S(2)}, u32[]{:S(2)}) async-start(bf16[64,134,64]{1,2,0:T(8,128)(2,1)} %broadcast_in_dim.90), calls=%async_computation | async-start | bytes 4194304 | tf_op jit(solution)/shard_map/all_to_all | solution.py:101
  17.1 1.4 copy.192
  18.5 49.8 %all-to-all-done = bf16[64,134,64]{1,2,0:T(8,128)(2,1)S(1)} async-done(((bf16[64,134,64]{1,2,0:T(8,128)(2,1)}), bf16[64,134,64]{1,2,0:T(8,128)(2,1)S(1)}, u32[]{:S(2)}, u32[]{:S(2)}) %all-to-all-start) | async-done | bytes 1097760 | tf_op jit(solution)/shard_map/all_to_all | solution.py:101
  68.2 2.6 copy.225
  70.9 1.6 convert_reduce_fusion
  72.4 0.9 slice_convert_fusion
  73.3 1.3 reshape.382
  74.6 5.9 %all-to-all-start.1 = ((bf16[64,2,1536]{2,1,0:T(2,128)(2,1)}), bf16[64,2,1536]{2,1,0:T(2,128)(2,1)S(1)}, u32[]{:S(2)}, u32[]{:S(2)}) async-start(bf16[64,2,1536]{2,1,0:T(2,128)(2,1)} %reshape.382), calls=%async_computation.1 | async-start | bytes 786432 | tf_op jit(solution)/shard_map/all_to_all | solution.py:208
  80.5 14.4 %all-to-all-done.1 = bf16[64,2,1536]{2,1,0:T(2,128)(2,1)S(1)} async-done(((bf16[64,2,1536]{2,1,0:T(2,128)(2,1)}), bf16[64,2,1536]{2,1,0:T(2,128)(2,1)S(1)}, u32[]{:S(2)}, u32[]{:S(2)}) %all-to-all-start.1) | async-done | bytes 393248 | tf_op jit(solution)/shard_map/all_to_all | solution.py:208
  95.7 0.6 reshape.338
  96.7 0.5 convolution_convert_fusion
  97.3 1.0 broadcast_in_dim.91
  98.3 6.3 %all-to-all-start.2 = ((bf16[64,128,48]{1,2,0:T(8,128)(2,1)}), bf16[64,128,48]{1,2,0:T(8,128)(2,1)S(1)}, u32[]{:S(2)}, u32[]{:S(2)}) async-start(bf16[64,128,48]{1,2,0:T(8,128)(2,1)} %broadcast_in_dim.91), calls=%async_computation.2 | async-start | bytes 1572864 | tf_op jit(solution)/shard_map/all_to_all | solution.py:101
  105.2 0.7 gather_fusion
  106.4 21.1 %all-to-all-done.2 = bf16[64,128,48]{1,2,0:T(8,128)(2,1)S(1)} async-done(((bf16[64,128,48]{1,2,0:T(8,128)(2,1)}), bf16[64,128,48]{1,2,0:T(8,128)(2,1)S(1)}, u32[]{:S(2)}, u32[]{:S(2)}) %all-to-all-start.2) | async-done | bytes 786464 | tf_op jit(solution)/shard_map/all_to_all | solution.py:101
  127.7 0.6 gather_fusion.1
  128.5 4.5 %fusion.72 = (f32[2,32,8]{0,2,1:T(8,128)S(1)}, f32[2,32,64,8]{2,0,3,1:T(2,128)S(1)}) fusion(f32[8]{0:T(128)S(1)} %copy-done.8, f32[2,32,64]{2,0,1:T(2,128)S(1)} %subtract_convert_fusion, bf16[2,32,8,128]{3,2,0,1:T(8,128)(2,1)S(1)} %select_bitcast_fusion, pred[32,64]{1,0:T(8,128)(4,1)S(1)} %compare_and_fusion, bf16[32,64,1024]{2,1,0:T(8,128)(2,1)} %param.17), kind=kOutput, calls=%fused_computation.132 | convolution fusion | flops 8551936 | bytes 4476960 | tf_op jit(solution)/shard_map/sbhe,bthe->sbth/dot_general | solution.py:38
  133.6 0.6 gather_fusion.2
  134.6 3.4 %fusion.19 = f32[2,32,8,128]{3,0,2,1:T(2,128)S(1)} fusion(f32[2,32,64,8]{2,0,3,1:T(2,128)S(1)} %get-tuple-element.52, pred[32,64]{1,0:T(8,128)(4,1)S(1)} %compare_and_fusion, f32[2,32,8]{0,2,1:T(8,128)S(1)} %copy.205, bf16[32,64,1024]{2,1,0:T(8,128)(2,1)} %param.18), kind=kOutput, calls=%fused_computation.23 | convolution fusion | flops 8486912 | bytes 4591616 | tf_op jit(solution)/shard_map/sbth,bthe->sbhe/dot_general | solution.py:62
  138.1 1.5 reshape.384
  139.6 6.3 %all-to-all-start.3 = ((bf16[64,2,2048]{2,1,0:T(2,128)(2,1)}), bf16[64,2,2048]{2,1,0:T(2,128)(2,1)S(1)}, u32[]{:S(2)}, u32[]{:S(2)}) async-start(bf16[64,2,2048]{2,1,0:T(2,128)(2,1)} %reshape.384), calls=%async_computation.3 | async-start | bytes 1048576 | tf_op jit(solution)/shard_map/all_to_all | solution.py:215
  146.7 0.7 fusion.55
  148.0 15.0 %all-to-all-done.3 = bf16[64,2,2048]{2,1,0:T(2,128)(2,1)S(1)} async-done(((bf16[64,2,2048]{2,1,0:T(2,128)(2,1)}), bf16[64,2,2048]{2,1,0:T(2,128)(2,1)S(1)}, u32[]{:S(2)}, u32[]{:S(2)}) %all-to-all-start.3) | async-done | bytes 524320 | tf_op jit(solution)/shard_map/all_to_all | solution.py:215
  163.0 0.7 reshape.385
  163.7 0.7 copy.198
  164.4 1.6 reshape.340
  167.3 0.9 pad_maximum_fusion
  168.2 6.5 %all-to-all-start.4 = ((f32[64,3,8,128]{3,2,1,0:T(8,128)}), f32[64,3,8,128]{3,2,1,0:T(8,128)S(1)}, u32[]{:S(2)}, u32[]{:S(2)}) async-start(f32[64,3,8,128]{3,2,1,0:T(8,128)} %pad_maximum_fusion), calls=%async_computation.4 | async-start | bytes 1572864 | tf_op jit(solution)/shard_map/all_to_all | solution.py:244
  175.6 22.0 %all-to-all-done.4 = f32[64,3,8,128]{3,2,1,0:T(8,128)S(1)} async-done(((f32[64,3,8,128]{3,2,1,0:T(8,128)}), f32[64,3,8,128]{3,2,1,0:T(8,128)S(1)}, u32[]{:S(2)}, u32[]{:S(2)}) %all-to-all-start.4) | async-done | bytes 786464 | tf_op jit(solution)/shard_map/all_to_all | solution.py:244
  199.3 18.1 %all_to_all.60 = bf16[64,2,1024]{2,1,0:T(2,128)(2,1)S(1)} all-to-all(bf16[64,2,1024]{2,1,0:T(2,128)(2,1)S(1)} %broadcast_in_dim.165), channel_id=1, replica_groups=mesh['seq'=64,'head'=4] {'seq'}, dimensions={0} | all-to-all | bytes 524288 | tf_op jit(solution)/shard_map/all_to_all | solution.py:101
  217.7 1.3 collective-permute-start
  219.0 2.7 collective-permute-done
  221.7 0.5 collective-permute-start.1
  222.2 4.9 %collective-permute-done.1 = f32[128,64]{0,1:T(8,128)S(1)} collective-permute-done((f32[128,64]{0,1:T(8,128)S(1)}, f32[128,64]{0,1:T(8,128)S(1)}, u32[]{:S(2)}, u32[]{:S(2)}) %collective-permute-start.1) | collective-permute-done | bytes 32800 | tf_op jit(solution)/shard_map/ppermute | solution.py:113
  227.4 34.0 %all_to_all.61 = bf16[64,128,64]{1,2,0:T(8,128)(2,1)S(1)} all-to-all(bf16[64,128,64]{1,2,0:T(8,128)(2,1)S(1)} %broadcast_in_dim.166), channel_id=1, replica_groups=mesh['seq'=64,'head'=4] {'seq'}, dimensions={0} | all-to-all | bytes 2097152 | tf_op jit(solution)/shard_map/all_to_all | solution.py:101
  261.4 0.6 convert_reduce_fusion.1
  261.9 0.7 fusion.12
  263.3 34.5 %all_to_all.62 = bf16[64,128,64]{1,2,0:T(8,128)(2,1)S(1)} all-to-all(bf16[64,128,64]{1,2,0:T(8,128)(2,1)S(1)} %broadcast_in_dim.167), channel_id=1, replica_groups=mesh['seq'=64,'head'=4] {'seq'}, dimensions={0} | all-to-all | bytes 2097152 | tf_op jit(solution)/shard_map/all_to_all | solution.py:101
  298.2 1.3 collective-permute-start.2
  299.4 2.7 collective-permute-done.2
  302.2 0.5 collective-permute-start.3
  302.7 4.9 %collective-permute-done.3 = f32[128,64]{0,1:T(8,128)S(1)} collective-permute-done((f32[128,64]{0,1:T(8,128)S(1)}, f32[128,64]{0,1:T(8,128)S(1)}, u32[]{:S(2)}, u32[]{:S(2)}) %collective-permute-start.3) | collective-permute-done | bytes 32800 | tf_op jit(solution)/shard_map/ppermute | solution.py:113
  307.6 0.7 copy.227
  (98 shorter events, 10.6 us)
Async XLA Ops:
  0.0 297.8 %copy-start = (bf16[64,4096]{1,0:T(8,128)(2,1)S(1)}, bf16[64,4096]{1,0:T(8,128)(2,1)}, u32[]{:S(2)}) copy-start(bf16[64,4096]{1,0:T(8,128)(2,1)} %param.25) | copy-start | bytes 1572868
  5.0 63.3 %all-to-all-start = ((bf16[64,134,64]{1,2,0:T(8,128)(2,1)}), bf16[64,134,64]{1,2,0:T(8,128)(2,1)S(1)}, u32[]{:S(2)}, u32[]{:S(2)}) async-start(bf16[64,134,64]{1,2,0:T(8,128)(2,1)} %broadcast_in_dim.90), calls=%async_computation | async-start | bytes 4194304 | tf_op jit(solution)/shard_map/all_to_all | solution.py:101
  74.6 20.4 %all-to-all-start.1 = ((bf16[64,2,1536]{2,1,0:T(2,128)(2,1)}), bf16[64,2,1536]{2,1,0:T(2,128)(2,1)S(1)}, u32[]{:S(2)}, u32[]{:S(2)}) async-start(bf16[64,2,1536]{2,1,0:T(2,128)(2,1)} %reshape.382), calls=%async_computation.1 | async-start | bytes 786432 | tf_op jit(solution)/shard_map/all_to_all | solution.py:208
  95.5 1.3 copy-start.2
  96.7 7.9 %copy-start.6 = (s32[32]{0:T(128)S(1)}, s32[32]{0:T(128)}, u32[]{:S(2)}) copy-start(s32[32]{0:T(128)} %param.15) | copy-start | bytes 388
  97.3 7.4 %copy-start.3 = (bf16[64,4096]{1,0:T(8,128)(2,1)S(1)}, bf16[64,4096]{1,0:T(8,128)(2,1)}, u32[]{:S(2)}) copy-start(bf16[64,4096]{1,0:T(8,128)(2,1)} %param.24) | copy-start | bytes 1572868
  97.3 7.9 %copy-start.1 = (s32[64]{0:T(128)S(1)}, s32[64]{0:T(128)}, u32[]{:S(2)}) copy-start(s32[64]{0:T(128)} %param.14) | copy-start | bytes 772
  97.3 8.6 %copy-start.7 = (s32[32]{0:T(128)S(1)}, s32[32]{0:T(128)}, u32[]{:S(2)}) copy-start(s32[32]{0:T(128)} %param.16) | copy-start | bytes 388
  98.3 29.2 %all-to-all-start.2 = ((bf16[64,128,48]{1,2,0:T(8,128)(2,1)}), bf16[64,128,48]{1,2,0:T(8,128)(2,1)S(1)}, u32[]{:S(2)}, u32[]{:S(2)}) async-start(bf16[64,128,48]{1,2,0:T(8,128)(2,1)} %broadcast_in_dim.91), calls=%async_computation.2 | async-start | bytes 1572864 | tf_op jit(solution)/shard_map/all_to_all | solution.py:101
  105.1 23.3 %copy-start.8 = (f32[8]{0:T(128)S(1)}, f32[8]{0:T(128)}, u32[]{:S(2)}) copy-start(f32[8]{0:T(128)} %param.19) | copy-start | bytes 100
  139.6 23.3 %all-to-all-start.3 = ((bf16[64,2,2048]{2,1,0:T(2,128)(2,1)}), bf16[64,2,2048]{2,1,0:T(2,128)(2,1)S(1)}, u32[]{:S(2)}, u32[]{:S(2)}) async-start(bf16[64,2,2048]{2,1,0:T(2,128)(2,1)} %reshape.384), calls=%async_computation.3 | async-start | bytes 1048576 | tf_op jit(solution)/shard_map/all_to_all | solution.py:215
  168.2 29.4 %all-to-all-start.4 = ((f32[64,3,8,128]{3,2,1,0:T(8,128)}), f32[64,3,8,128]{3,2,1,0:T(8,128)S(1)}, u32[]{:S(2)}, u32[]{:S(2)}) async-start(f32[64,3,8,128]{3,2,1,0:T(8,128)} %pad_maximum_fusion), calls=%async_computation.4 | async-start | bytes 1572864 | tf_op jit(solution)/shard_map/all_to_all | solution.py:244
  175.3 42.2 %copy-start.5 = (bf16[64,1024]{1,0:T(8,128)(2,1)S(1)}, bf16[64,1024]{1,0:T(8,128)(2,1)}, u32[]{:S(2)}) copy-start(bf16[64,1024]{1,0:T(8,128)(2,1)} %param.23) | copy-start | bytes 393220
  217.7 4.0 %collective-permute-start = (f32[128,64]{0,1:T(8,128)S(1)}, f32[128,64]{0,1:T(8,128)S(1)}, u32[]{:S(2)}, u32[]{:S(2)}) collective-permute-start(f32[128,64]{0,1:T(8,128)S(1)} %fusion.73), channel_id=1, source_target_pairs={{0,1},{1,0},{2,3},{3,2},{4,5},{5,4},{6,7},{7,6},{8,9},{9,8},{10,11... | collective-permute-start | bytes 98312 | tf_op jit(solution)/shard_map/ppermute | solution.py:113
  221.7 5.4 %collective-permute-start.1 = (f32[128,64]{0,1:T(8,128)S(1)}, f32[128,64]{0,1:T(8,128)S(1)}, u32[]{:S(2)}, u32[]{:S(2)}) collective-permute-start(f32[128,64]{0,1:T(8,128)S(1)} %add.154), channel_id=1, source_target_pairs={{0,2},{1,3},{2,0},{3,1},{4,6},{5,7},{6,4},{7,5},{8,10},{9,11},{10,... | collective-permute-start | bytes 98312 | tf_op jit(solution)/shard_map/ppermute | solution.py:113
  261.4 1.3 copy-start.4
  298.2 4.0 %collective-permute-start.2 = (f32[128,64]{0,1:T(8,128)S(1)}, f32[128,64]{0,1:T(8,128)S(1)}, u32[]{:S(2)}, u32[]{:S(2)}) collective-permute-start(f32[128,64]{0,1:T(8,128)S(1)} %fusion.74), channel_id=1, source_target_pairs={{0,1},{1,0},{2,3},{3,2},{4,5},{5,4},{6,7},{7,6},{8,9},{9,8},{10,11... | collective-permute-start | bytes 98312 | tf_op jit(solution)/shard_map/ppermute | solution.py:113
  302.2 5.4 %collective-permute-start.3 = (f32[128,64]{0,1:T(8,128)S(1)}, f32[128,64]{0,1:T(8,128)S(1)}, u32[]{:S(2)}, u32[]{:S(2)}) collective-permute-start(f32[128,64]{0,1:T(8,128)S(1)} %add.158), channel_id=1, source_target_pairs={{0,2},{1,3},{2,0},{3,1},{4,6},{5,7},{6,4},{7,5},{8,10},{9,11},{10,... | collective-permute-start | bytes 98312 | tf_op jit(solution)/shard_map/ppermute | solution.py:113

commit v7 on v6

--- a/solution.py
+++ b/solution.py
@@ -199,20 +199,24 @@
         gain_parts.append(piece)
         gain_pair = gain_pair - piece.astype(jnp.float32)
 
+    both = jnp.concatenate(
+        [
+            w_qkv.reshape(local_width, nseq, qkv_chunk),
+            w_up.reshape(local_width, nseq, up_chunk),
+        ],
+        axis=2,
+    )
+    both = lax.all_to_all(both, "seq", 1, 0, tiled=True).reshape(nseq * local_width, qkv_chunk + up_chunk)
+    qkv_cols = both[:, :qkv_chunk]
+    up_cols = both[:, qkv_chunk:]
     token_rows = tokens.reshape(rows, local_width)
     token_float = token_rows.astype(jnp.float32)
     gathered = gather_cols(jnp.concatenate([token_rows] + gain_parts, axis=0), nseq)
-    qkv_in, gathered = lax.optimization_barrier(
-        (w_qkv.reshape(local_width, nseq, qkv_chunk), gathered)
-    )
-    qkv_cols = lax.all_to_all(qkv_in, "seq", 1, 0, tiled=True).reshape(nseq * local_width, qkv_chunk)
     pieces = gathered[rows:].astype(jnp.float32)
     gains = (pieces[0:2] + pieces[2:4]) + pieces[4:6]
     normed = full_normalize(gathered[:rows], gains[0])
     qkv_part = jnp.dot(normed, qkv_cols, preferred_element_type=jnp.float32).astype(jnp.bfloat16)
     joined = gather_cols(qkv_part, nseq)
-    up_in, joined = lax.optimization_barrier((w_up.reshape(local_width, nseq, up_chunk), joined))
-    up_cols = lax.all_to_all(up_in, "seq", 1, 0, tiled=True).reshape(nseq * local_width, up_chunk)
     all_queries = joined[:, :head_width].reshape(nsteps, requests, nheads, head_size)
     new_keys = joined[:, head_width : 2 * head_width].reshape(nsteps, requests, nheads, head_size)
     new_values = joined[:, 2 * head_width :].reshape(nsteps, requests, nheads, head_size)
@@ -228,7 +232,7 @@
     )
 
     joined_state = tuple(part.reshape((rows,) + part.shape[2:]) for part in final_state)
-    up_cols, (run_max, run_sum, run_out) = lax.optimization_barrier((up_cols, joined_state))
+    run_max, run_sum, run_out = joined_state
     own_rows = rows // nseq
     stats = jnp.concatenate(
         [

time: 309 us -> 293 us (0.948)
  blocking collectives: 86.5 us -> 52.6 us
  waiting for transfers between devices: 138 us -> 150 us
  other arithmetic: 9.71 us -> 13.6 us
  matrix products: 10.1 us -> 13.3 us
    all_to_all x3 -> x2, blocking collectives: 86.5 us -> 52.6 us  [gather_rows(): return lax.all_to_all(copies, 'seq', 0, 0, tiled=True)]
    all_to_all x2 -> x3, waiting for transfers between devices: 70.9 us -> 89.6 us  [gather_rows(): return lax.all_to_all(copies, 'seq', 0, 0, tiled=True)]
    all_to_all x2 -> x3, starting transfers between devices: 18.4 us -> 25.2 us  [gather_rows(): return lax.all_to_all(copies, 'seq', 0, 0, tiled=True)]
    all_to_all x2 -> x1, waiting for transfers between devices: 29.4 us -> 23 us  [on_device(): lax.all_to_all(both, 'seq', 1, 0, tiled=True)]
    all_to_all x2 -> x1, starting transfers between devices: 12.2 us -> 6.15 us  [on_device(): lax.all_to_all(both, 'seq', 1, 0, tiled=True)]
    unnamed x29 -> x20, local copies, waits for them, and re-layouts: 6.58 us -> 1.83 us
    concatenate x0 -> x1, other arithmetic: none -> 3.1 us  [on_device(): jnp.concatenate([w_qkv.reshape(local_width, nseq, qkv_chunk), w_up.reshap...]
    reshape x6 -> x3, local copies, waits for them, and re-layouts: 5.85 us -> 6.33 us  [the longest x2 4.98 us: on_device(): w_up.reshape(local_width, nseq, up_chunk)]
  transfers between devices with their start and end apart: 9 -> 9, of which waited for: 9 -> 9; matrix products, arithmetic and copies ran while one was open for 2% -> 6% of each run, Pallas kernels for 0% -> 0%
where the time goes in v7:
time: 293 us
  waiting for transfers between devices  150 us (51%)
  blocking collectives  52.6 us (18%)
  starting transfers between devices  41.2 us (14%)
  local copies, waits for them, and re-layouts  21.5 us (7%)
  other arithmetic  13.6 us (5%)
  matrix products  13.3 us (5%)
    all_to_all x3, waiting for transfers between devices, gather_rows(): return lax.all_to_all(copies, 'seq', 0, 0, tiled=True)  89.6 us
    all_to_all x2, blocking collectives, gather_rows(): return lax.all_to_all(copies, 'seq', 0, 0, tiled=True)  52.6 us
    all_to_all x3, starting transfers between devices, gather_rows(): return lax.all_to_all(copies, 'seq', 0, 0, tiled=True)  25.2 us
    all_to_all x1, waiting for transfers between devices, on_device(): lax.all_to_all(both, 'seq', 1, 0, tiled=True)  23 us
    all_to_all x1, waiting for transfers between devices, on_device(): packed = lax.all_to_all(packed, 'seq', 0, 0, tiled=True)  22 us
    ppermute x4, waiting for transfers between devices, head_sum(): other = lax.ppermute(part, 'head', [(i, i ^ stride) for i in range(nhead)])  15.3 us
    all_to_all x1, starting transfers between devices, on_device(): packed = lax.all_to_all(packed, 'seq', 0, 0, tiled=True)  6.28 us
    all_to_all x1, starting transfers between devices, on_device(): lax.all_to_all(both, 'seq', 1, 0, tiled=True)  6.15 us
  transfers between devices with their start and end apart: 9, of which 9 were waited for; matrix products, arithmetic and copies ran while one was open for 6% of the time, Pallas kernels for 0%

profile of v7, /device:TPU:4, one launch (start us, length us, event | category | flops | bytes accessed | tf_op | source)
XLA Modules:
  0.0 292.5 jit_solution(4830639925754517548)
XLA Ops:
  0.0 0.7 fusion.67
  0.7 0.7 fusion.63
  1.4 0.7 subtract_convert_fusion.1
  2.4 0.8 copy.220
  3.4 1.6 broadcast_in_dim.150
  5.0 12.2 %all-to-all-start = ((bf16[64,134,64]{1,2,0:T(8,128)(2,1)}), bf16[64,134,64]{1,2,0:T(8,128)(2,1)S(1)}, u32[]{:S(2)}, u32[]{:S(2)}) async-start(bf16[64,134,64]{1,2,0:T(8,128)(2,1)} %broadcast_in_dim.150), calls=%async_computation | async-start | bytes 4194304 | tf_op jit(solution)/shard_map/all_to_all | solution.py:101
  17.3 2.1 reshape.330
  19.4 2.9 copy.197
  22.2 1.4 copy.195
  23.6 1.3 copy.196
  25.0 3.1 %pad_maximum_fusion = bf16[64,64,112]{2,0,1:T(8,128)(2,1)} fusion(bf16[64,64,64]{2,0,1:T(8,128)(2,1)} %copy.197, bf16[64,64,48]{2,0,1:T(8,128)(2,1)} %copy.196), kind=kLoop, calls=%fused_computation.35 | loop fusion | flops 1835008 | bytes 1835008 | tf_op jit(solution)/shard_map/concatenate | solution.py:202
  28.1 40.3 %all-to-all-done = bf16[64,134,64]{1,2,0:T(8,128)(2,1)S(1)} async-done(((bf16[64,134,64]{1,2,0:T(8,128)(2,1)}), bf16[64,134,64]{1,2,0:T(8,128)(2,1)S(1)}, u32[]{:S(2)}, u32[]{:S(2)}) %all-to-all-start) | async-done | bytes 1097760 | tf_op jit(solution)/shard_map/all_to_all | solution.py:101
  68.4 6.2 %all-to-all-start.1 = ((bf16[64,64,112]{2,0,1:T(8,128)(2,1)}), bf16[64,64,112]{2,0,1:T(8,128)(2,1)}, u32[]{:S(2)}, u32[]{:S(2)}) async-start(bf16[64,64,112]{2,0,1:T(8,128)(2,1)} %pad_maximum_fusion), calls=%async_computation.1 | async-start | bytes 2097152 | tf_op jit(solution)/shard_map/all_to_all | solution.py:209
  74.8 1.1 slice_add_fusion
  76.0 1.7 slice_reduce_fusion
  77.8 0.6 fusion.31
  78.7 0.9 fusion.11
  79.5 23.0 %all-to-all-done.1 = bf16[64,64,112]{2,0,1:T(8,128)(2,1)} async-done(((bf16[64,64,112]{2,0,1:T(8,128)(2,1)}), bf16[64,64,112]{2,0,1:T(8,128)(2,1)}, u32[]{:S(2)}, u32[]{:S(2)}) %all-to-all-start.1) | async-done | bytes 917536 | tf_op jit(solution)/shard_map/all_to_all | solution.py:209
  102.5 1.8 convolution_convert_fusion
  104.3 1.0 broadcast_in_dim.151
  105.3 6.8 %all-to-all-start.2 = ((bf16[64,128,48]{1,2,0:T(8,128)(2,1)}), bf16[64,128,48]{1,2,0:T(8,128)(2,1)S(1)}, u32[]{:S(2)}, u32[]{:S(2)}) async-start(bf16[64,128,48]{1,2,0:T(8,128)(2,1)} %broadcast_in_dim.151), calls=%async_computation.2 | async-start | bytes 1572864 | tf_op jit(solution)/shard_map/all_to_all | solution.py:101
  112.2 0.7 gather_fusion
  113.4 21.4 %all-to-all-done.2 = bf16[64,128,48]{1,2,0:T(8,128)(2,1)S(1)} async-done(((bf16[64,128,48]{1,2,0:T(8,128)(2,1)}), bf16[64,128,48]{1,2,0:T(8,128)(2,1)S(1)}, u32[]{:S(2)}, u32[]{:S(2)}) %all-to-all-start.2) | async-done | bytes 786464 | tf_op jit(solution)/shard_map/all_to_all | solution.py:101
  135.1 0.6 gather_fusion.1
  135.8 4.5 %fusion.71 = (f32[2,32,8]{0,2,1:T(8,128)S(1)}, f32[2,32,64,8]{2,0,3,1:T(2,128)S(1)}) fusion(f32[8]{0:T(128)S(1)} %copy-done.6, f32[2,32,64]{2,0,1:T(2,128)S(1)} %subtract_convert_fusion, bf16[2,32,8,128]{3,2,0,1:T(8,128)(2,1)S(1)} %select_bitcast_fusion, pred[32,64]{1,0:T(8,128)(4,1)S(1)} %compare_and_fusion, bf16[32,64,1024]{2,1,0:T(8,128)(2,1)} %param.17), kind=kOutput, calls=%fused_computation.133 | convolution fusion | flops 8551936 | bytes 4476960 | tf_op jit(solution)/shard_map/sbhe,bthe->sbth/dot_general | solution.py:38
  141.0 0.6 gather_fusion.2
  142.0 0.7 fusion.55
  142.6 3.4 %fusion.18 = f32[2,32,8,128]{3,0,2,1:T(2,128)S(1)} fusion(f32[2,32,64,8]{2,0,3,1:T(2,128)S(1)} %get-tuple-element.36, pred[32,64]{1,0:T(8,128)(4,1)S(1)} %compare_and_fusion, f32[2,32,8]{0,2,1:T(8,128)S(1)} %copy.204, bf16[32,64,1024]{2,1,0:T(8,128)(2,1)} %param.18), kind=kOutput, calls=%fused_computation.25 | convolution fusion | flops 8486912 | bytes 4591616 | tf_op jit(solution)/shard_map/sbth,bthe->sbhe/dot_general | solution.py:62
  148.5 1.0 pad_maximum_fusion.1
  149.5 6.3 %all-to-all-start.3 = ((f32[64,3,8,128]{3,2,1,0:T(8,128)}), f32[64,3,8,128]{3,2,1,0:T(8,128)S(1)}, u32[]{:S(2)}, u32[]{:S(2)}) async-start(f32[64,3,8,128]{3,2,1,0:T(8,128)} %pad_maximum_fusion.1), calls=%async_computation.3 | async-start | bytes 1572864 | tf_op jit(solution)/shard_map/all_to_all | solution.py:248
  156.7 22.0 %all-to-all-done.3 = f32[64,3,8,128]{3,2,1,0:T(8,128)S(1)} async-done(((f32[64,3,8,128]{3,2,1,0:T(8,128)}), f32[64,3,8,128]{3,2,1,0:T(8,128)S(1)}, u32[]{:S(2)}, u32[]{:S(2)}) %all-to-all-start.3) | async-done | bytes 786464 | tf_op jit(solution)/shard_map/all_to_all | solution.py:248
  180.4 18.1 %all_to_all.45 = bf16[64,2,1024]{2,1,0:T(2,128)(2,1)S(1)} all-to-all(bf16[64,2,1024]{2,1,0:T(2,128)(2,1)S(1)} %broadcast_in_dim.165), channel_id=1, replica_groups=mesh['seq'=64,'head'=4] {'seq'}, dimensions={0} | all-to-all | bytes 524288 | tf_op jit(solution)/shard_map/all_to_all | solution.py:101
  198.8 1.3 collective-permute-start
  200.0 2.7 collective-permute-done
  202.8 0.5 collective-permute-start.1
  203.3 4.9 %collective-permute-done.1 = f32[128,64]{0,1:T(8,128)S(1)} collective-permute-done((f32[128,64]{0,1:T(8,128)S(1)}, f32[128,64]{0,1:T(8,128)S(1)}, u32[]{:S(2)}, u32[]{:S(2)}) %collective-permute-start.1) | collective-permute-done | bytes 32800 | tf_op jit(solution)/shard_map/ppermute | solution.py:113
  208.2 1.3 broadcast_in_dim.166
  209.5 6.2 %all-to-all-start.5 = ((bf16[64,128,64]{1,2,0:T(8,128)(2,1)}), bf16[64,128,64]{1,2,0:T(8,128)(2,1)S(1)}, u32[]{:S(2)}, u32[]{:S(2)}) async-start(bf16[64,128,64]{1,2,0:T(8,128)(2,1)} %broadcast_in_dim.166), calls=%async_computation.5 | async-start | bytes 2097152 | tf_op jit(solution)/shard_map/all_to_all | solution.py:101
  215.8 27.9 %all-to-all-done.5 = bf16[64,128,64]{1,2,0:T(8,128)(2,1)S(1)} async-done(((bf16[64,128,64]{1,2,0:T(8,128)(2,1)}), bf16[64,128,64]{1,2,0:T(8,128)(2,1)S(1)}, u32[]{:S(2)}, u32[]{:S(2)}) %all-to-all-start.5) | async-done | bytes 1048608 | tf_op jit(solution)/shard_map/all_to_all | solution.py:101
  243.7 0.6 convert_reduce_fusion
  244.2 0.7 fusion.8
  245.0 2.3 fusion.42
  247.5 34.5 %all_to_all.46 = bf16[64,128,64]{1,2,0:T(8,128)(2,1)S(1)} all-to-all(bf16[64,128,64]{1,2,0:T(8,128)(2,1)S(1)} %broadcast_in_dim.167), channel_id=1, replica_groups=mesh['seq'=64,'head'=4] {'seq'}, dimensions={0} | all-to-all | bytes 2097152 | tf_op jit(solution)/shard_map/all_to_all | solution.py:101
  282.4 1.3 collective-permute-start.2
  283.6 2.7 collective-permute-done.2
  286.4 0.5 collective-permute-start.3
  286.9 4.9 %collective-permute-done.3 = f32[128,64]{0,1:T(8,128)S(1)} collective-permute-done((f32[128,64]{0,1:T(8,128)S(1)}, f32[128,64]{0,1:T(8,128)S(1)}, u32[]{:S(2)}, u32[]{:S(2)}) %collective-permute-start.3) | collective-permute-done | bytes 32800 | tf_op jit(solution)/shard_map/ppermute | solution.py:113
  291.8 0.7 copy.222
  (84 shorter events, 8.8 us)
Async XLA Ops:
  0.0 282.0 %copy-start = (bf16[64,4096]{1,0:T(8,128)(2,1)S(1)}, bf16[64,4096]{1,0:T(8,128)(2,1)}, u32[]{:S(2)}) copy-start(bf16[64,4096]{1,0:T(8,128)(2,1)} %param.25) | copy-start | bytes 1572868
  5.0 12.3 %copy-start.2 = (bf16[64,4096]{1,0:T(8,128)(2,1)S(1)}, bf16[64,4096]{1,0:T(8,128)(2,1)}, u32[]{:S(2)}) copy-start(bf16[64,4096]{1,0:T(8,128)(2,1)} %param.24) | copy-start | bytes 1572868
  5.0 63.4 %all-to-all-start = ((bf16[64,134,64]{1,2,0:T(8,128)(2,1)}), bf16[64,134,64]{1,2,0:T(8,128)(2,1)S(1)}, u32[]{:S(2)}, u32[]{:S(2)}) async-start(bf16[64,134,64]{1,2,0:T(8,128)(2,1)} %broadcast_in_dim.150), calls=%async_computation | async-start | bytes 4194304 | tf_op jit(solution)/shard_map/all_to_all | solution.py:101
  68.4 34.2 %all-to-all-start.1 = ((bf16[64,64,112]{2,0,1:T(8,128)(2,1)}), bf16[64,64,112]{2,0,1:T(8,128)(2,1)}, u32[]{:S(2)}, u32[]{:S(2)}) async-start(bf16[64,64,112]{2,0,1:T(8,128)(2,1)} %pad_maximum_fusion), calls=%async_computation.1 | async-start | bytes 2097152 | tf_op jit(solution)/shard_map/all_to_all | solution.py:209
  102.5 9.6 %copy-start.4 = (s32[32]{0:T(128)S(1)}, s32[32]{0:T(128)}, u32[]{:S(2)}) copy-start(s32[32]{0:T(128)} %param.15) | copy-start | bytes 388
  102.5 9.6 %copy-start.1 = (s32[64]{0:T(128)S(1)}, s32[64]{0:T(128)}, u32[]{:S(2)}) copy-start(s32[64]{0:T(128)} %param.14) | copy-start | bytes 772
  102.5 10.4 %copy-start.5 = (s32[32]{0:T(128)S(1)}, s32[32]{0:T(128)}, u32[]{:S(2)}) copy-start(s32[32]{0:T(128)} %param.16) | copy-start | bytes 388
  105.3 29.5 %all-to-all-start.2 = ((bf16[64,128,48]{1,2,0:T(8,128)(2,1)}), bf16[64,128,48]{1,2,0:T(8,128)(2,1)S(1)}, u32[]{:S(2)}, u32[]{:S(2)}) async-start(bf16[64,128,48]{1,2,0:T(8,128)(2,1)} %broadcast_in_dim.151), calls=%async_computation.2 | async-start | bytes 1572864 | tf_op jit(solution)/shard_map/all_to_all | solution.py:101
  112.1 23.7 %copy-start.6 = (f32[8]{0:T(128)S(1)}, f32[8]{0:T(128)}, u32[]{:S(2)}) copy-start(f32[8]{0:T(128)} %param.19) | copy-start | bytes 100
  149.5 29.2 %all-to-all-start.3 = ((f32[64,3,8,128]{3,2,1,0:T(8,128)}), f32[64,3,8,128]{3,2,1,0:T(8,128)S(1)}, u32[]{:S(2)}, u32[]{:S(2)}) async-start(f32[64,3,8,128]{3,2,1,0:T(8,128)} %pad_maximum_fusion.1), calls=%async_computation.3 | async-start | bytes 1572864 | tf_op jit(solution)/shard_map/all_to_all | solution.py:248
  156.4 42.2 %copy-start.3 = (bf16[64,1024]{1,0:T(8,128)(2,1)S(1)}, bf16[64,1024]{1,0:T(8,128)(2,1)}, u32[]{:S(2)}) copy-start(bf16[64,1024]{1,0:T(8,128)(2,1)} %param.23) | copy-start | bytes 393220
  198.8 4.0 %collective-permute-start = (f32[128,64]{0,1:T(8,128)S(1)}, f32[128,64]{0,1:T(8,128)S(1)}, u32[]{:S(2)}, u32[]{:S(2)}) collective-permute-start(f32[128,64]{0,1:T(8,128)S(1)} %fusion.72), channel_id=1, source_target_pairs={{0,1},{1,0},{2,3},{3,2},{4,5},{5,4},{6,7},{7,6},{8,9},{9,8},{10,11... | collective-permute-start | bytes 98312 | tf_op jit(solution)/shard_map/ppermute | solution.py:113
  202.8 5.4 %collective-permute-start.1 = (f32[128,64]{0,1:T(8,128)S(1)}, f32[128,64]{0,1:T(8,128)S(1)}, u32[]{:S(2)}, u32[]{:S(2)}) collective-permute-start(f32[128,64]{0,1:T(8,128)S(1)} %add.156), channel_id=1, source_target_pairs={{0,2},{1,3},{2,0},{3,1},{4,6},{5,7},{6,4},{7,5},{8,10},{9,11},{10,... | collective-permute-start | bytes 98312 | tf_op jit(solution)/shard_map/ppermute | solution.py:113
  209.5 34.2 %all-to-all-start.5 = ((bf16[64,128,64]{1,2,0:T(8,128)(2,1)}), bf16[64,128,64]{1,2,0:T(8,128)(2,1)S(1)}, u32[]{:S(2)}, u32[]{:S(2)}) async-start(bf16[64,128,64]{1,2,0:T(8,128)(2,1)} %broadcast_in_dim.166), calls=%async_computation.5 | async-start | bytes 2097152 | tf_op jit(solution)/shard_map/all_to_all | solution.py:101
  282.4 4.0 %collective-permute-start.2 = (f32[128,64]{0,1:T(8,128)S(1)}, f32[128,64]{0,1:T(8,128)S(1)}, u32[]{:S(2)}, u32[]{:S(2)}) collective-permute-start(f32[128,64]{0,1:T(8,128)S(1)} %fusion.73), channel_id=1, source_target_pairs={{0,1},{1,0},{2,3},{3,2},{4,5},{5,4},{6,7},{7,6},{8,9},{9,8},{10,11... | collective-permute-start | bytes 98312 | tf_op jit(solution)/shard_map/ppermute | solution.py:113
  286.4 5.4 %collective-permute-start.3 = (f32[128,64]{0,1:T(8,128)S(1)}, f32[128,64]{0,1:T(8,128)S(1)}, u32[]{:S(2)}, u32[]{:S(2)}) collective-permute-start(f32[128,64]{0,1:T(8,128)S(1)} %add.160), channel_id=1, source_target_pairs={{0,2},{1,3},{2,0},{3,1},{4,6},{5,7},{6,4},{7,5},{8,10},{9,11},{10,... | collective-permute-start | bytes 98312 | tf_op jit(solution)/shard_map/ppermute | solution.py:113

commit v8 on v6

--- a/solution.py
+++ b/solution.py
@@ -201,18 +201,31 @@
 
     token_rows = tokens.reshape(rows, local_width)
     token_float = token_rows.astype(jnp.float32)
-    gathered = gather_cols(jnp.concatenate([token_rows] + gain_parts, axis=0), nseq)
-    qkv_in, gathered = lax.optimization_barrier(
-        (w_qkv.reshape(local_width, nseq, qkv_chunk), gathered)
-    )
-    qkv_cols = lax.all_to_all(qkv_in, "seq", 1, 0, tiled=True).reshape(nseq * local_width, qkv_chunk)
+    pad_width = max(local_width, qkv_chunk, up_chunk)
+    head_rows = -(-(rows + 6) // 16) * 16
+
+    def lanes(block):
+        return jnp.pad(block, [(0, 0)] * (block.ndim - 1) + [(0, pad_width - block.shape[-1])])
+
+    token_pack = jnp.concatenate([token_rows] + gain_parts, axis=0)
+    token_pack = jnp.pad(lanes(token_pack), ((0, head_rows - rows - 6), (0, 0)))
+    payload = jnp.concatenate(
+        [
+            jnp.broadcast_to(token_pack[None], (nseq,) + token_pack.shape),
+            lanes(jnp.swapaxes(w_qkv.reshape(local_width, nseq, qkv_chunk), 0, 1)),
+            lanes(jnp.swapaxes(w_up.reshape(local_width, nseq, up_chunk), 0, 1)),
+        ],
+        axis=1,
+    )
+    got = lax.all_to_all(payload, "seq", 0, 0, tiled=True)
+    gathered = jnp.moveaxis(got[:, : rows + 6, :local_width], 0, -2).reshape(rows + 6, nseq * local_width)
+    qkv_cols = got[:, head_rows : head_rows + local_width, :qkv_chunk].reshape(nseq * local_width, qkv_chunk)
+    up_cols = got[:, head_rows + local_width :, :up_chunk].reshape(nseq * local_width, up_chunk)
     pieces = gathered[rows:].astype(jnp.float32)
     gains = (pieces[0:2] + pieces[2:4]) + pieces[4:6]
     normed = full_normalize(gathered[:rows], gains[0])
     qkv_part = jnp.dot(normed, qkv_cols, preferred_element_type=jnp.float32).astype(jnp.bfloat16)
     joined = gather_cols(qkv_part, nseq)
-    up_in, joined = lax.optimization_barrier((w_up.reshape(local_width, nseq, up_chunk), joined))
-    up_cols = lax.all_to_all(up_in, "seq", 1, 0, tiled=True).reshape(nseq * local_width, up_chunk)
     all_queries = joined[:, :head_width].reshape(nsteps, requests, nheads, head_size)
     new_keys = joined[:, head_width : 2 * head_width].reshape(nsteps, requests, nheads, head_size)
     new_values = joined[:, 2 * head_width :].reshape(nsteps, requests, nheads, head_size)
@@ -228,7 +241,7 @@
     )
 
     joined_state = tuple(part.reshape((rows,) + part.shape[2:]) for part in final_state)
-    up_cols, (run_max, run_sum, run_out) = lax.optimization_barrier((up_cols, joined_state))
+    run_max, run_sum, run_out = joined_state
     own_rows = rows // nseq
     stats = jnp.concatenate(
         [

time: 309 us -> 286 us (0.926)
  blocking collectives: 86.5 us -> 171 us
  waiting for transfers between devices: 138 us -> 58.6 us
  starting transfers between devices: 40.7 us -> 16.7 us
  local copies, waits for them, and re-layouts: 23.2 us -> 14.3 us
    all_to_all x0 -> x1, blocking collectives: none -> 84.9 us  [on_device(): got = lax.all_to_all(payload, 'seq', 0, 0, tiled=True)]
    all_to_all x2 -> x1, waiting for transfers between devices: 70.9 us -> 21.4 us  [gather_rows(): return lax.all_to_all(copies, 'seq', 0, 0, tiled=True)]
    all_to_all x2 -> x0, waiting for transfers between devices: 29.4 us -> none  [the longest x1 15 us: on_device(): lax.all_to_all(up_in, 'seq', 1, 0, tiled=True)]
    all_to_all x2 -> x0, starting transfers between devices: 12.2 us -> none  [the longest x1 6.28 us: on_device(): lax.all_to_all(up_in, 'seq', 1, 0, tiled=True)]
    all_to_all x2 -> x1, starting transfers between devices: 18.4 us -> 6.87 us  [gather_rows(): return lax.all_to_all(copies, 'seq', 0, 0, tiled=True)]
    reshape x6 -> x0, local copies, waits for them, and re-layouts: 5.85 us -> none  [the longest x1 2.62 us: gather_cols(): jnp.moveaxis(got, 0, -2).reshape(part.shape[:-1] + (nseq * part.shape[-1],))]
    unnamed x29 -> x21, local copies, waits for them, and re-layouts: 6.58 us -> 3.38 us
  transfers between devices with their start and end apart: 9 -> 6, of which waited for: 9 -> 6; matrix products, arithmetic and copies ran while one was open for 2% -> 1% of each run, Pallas kernels for 0% -> 0%
where the time goes in v8:
time: 286 us; the launch traced here: 285 us
  blocking collectives  171 us (60%)
  waiting for transfers between devices  58.6 us (20%)
  starting transfers between devices  16.7 us (6%)
  local copies, waits for them, and re-layouts  14.3 us (5%)
  matrix products  12.9 us (5%)
  other arithmetic  10.6 us (4%)
    all_to_all x3, blocking collectives, gather_rows(): return lax.all_to_all(copies, 'seq', 0, 0, tiled=True)  86.5 us
    all_to_all x1, blocking collectives, on_device(): got = lax.all_to_all(payload, 'seq', 0, 0, tiled=True)  84.9 us
    all_to_all x1, waiting for transfers between devices, on_device(): packed = lax.all_to_all(packed, 'seq', 0, 0, tiled=True)  22 us
    all_to_all x1, waiting for transfers between devices, gather_rows(): return lax.all_to_all(copies, 'seq', 0, 0, tiled=True)  21.4 us
    ppermute x4, waiting for transfers between devices, head_sum(): other = lax.ppermute(part, 'head', [(i, i ^ stride) for i in range(nhead)])  15.3 us
    all_to_all x1, starting transfers between devices, gather_rows(): return lax.all_to_all(copies, 'seq', 0, 0, tiled=True)  6.87 us
    all_to_all x1, starting transfers between devices, on_device(): packed = lax.all_to_all(packed, 'seq', 0, 0, tiled=True)  6.28 us
  transfers between devices with their start and end apart: 6, of which 6 were waited for; matrix products, arithmetic and copies ran while one was open for 1% of the time, Pallas kernels for 0%

profile of v8, /device:TPU:4, one launch (start us, length us, event | category | flops | bytes accessed | tf_op | source)
XLA Modules:
  0.0 285.2 jit_solution(15919051695017341233)
XLA Ops:
  0.0 0.7 fusion.91
  0.7 0.7 fusion.87
  1.4 0.7 subtract_convert_fusion.1
  2.4 0.8 copy.192
  3.3 1.5 copy.169
  4.8 1.4 copy.168
  6.3 0.2 broadcast_in_dim.150
  6.5 2.1 fusion.9
  8.6 84.9 %all_to_all.30 = bf16[64,272,64]{1,2,0:T(8,128)(2,1)S(1)} all-to-all(bf16[64,272,64]{1,2,0:T(8,128)(2,1)S(1)} %fusion.9), channel_id=1, replica_groups=mesh['seq'=64,'head'=4] {'seq'}, dimensions={0} | all-to-all | bytes 4456448 | tf_op jit(solution)/shard_map/all_to_all | solution.py:220
  93.7 0.6 convert_reduce_fusion.1
  94.3 0.3 slice_convert_fusion
  94.5 1.1 slice_add_fusion
  95.7 1.7 slice_reduce_fusion
  97.4 1.0 fusion.30
  98.5 1.0 broadcast_in_dim.151
  99.5 6.9 %all-to-all-start.1 = ((bf16[64,128,48]{1,2,0:T(8,128)(2,1)}), bf16[64,128,48]{1,2,0:T(8,128)(2,1)S(1)}, u32[]{:S(2)}, u32[]{:S(2)}) async-start(bf16[64,128,48]{1,2,0:T(8,128)(2,1)} %broadcast_in_dim.151), calls=%async_computation.1 | async-start | bytes 1572864 | tf_op jit(solution)/shard_map/all_to_all | solution.py:101
  106.4 0.7 gather_fusion
  107.6 21.4 %all-to-all-done.1 = bf16[64,128,48]{1,2,0:T(8,128)(2,1)S(1)} async-done(((bf16[64,128,48]{1,2,0:T(8,128)(2,1)}), bf16[64,128,48]{1,2,0:T(8,128)(2,1)S(1)}, u32[]{:S(2)}, u32[]{:S(2)}) %all-to-all-start.1) | async-done | bytes 786464 | tf_op jit(solution)/shard_map/all_to_all | solution.py:101
  129.3 0.6 gather_fusion.1
  130.1 4.5 %fusion.95 = (f32[2,32,8]{0,2,1:T(8,128)S(1)}, f32[2,32,64,8]{2,0,3,1:T(2,128)S(1)}) fusion(f32[8]{0:T(128)S(1)} %copy-done.6, f32[2,32,64]{2,0,1:T(2,128)S(1)} %subtract_convert_fusion, bf16[2,32,8,128]{3,2,0,1:T(8,128)(2,1)S(1)} %select_bitcast_fusion, pred[32,64]{1,0:T(8,128)(4,1)S(1)} %compare_and_fusion, bf16[32,64,1024]{2,1,0:T(8,128)(2,1)} %param.17), kind=kOutput, calls=%fused_computation.156 | convolution fusion | flops 8551936 | bytes 4476960 | tf_op jit(solution)/shard_map/sbhe,bthe->sbth/dot_general | solution.py:38
  134.6 0.3 copy.173
  135.3 0.6 gather_fusion.2
  136.0 0.3 copy.176
  136.2 0.7 fusion.79
  136.9 3.4 %fusion.24 = f32[2,32,8,128]{3,0,2,1:T(2,128)S(1)} fusion(f32[2,32,64,8]{2,0,3,1:T(2,128)S(1)} %get-tuple-element.36, pred[32,64]{1,0:T(8,128)(4,1)S(1)} %compare_and_fusion, f32[2,32,8]{0,2,1:T(8,128)S(1)} %copy.176, bf16[32,64,1024]{2,1,0:T(8,128)(2,1)} %param.18), kind=kOutput, calls=%fused_computation.36 | convolution fusion | flops 8486912 | bytes 4591616 | tf_op jit(solution)/shard_map/sbth,bthe->sbhe/dot_general | solution.py:62
  140.4 0.5 fusion.77
  141.5 0.4 copy.182
  142.0 0.4 copy.181
  142.8 0.9 pad_maximum_fusion
  143.7 6.3 %all-to-all-start.2 = ((f32[64,3,8,128]{3,2,1,0:T(8,128)}), f32[64,3,8,128]{3,2,1,0:T(8,128)S(1)}, u32[]{:S(2)}, u32[]{:S(2)}) async-start(f32[64,3,8,128]{3,2,1,0:T(8,128)} %pad_maximum_fusion), calls=%async_computation.2 | async-start | bytes 1572864 | tf_op jit(solution)/shard_map/all_to_all | solution.py:257
  150.6 0.3 fusion.48
  150.9 22.0 %all-to-all-done.2 = f32[64,3,8,128]{3,2,1,0:T(8,128)S(1)} async-done(((f32[64,3,8,128]{3,2,1,0:T(8,128)}), f32[64,3,8,128]{3,2,1,0:T(8,128)S(1)}, u32[]{:S(2)}, u32[]{:S(2)}) %all-to-all-start.2) | async-done | bytes 786464 | tf_op jit(solution)/shard_map/all_to_all | solution.py:257
  173.1 0.4 copy.184
  174.6 18.1 %all_to_all.31 = bf16[64,2,1024]{2,1,0:T(2,128)(2,1)S(1)} all-to-all(bf16[64,2,1024]{2,1,0:T(2,128)(2,1)S(1)} %broadcast_in_dim.165), channel_id=1, replica_groups=mesh['seq'=64,'head'=4] {'seq'}, dimensions={0} | all-to-all | bytes 524288 | tf_op jit(solution)/shard_map/all_to_all | solution.py:101
  193.0 1.3 collective-permute-start
  194.3 2.7 collective-permute-done
  197.0 0.5 collective-permute-start.1
  197.5 4.9 %collective-permute-done.1 = f32[128,64]{0,1:T(8,128)S(1)} collective-permute-done((f32[128,64]{0,1:T(8,128)S(1)}, f32[128,64]{0,1:T(8,128)S(1)}, u32[]{:S(2)}, u32[]{:S(2)}) %collective-permute-start.1) | collective-permute-done | bytes 32800 | tf_op jit(solution)/shard_map/ppermute | solution.py:113
  202.7 34.0 %all_to_all.32 = bf16[64,128,64]{1,2,0:T(8,128)(2,1)S(1)} all-to-all(bf16[64,128,64]{1,2,0:T(8,128)(2,1)S(1)} %broadcast_in_dim.166), channel_id=1, replica_groups=mesh['seq'=64,'head'=4] {'seq'}, dimensions={0} | all-to-all | bytes 2097152 | tf_op jit(solution)/shard_map/all_to_all | solution.py:101
  236.6 0.6 convert_reduce_fusion
  237.2 2.7 fusion.61
  240.2 34.5 %all_to_all.33 = bf16[64,128,64]{1,2,0:T(8,128)(2,1)S(1)} all-to-all(bf16[64,128,64]{1,2,0:T(8,128)(2,1)S(1)} %broadcast_in_dim.167), channel_id=1, replica_groups=mesh['seq'=64,'head'=4] {'seq'}, dimensions={0} | all-to-all | bytes 2097152 | tf_op jit(solution)/shard_map/all_to_all | solution.py:101
  274.7 0.3 fusion.97
  275.0 1.3 collective-permute-start.2
  276.3 2.7 collective-permute-done.2
  279.0 0.5 collective-permute-start.3
  279.6 4.9 %collective-permute-done.3 = f32[128,64]{0,1:T(8,128)S(1)} collective-permute-done((f32[128,64]{0,1:T(8,128)S(1)}, f32[128,64]{0,1:T(8,128)S(1)}, u32[]{:S(2)}, u32[]{:S(2)}) %collective-permute-start.3) | collective-permute-done | bytes 32800 | tf_op jit(solution)/shard_map/ppermute | solution.py:113
  284.5 0.7 copy.194
  (74 shorter events, 5.5 us)
Async XLA Ops:
  0.0 274.7 %copy-start = (bf16[64,4096]{1,0:T(8,128)(2,1)S(1)}, bf16[64,4096]{1,0:T(8,128)(2,1)}, u32[]{:S(2)}) copy-start(bf16[64,4096]{1,0:T(8,128)(2,1)} %param.25) | copy-start | bytes 1572868
  93.5 3.9 %copy-start.2 = (bf16[64,272,64]{1,2,0:T(8,128)(2,1)}, bf16[64,272,64]{1,2,0:T(8,128)(2,1)S(1)}, u32[]{:S(2)}) copy-start(bf16[64,272,64]{1,2,0:T(8,128)(2,1)S(1)} %all_to_all.30) | copy-start | bytes 6684676
  98.5 7.9 %copy-start.4 = (s32[32]{0:T(128)S(1)}, s32[32]{0:T(128)}, u32[]{:S(2)}) copy-start(s32[32]{0:T(128)} %param.15) | copy-start | bytes 388
  98.5 7.9 %copy-start.1 = (s32[64]{0:T(128)S(1)}, s32[64]{0:T(128)}, u32[]{:S(2)}) copy-start(s32[64]{0:T(128)} %param.14) | copy-start | bytes 772
  98.5 8.7 %copy-start.5 = (s32[32]{0:T(128)S(1)}, s32[32]{0:T(128)}, u32[]{:S(2)}) copy-start(s32[32]{0:T(128)} %param.16) | copy-start | bytes 388
  99.5 29.6 %all-to-all-start.1 = ((bf16[64,128,48]{1,2,0:T(8,128)(2,1)}), bf16[64,128,48]{1,2,0:T(8,128)(2,1)S(1)}, u32[]{:S(2)}, u32[]{:S(2)}) async-start(bf16[64,128,48]{1,2,0:T(8,128)(2,1)} %broadcast_in_dim.151), calls=%async_computation.1 | async-start | bytes 1572864 | tf_op jit(solution)/shard_map/all_to_all | solution.py:101
  106.4 23.7 %copy-start.6 = (f32[8]{0:T(128)S(1)}, f32[8]{0:T(128)}, u32[]{:S(2)}) copy-start(f32[8]{0:T(128)} %param.19) | copy-start | bytes 100
  143.7 29.2 %all-to-all-start.2 = ((f32[64,3,8,128]{3,2,1,0:T(8,128)}), f32[64,3,8,128]{3,2,1,0:T(8,128)S(1)}, u32[]{:S(2)}, u32[]{:S(2)}) async-start(f32[64,3,8,128]{3,2,1,0:T(8,128)} %pad_maximum_fusion), calls=%async_computation.2 | async-start | bytes 1572864 | tf_op jit(solution)/shard_map/all_to_all | solution.py:257
  150.6 42.2 %copy-start.3 = (bf16[64,1024]{1,0:T(8,128)(2,1)S(1)}, bf16[64,1024]{1,0:T(8,128)(2,1)}, u32[]{:S(2)}) copy-start(bf16[64,1024]{1,0:T(8,128)(2,1)} %param.23) | copy-start | bytes 393220
  193.0 4.0 %collective-permute-start = (f32[128,64]{0,1:T(8,128)S(1)}, f32[128,64]{0,1:T(8,128)S(1)}, u32[]{:S(2)}, u32[]{:S(2)}) collective-permute-start(f32[128,64]{0,1:T(8,128)S(1)} %fusion.96), channel_id=1, source_target_pairs={{0,1},{1,0},{2,3},{3,2},{4,5},{5,4},{6,7},{7,6},{8,9},{9,8},{10,11... | collective-permute-start | bytes 98312 | tf_op jit(solution)/shard_map/ppermute | solution.py:113
  197.0 5.4 %collective-permute-start.1 = (f32[128,64]{0,1:T(8,128)S(1)}, f32[128,64]{0,1:T(8,128)S(1)}, u32[]{:S(2)}, u32[]{:S(2)}) collective-permute-start(f32[128,64]{0,1:T(8,128)S(1)} %add.160), channel_id=1, source_target_pairs={{0,2},{1,3},{2,0},{3,1},{4,6},{5,7},{6,4},{7,5},{8,10},{9,11},{10,... | collective-permute-start | bytes 98312 | tf_op jit(solution)/shard_map/ppermute | solution.py:113
  275.0 4.0 %collective-permute-start.2 = (f32[128,64]{0,1:T(8,128)S(1)}, f32[128,64]{0,1:T(8,128)S(1)}, u32[]{:S(2)}, u32[]{:S(2)}) collective-permute-start(f32[128,64]{0,1:T(8,128)S(1)} %fusion.97), channel_id=1, source_target_pairs={{0,1},{1,0},{2,3},{3,2},{4,5},{5,4},{6,7},{7,6},{8,9},{9,8},{10,11... | collective-permute-start | bytes 98312 | tf_op jit(solution)/shard_map/ppermute | solution.py:113
  279.0 5.4 %collective-permute-start.3 = (f32[128,64]{0,1:T(8,128)S(1)}, f32[128,64]{0,1:T(8,128)S(1)}, u32[]{:S(2)}, u32[]{:S(2)}) collective-permute-start(f32[128,64]{0,1:T(8,128)S(1)} %add.164), channel_id=1, source_target_pairs={{0,2},{1,3},{2,0},{3,1},{4,6},{5,7},{6,4},{7,5},{8,10},{9,11},{10,... | collective-permute-start | bytes 98312 | tf_op jit(solution)/shard_map/ppermute | solution.py:113

commit v9 on v8

--- a/solution.py
+++ b/solution.py
@@ -201,29 +201,32 @@
 
     token_rows = tokens.reshape(rows, local_width)
     token_float = token_rows.astype(jnp.float32)
-    pad_width = max(local_width, qkv_chunk, up_chunk)
-    head_rows = -(-(rows + 6) // 16) * 16
+    pad_width = max(local_width, qkv_chunk + 6, up_chunk)
 
     def lanes(block):
         return jnp.pad(block, [(0, 0)] * (block.ndim - 1) + [(0, pad_width - block.shape[-1])])
 
-    token_pack = jnp.concatenate([token_rows] + gain_parts, axis=0)
-    token_pack = jnp.pad(lanes(token_pack), ((0, head_rows - rows - 6), (0, 0)))
+    gain_cols = jnp.concatenate(gain_parts, axis=0).T
+    qkv_block = jnp.swapaxes(w_qkv.reshape(local_width, nseq, qkv_chunk), 0, 1)
+    qkv_block = jnp.concatenate(
+        [qkv_block, jnp.broadcast_to(gain_cols[None], (nseq,) + gain_cols.shape)], axis=2
+    )
     payload = jnp.concatenate(
         [
-            jnp.broadcast_to(token_pack[None], (nseq,) + token_pack.shape),
-            lanes(jnp.swapaxes(w_qkv.reshape(local_width, nseq, qkv_chunk), 0, 1)),
+            jnp.broadcast_to(lanes(token_rows)[None], (nseq, rows, pad_width)),
+            lanes(qkv_block),
             lanes(jnp.swapaxes(w_up.reshape(local_width, nseq, up_chunk), 0, 1)),
         ],
         axis=1,
     )
     got = lax.all_to_all(payload, "seq", 0, 0, tiled=True)
-    gathered = jnp.moveaxis(got[:, : rows + 6, :local_width], 0, -2).reshape(rows + 6, nseq * local_width)
-    qkv_cols = got[:, head_rows : head_rows + local_width, :qkv_chunk].reshape(nseq * local_width, qkv_chunk)
-    up_cols = got[:, head_rows + local_width :, :up_chunk].reshape(nseq * local_width, up_chunk)
-    pieces = gathered[rows:].astype(jnp.float32)
+    gathered = jnp.moveaxis(got[:, :rows, :local_width], 0, -2).reshape(rows, nseq * local_width)
+    qkv_got = got[:, rows : rows + local_width]
+    qkv_cols = qkv_got[:, :, :qkv_chunk].reshape(nseq * local_width, qkv_chunk)
+    pieces = qkv_got[:, :, qkv_chunk : qkv_chunk + 6].reshape(nseq * local_width, 6).T.astype(jnp.float32)
+    up_cols = got[:, rows + local_width :, :up_chunk].reshape(nseq * local_width, up_chunk)
     gains = (pieces[0:2] + pieces[2:4]) + pieces[4:6]
-    normed = full_normalize(gathered[:rows], gains[0])
+    normed = full_normalize(gathered, gains[0])
     qkv_part = jnp.dot(normed, qkv_cols, preferred_element_type=jnp.float32).astype(jnp.bfloat16)
     joined = gather_cols(qkv_part, nseq)
     all_queries = joined[:, :head_width].reshape(nsteps, requests, nheads, head_size)

time: 286 us -> 273 us (0.955)
  blocking collectives: 171 us -> 116 us
  waiting for transfers between devices: 58.6 us -> 80.9 us
  local copies, waits for them, and re-layouts: 14.3 us -> 25.2 us
  starting transfers between devices: 16.7 us -> 22.4 us
    all_to_all x3 -> x2, blocking collectives: 86.5 us -> 52.6 us  [gather_rows(): return lax.all_to_all(copies, 'seq', 0, 0, tiled=True)]
    all_to_all x1 -> x2, waiting for transfers between devices: 21.4 us -> 48.6 us  [gather_rows(): return lax.all_to_all(copies, 'seq', 0, 0, tiled=True)]
    all_to_all x1, blocking collectives: 84.9 us -> 63 us  [on_device(): got = lax.all_to_all(payload, 'seq', 0, 0, tiled=True)]
    all_to_all x1 -> x2, starting transfers between devices: 6.87 us -> 12.6 us  [gather_rows(): return lax.all_to_all(copies, 'seq', 0, 0, tiled=True)]
    all_to_all x1, waiting for transfers between devices: 22 us -> 17.1 us  [on_device(): packed = lax.all_to_all(packed, 'seq', 0, 0, tiled=True)]
  transfers between devices with their start and end apart: 6 -> 7, of which waited for: 6 -> 7; matrix products, arithmetic and copies ran while one was open for 1% -> 3% of each run, Pallas kernels for 0% -> 0%
where the time goes in v9:
time: 273 us; the launch traced here: 271 us
  blocking collectives  116 us (42%)
  waiting for transfers between devices  80.9 us (30%)
  local copies, waits for them, and re-layouts  25.2 us (9%)
  starting transfers between devices  22.4 us (8%)
  other arithmetic  13.4 us (5%)
  matrix products  13.4 us (5%)
    all_to_all x1, blocking collectives, on_device(): got = lax.all_to_all(payload, 'seq', 0, 0, tiled=True)  63 us
    all_to_all x2, blocking collectives, gather_rows(): return lax.all_to_all(copies, 'seq', 0, 0, tiled=True)  52.6 us
    all_to_all x2, waiting for transfers between devices, gather_rows(): return lax.all_to_all(copies, 'seq', 0, 0, tiled=True)  48.6 us
    all_to_all x1, waiting for transfers between devices, on_device(): packed = lax.all_to_all(packed, 'seq', 0, 0, tiled=True)  17.1 us
    ppermute x4, waiting for transfers between devices, head_sum(): other = lax.ppermute(part, 'head', [(i, i ^ stride) for i in range(nhead)])  15.3 us
    all_to_all x2, starting transfers between devices, gather_rows(): return lax.all_to_all(copies, 'seq', 0, 0, tiled=True)  12.6 us
    all_to_all x1, starting transfers between devices, on_device(): packed = lax.all_to_all(packed, 'seq', 0, 0, tiled=True)  6.28 us
  transfers between devices with their start and end apart: 7, of which 7 were waited for; matrix products, arithmetic and copies ran while one was open for 3% of the time, Pallas kernels for 0%

profile of v9, /device:TPU:4, one launch (start us, length us, event | category | flops | bytes accessed | tf_op | source)
XLA Modules:
  0.0 271.5 jit_solution(3295677953410337329)
XLA Ops:
  0.0 0.7 fusion.84
  1.4 0.7 subtract_convert_fusion.1
  2.1 1.4 copy.214
  3.5 0.8 copy.243
  4.3 2.1 reshape.349
  6.4 1.2 copy.215
  8.2 0.7 pad_maximum_fusion
  9.0 63.0 %all_to_all.30 = bf16[64,256,64]{1,2,0:T(8,128)(2,1)S(1)} all-to-all(bf16[64,256,64]{1,2,0:T(8,128)(2,1)S(1)} %pad_maximum_fusion), channel_id=1, replica_groups=mesh['seq'=64,'head'=4] {'seq'}, dimensions={0} | all-to-all | bytes 4194304 | tf_op jit(solution)/shard_map/all_to_all | solution.py:222
  73.5 0.8 fusion.28
  74.4 1.0 broadcast_in_dim.158
  75.4 6.1 %all-to-all-start.1 = ((bf16[64,128,48]{1,2,0:T(8,128)(2,1)}), bf16[64,128,48]{1,2,0:T(8,128)(2,1)S(1)}, u32[]{:S(2)}, u32[]{:S(2)}) async-start(bf16[64,128,48]{1,2,0:T(8,128)(2,1)} %broadcast_in_dim.158), calls=%async_computation.1 | async-start | bytes 1572864 | tf_op jit(solution)/shard_map/all_to_all | solution.py:101
  81.5 0.7 gather_fusion
  83.3 20.9 %all-to-all-done.1 = bf16[64,128,48]{1,2,0:T(8,128)(2,1)S(1)} async-done(((bf16[64,128,48]{1,2,0:T(8,128)(2,1)}), bf16[64,128,48]{1,2,0:T(8,128)(2,1)S(1)}, u32[]{:S(2)}, u32[]{:S(2)}) %all-to-all-start.1) | async-done | bytes 786464 | tf_op jit(solution)/shard_map/all_to_all | solution.py:101
  104.1 0.9 fusion.87
  105.1 1.1 copy.219
  106.9 4.5 %fusion.88 = (f32[2,32,8]{0,2,1:T(8,128)S(1)}, f32[2,32,64,8]{2,0,3,1:T(2,128)S(1)}) fusion(f32[8]{0:T(128)S(1)} %copy-done.9, f32[2,32,64]{2,0,1:T(2,128)S(1)} %subtract_convert_fusion, bf16[2,32,8,128]{3,2,0,1:T(8,128)(2,1)S(1)} %select_bitcast_fusion, pred[32,64]{1,0:T(8,128)(4,1)S(1)} %compare_and_fusion, bf16[32,64,1024]{2,1,0:T(8,128)(2,1)} %param.17), kind=kOutput, calls=%fused_computation.148 | convolution fusion | flops 8551936 | bytes 4476960 | tf_op jit(solution)/shard_map/sbhe,bthe->sbth/dot_general | solution.py:38
  112.1 0.7 gather_fusion.2
  112.9 0.8 select_bitcast_fusion.1
  113.9 1.3 fusion.72
  115.3 3.4 %fusion.22 = f32[2,32,8,128]{3,0,2,1:T(2,128)S(1)} fusion(f32[2,32,64,8]{2,0,3,1:T(2,128)S(1)} %get-tuple-element.36, pred[32,64]{1,0:T(8,128)(4,1)} %copy-done.3, f32[2,32,8]{0,2,1:T(8,128)S(1)} %copy.225, bf16[32,64,1024]{2,1,0:T(8,128)(2,1)} %param.18), kind=kOutput, calls=%fused_computation.29 | convolution fusion | flops 8486912 | bytes 4591616 | tf_op jit(solution)/shard_map/sbth,bthe->sbhe/dot_general | solution.py:62
  119.8 0.7 copy.229
  120.5 1.3 copy.231
  121.8 1.1 copy.230
  123.2 1.1 maximum_bitcast_fusion
  124.3 0.9 pad_maximum_fusion.1
  125.2 6.3 %all-to-all-start.2 = ((f32[64,3,8,128]{3,2,1,0:T(8,128)}), f32[64,3,8,128]{3,2,1,0:T(8,128)S(1)}, u32[]{:S(2)}, u32[]{:S(2)}) async-start(f32[64,3,8,128]{3,2,1,0:T(8,128)} %pad_maximum_fusion.1), calls=%async_computation.2 | async-start | bytes 1572864 | tf_op jit(solution)/shard_map/all_to_all | solution.py:260
  131.5 2.1 constant_dynamic-slice_fusion
  133.6 1.1 copy.249
  134.7 1.1 copy.250
  135.8 1.4 fusion.48
  137.2 17.1 %all-to-all-done.2 = f32[64,3,8,128]{3,2,1,0:T(8,128)S(1)} async-done(((f32[64,3,8,128]{3,2,1,0:T(8,128)}), f32[64,3,8,128]{3,2,1,0:T(8,128)S(1)}, u32[]{:S(2)}, u32[]{:S(2)}) %all-to-all-start.2) | async-done | bytes 786464 | tf_op jit(solution)/shard_map/all_to_all | solution.py:260
  154.4 0.8 fusion.51
  155.2 1.4 copy.233
  157.6 18.1 %all_to_all.31 = bf16[64,2,1024]{2,1,0:T(2,128)(2,1)S(1)} all-to-all(bf16[64,2,1024]{2,1,0:T(2,128)(2,1)S(1)} %broadcast_in_dim.172), channel_id=1, replica_groups=mesh['seq'=64,'head'=4] {'seq'}, dimensions={0} | all-to-all | bytes 524288 | tf_op jit(solution)/shard_map/all_to_all | solution.py:101
  175.8 1.1 fusion.89
  176.9 1.3 collective-permute-start
  178.2 2.7 %collective-permute-done = f32[128,64]{0,1:T(8,128)S(1)} collective-permute-done((f32[128,64]{0,1:T(8,128)S(1)}, f32[128,64]{0,1:T(8,128)S(1)}, u32[]{:S(2)}, u32[]{:S(2)}) %collective-permute-start) | collective-permute-done | bytes 32800 | tf_op jit(solution)/shard_map/ppermute | solution.py:113
  181.4 4.9 %collective-permute-done.1 = f32[128,64]{0,1:T(8,128)S(1)} collective-permute-done((f32[128,64]{0,1:T(8,128)S(1)}, f32[128,64]{0,1:T(8,128)S(1)}, u32[]{:S(2)}, u32[]{:S(2)}) %collective-permute-start.1) | collective-permute-done | bytes 32800 | tf_op jit(solution)/shard_map/ppermute | solution.py:113
  186.4 1.3 broadcast_in_dim.173
  187.6 6.5 %all-to-all-start.4 = ((bf16[64,128,64]{1,2,0:T(8,128)(2,1)}), bf16[64,128,64]{1,2,0:T(8,128)(2,1)}, u32[]{:S(2)}, u32[]{:S(2)}) async-start(bf16[64,128,64]{1,2,0:T(8,128)(2,1)} %broadcast_in_dim.173), calls=%async_computation.4 | async-start | bytes 2097152 | tf_op jit(solution)/shard_map/all_to_all | solution.py:101
  194.2 27.7 %all-to-all-done.4 = bf16[64,128,64]{1,2,0:T(8,128)(2,1)} async-done(((bf16[64,128,64]{1,2,0:T(8,128)(2,1)}), bf16[64,128,64]{1,2,0:T(8,128)(2,1)}, u32[]{:S(2)}, u32[]{:S(2)}) %all-to-all-start.4) | async-done | bytes 1048608 | tf_op jit(solution)/shard_map/all_to_all | solution.py:101
  221.9 1.8 convert_reduce_fusion
  223.7 2.5 fusion.57
  226.5 34.5 %all_to_all.32 = bf16[64,128,64]{1,2,0:T(8,128)(2,1)S(1)} all-to-all(bf16[64,128,64]{1,2,0:T(8,128)(2,1)S(1)} %broadcast_in_dim.174), channel_id=1, replica_groups=mesh['seq'=64,'head'=4] {'seq'}, dimensions={0} | all-to-all | bytes 2097152 | tf_op jit(solution)/shard_map/all_to_all | solution.py:101
  261.3 1.3 collective-permute-start.2
  262.6 2.7 %collective-permute-done.2 = f32[128,64]{0,1:T(8,128)S(1)} collective-permute-done((f32[128,64]{0,1:T(8,128)S(1)}, f32[128,64]{0,1:T(8,128)S(1)}, u32[]{:S(2)}, u32[]{:S(2)}) %collective-permute-start.2) | collective-permute-done | bytes 32800 | tf_op jit(solution)/shard_map/ppermute | solution.py:113
  265.8 4.9 %collective-permute-done.3 = f32[128,64]{0,1:T(8,128)S(1)} collective-permute-done((f32[128,64]{0,1:T(8,128)S(1)}, f32[128,64]{0,1:T(8,128)S(1)}, u32[]{:S(2)}, u32[]{:S(2)}) %collective-permute-start.3) | collective-permute-done | bytes 32800 | tf_op jit(solution)/shard_map/ppermute | solution.py:113
  270.8 0.7 copy.245
  (86 shorter events, 9.6 us)
Async XLA Ops:
  0.0 261.0 %copy-start = (bf16[64,4096]{1,0:T(8,128)(2,1)S(1)}, bf16[64,4096]{1,0:T(8,128)(2,1)}, u32[]{:S(2)}) copy-start(bf16[64,4096]{1,0:T(8,128)(2,1)} %param.25) | copy-start | bytes 1572868
  74.4 7.1 %copy-start.6 = (s32[32]{0:T(128)S(1)}, s32[32]{0:T(128)}, u32[]{:S(2)}) copy-start(s32[32]{0:T(128)} %param.15) | copy-start | bytes 388
  74.4 7.1 %copy-start.1 = (s32[64]{0:T(128)S(1)}, s32[64]{0:T(128)}, u32[]{:S(2)}) copy-start(s32[64]{0:T(128)} %param.14) | copy-start | bytes 772
  74.4 8.5 %copy-start.8 = (s32[32]{0:T(128)S(1)}, s32[32]{0:T(128)}, u32[]{:S(2)}) copy-start(s32[32]{0:T(128)} %param.16) | copy-start | bytes 388
  75.4 28.8 %all-to-all-start.1 = ((bf16[64,128,48]{1,2,0:T(8,128)(2,1)}), bf16[64,128,48]{1,2,0:T(8,128)(2,1)S(1)}, u32[]{:S(2)}, u32[]{:S(2)}) async-start(bf16[64,128,48]{1,2,0:T(8,128)(2,1)} %broadcast_in_dim.158), calls=%async_computation.1 | async-start | bytes 1572864 | tf_op jit(solution)/shard_map/all_to_all | solution.py:101
  81.5 25.5 %copy-start.9 = (f32[8]{0:T(128)S(1)}, f32[8]{0:T(128)}, u32[]{:S(2)}) copy-start(f32[8]{0:T(128)} %param.19) | copy-start | bytes 100
  81.5 30.0 %copy-start.5 = (pred[32]{0:T(512)(128)(4,1)}, pred[32]{0:T(512)(128)(4,1)S(1)}, u32[]{:S(2)}) copy-start(pred[32]{0:T(512)(128)(4,1)S(1)} %get-tuple-element.20) | copy-start | bytes 100
  81.5 30.0 %copy-start.4 = (s32[1024]{0:T(1024)}, s32[1024]{0:T(1024)S(1)}, u32[]{:S(2)}) copy-start(s32[1024]{0:T(1024)S(1)} %pad_clamp_fusion) | copy-start | bytes 12292
  83.0 28.5 %copy-start.3 = (pred[32,64]{1,0:T(8,128)(4,1)}, pred[32,64]{1,0:T(8,128)(4,1)S(1)}, u32[]{:S(2)}) copy-start(pred[32,64]{1,0:T(8,128)(4,1)S(1)} %compare_and_fusion) | copy-start | bytes 6148
  115.3 3.6 %copy-start.7 = (s32[32]{0:T(128)S(1)}, s32[32]{0:T(128)}, u32[]{:S(2)}) copy-start(s32[32]{0:T(128)} %param.15) | copy-start | bytes 388
  123.2 8.4 %copy-start.10 = (f32[8]{0:T(128)S(1)}, f32[8]{0:T(128)}, u32[]{:S(2)}) copy-start(f32[8]{0:T(128)} %param.19) | copy-start | bytes 100
  125.2 29.2 %all-to-all-start.2 = ((f32[64,3,8,128]{3,2,1,0:T(8,128)}), f32[64,3,8,128]{3,2,1,0:T(8,128)S(1)}, u32[]{:S(2)}, u32[]{:S(2)}) async-start(f32[64,3,8,128]{3,2,1,0:T(8,128)} %pad_maximum_fusion.1), calls=%async_computation.2 | async-start | bytes 1572864 | tf_op jit(solution)/shard_map/all_to_all | solution.py:260
  175.7 18.5 %copy-start.2 = (f32[4096]{0:T(1024)S(1)}, f32[4096]{0:T(1024)}, u32[]{:S(2)}) copy-start(f32[4096]{0:T(1024)} %get-tuple-element.11) | copy-start | bytes 49156
  176.9 4.0 %collective-permute-start = (f32[128,64]{0,1:T(8,128)S(1)}, f32[128,64]{0,1:T(8,128)S(1)}, u32[]{:S(2)}, u32[]{:S(2)}) collective-permute-start(f32[128,64]{0,1:T(8,128)S(1)} %fusion.89), channel_id=1, source_target_pairs={{0,1},{1,0},{2,3},{3,2},{4,5},{5,4},{6,7},{7,6},{8,9},{9,8},{10,11... | collective-permute-start | bytes 98312 | tf_op jit(solution)/shard_map/ppermute | solution.py:113
  180.9 5.4 %collective-permute-start.1 = (f32[128,64]{0,1:T(8,128)S(1)}, f32[128,64]{0,1:T(8,128)S(1)}, u32[]{:S(2)}, u32[]{:S(2)}) collective-permute-start(f32[128,64]{0,1:T(8,128)S(1)} %add.156), channel_id=1, source_target_pairs={{0,2},{1,3},{2,0},{3,1},{4,6},{5,7},{6,4},{7,5},{8,10},{9,11},{10,... | collective-permute-start | bytes 98312 | tf_op jit(solution)/shard_map/ppermute | solution.py:113
  187.6 34.3 %all-to-all-start.4 = ((bf16[64,128,64]{1,2,0:T(8,128)(2,1)}), bf16[64,128,64]{1,2,0:T(8,128)(2,1)}, u32[]{:S(2)}, u32[]{:S(2)}) async-start(bf16[64,128,64]{1,2,0:T(8,128)(2,1)} %broadcast_in_dim.173), calls=%async_computation.4 | async-start | bytes 2097152 | tf_op jit(solution)/shard_map/all_to_all | solution.py:101
  261.3 4.0 %collective-permute-start.2 = (f32[128,64]{0,1:T(8,128)S(1)}, f32[128,64]{0,1:T(8,128)S(1)}, u32[]{:S(2)}, u32[]{:S(2)}) collective-permute-start(f32[128,64]{0,1:T(8,128)S(1)} %fusion.90), channel_id=1, source_target_pairs={{0,1},{1,0},{2,3},{3,2},{4,5},{5,4},{6,7},{7,6},{8,9},{9,8},{10,11... | collective-permute-start | bytes 98312 | tf_op jit(solution)/shard_map/ppermute | solution.py:113
  265.3 5.4 %collective-permute-start.3 = (f32[128,64]{0,1:T(8,128)S(1)}, f32[128,64]{0,1:T(8,128)S(1)}, u32[]{:S(2)}, u32[]{:S(2)}) collective-permute-start(f32[128,64]{0,1:T(8,128)S(1)} %add.160), channel_id=1, source_target_pairs={{0,2},{1,3},{2,0},{3,1},{4,6},{5,7},{6,4},{7,5},{8,10},{9,11},{10,... | collective-permute-start | bytes 98312 | tf_op jit(solution)/shard_map/ppermute | solution.py:113

commit v10 on v9

--- a/solution.py
+++ b/solution.py
@@ -107,14 +107,12 @@
 
 
 def head_sum(part, nhead):
-    my_index = lax.axis_index("head")
-    stride = 1
-    while stride < nhead:
-        other = lax.ppermute(part, "head", [(i, i ^ stride) for i in range(nhead)])
-        low = (my_index & stride) == 0
-        part = jnp.where(low, part + other, other + part)
-        stride *= 2
-    return part
+    copies = jnp.broadcast_to(part[None], (nhead,) + part.shape)
+    got = lax.all_to_all(copies, "head", 0, 0, tiled=True)
+    while got.shape[0] > 1:
+        half = got.shape[0] // 2
+        got = got[:half] + got[half:]
+    return got[0]
 
 
 def full_normalize(rows, gain_full):

time: 273 us -> 278 us (1.018)
  waiting for transfers between devices: 80.9 us -> 72.8 us
  starting transfers between devices: 22.4 us -> 29.7 us
    ppermute x4 -> x0, waiting for transfers between devices: 15.3 us -> none  [head_sum(): other = lax.ppermute(part, 'head', [(i, i ^ stride) for i in range(nhead)])]
    all_to_all x0 -> x2, starting transfers between devices: none -> 10.8 us  [head_sum(): got = lax.all_to_all(copies, 'head', 0, 0, tiled=True)]
    all_to_all x0 -> x2, waiting for transfers between devices: none -> 6.54 us  [head_sum(): got = lax.all_to_all(copies, 'head', 0, 0, tiled=True)]
    ppermute x4 -> x0, starting transfers between devices: 3.57 us -> none  [head_sum(): other = lax.ppermute(part, 'head', [(i, i ^ stride) for i in range(nhead)])]
  transfers between devices with their start and end apart: 7 -> 5, of which waited for: 7 -> 5; matrix products, arithmetic and copies ran while one was open for 3% -> 3% of each run, Pallas kernels for 0% -> 0%
where the time goes in v10:
time: 278 us; the launch traced here: 274 us
  blocking collectives  116 us (42%)
  waiting for transfers between devices  72.8 us (26%)
  starting transfers between devices  29.7 us (11%)
  local copies, waits for them, and re-layouts  26 us (9%)
  other arithmetic  15.9 us (6%)
  matrix products  13.4 us (5%)
    all_to_all x1, blocking collectives, on_device(): got = lax.all_to_all(payload, 'seq', 0, 0, tiled=True)  63 us
    all_to_all x2, blocking collectives, gather_rows(): return lax.all_to_all(copies, 'seq', 0, 0, tiled=True)  52.6 us
    all_to_all x2, waiting for transfers between devices, gather_rows(): return lax.all_to_all(copies, 'seq', 0, 0, tiled=True)  49.1 us
    all_to_all x1, waiting for transfers between devices, on_device(): packed = lax.all_to_all(packed, 'seq', 0, 0, tiled=True)  17.1 us
    all_to_all x2, starting transfers between devices, gather_rows(): return lax.all_to_all(copies, 'seq', 0, 0, tiled=True)  12.6 us
    all_to_all x2, starting transfers between devices, head_sum(): got = lax.all_to_all(copies, 'head', 0, 0, tiled=True)  10.8 us
    all_to_all x2, waiting for transfers between devices, head_sum(): got = lax.all_to_all(copies, 'head', 0, 0, tiled=True)  6.54 us
    all_to_all x1, starting transfers between devices, on_device(): packed = lax.all_to_all(packed, 'seq', 0, 0, tiled=True)  6.28 us
  transfers between devices with their start and end apart: 5, of which 5 were waited for; matrix products, arithmetic and copies ran while one was open for 3% of the time, Pallas kernels for 0%

profile of v10, /device:TPU:4, one launch (start us, length us, event | category | flops | bytes accessed | tf_op | source)
XLA Modules:
  0.0 273.9 jit_solution(16139229058576724093)
XLA Ops:
  0.0 0.7 fusion.85
  0.7 0.7 fusion.81
  1.4 0.7 subtract_convert_fusion.1
  2.1 1.4 copy.230
  3.5 2.1 reshape.359
  5.6 1.2 copy.231
  7.5 0.7 pad_maximum_fusion
  8.2 63.0 %all_to_all.40 = bf16[64,256,64]{1,2,0:T(8,128)(2,1)S(1)} all-to-all(bf16[64,256,64]{1,2,0:T(8,128)(2,1)S(1)} %pad_maximum_fusion), channel_id=1, replica_groups=mesh['seq'=64,'head'=4] {'seq'}, dimensions={0} | all-to-all | bytes 4194304 | tf_op jit(solution)/shard_map/all_to_all | solution.py:220
  72.2 0.8 fusion.28
  73.1 1.0 broadcast_in_dim.175
  74.1 6.1 %all-to-all-start.1 = ((bf16[64,128,48]{1,2,0:T(8,128)(2,1)}), bf16[64,128,48]{1,2,0:T(8,128)(2,1)S(1)}, u32[]{:S(2)}, u32[]{:S(2)}) async-start(bf16[64,128,48]{1,2,0:T(8,128)(2,1)} %broadcast_in_dim.175), calls=%async_computation.1 | async-start | bytes 1572864 | tf_op jit(solution)/shard_map/all_to_all | solution.py:101
  80.2 0.7 gather_fusion
  81.4 21.4 %all-to-all-done.1 = bf16[64,128,48]{1,2,0:T(8,128)(2,1)S(1)} async-done(((bf16[64,128,48]{1,2,0:T(8,128)(2,1)}), bf16[64,128,48]{1,2,0:T(8,128)(2,1)S(1)}, u32[]{:S(2)}, u32[]{:S(2)}) %all-to-all-start.1) | async-done | bytes 786464 | tf_op jit(solution)/shard_map/all_to_all | solution.py:101
  102.9 0.9 fusion.88
  103.8 1.1 copy.235
  105.6 4.5 %fusion.89 = (f32[2,32,8]{0,2,1:T(8,128)S(1)}, f32[2,32,64,8]{2,0,3,1:T(2,128)S(1)}) fusion(f32[8]{0:T(128)S(1)} %copy-done.7, f32[2,32,64]{2,0,1:T(2,128)S(1)} %subtract_convert_fusion, bf16[2,32,8,128]{3,2,0,1:T(8,128)(2,1)S(1)} %select_bitcast_fusion, pred[32,64]{1,0:T(8,128)(4,1)S(1)} %compare_and_fusion, bf16[32,64,1024]{2,1,0:T(8,128)(2,1)} %param.17), kind=kOutput, calls=%fused_computation.154 | convolution fusion | flops 8551936 | bytes 4476960 | tf_op jit(solution)/shard_map/sbhe,bthe->sbth/dot_general | solution.py:38
  112.5 3.4 %fusion.22 = f32[2,32,8,128]{3,0,2,1:T(2,128)S(1)} fusion(f32[2,32,64,8]{2,0,3,1:T(2,128)S(1)} %get-tuple-element.38, pred[32,64]{1,0:T(8,128)(4,1)S(1)} %compare_and_fusion, f32[2,32,8]{0,2,1:T(8,128)S(1)} %copy.241, bf16[32,64,1024]{2,1,0:T(8,128)(2,1)} %param.18), kind=kOutput, calls=%fused_computation.29 | convolution fusion | flops 8486912 | bytes 4591616 | tf_op jit(solution)/shard_map/sbth,bthe->sbhe/dot_general | solution.py:62
  117.6 0.7 copy.245
  118.3 1.3 copy.247
  119.6 1.1 copy.246
  120.8 1.0 broadcast_add_fusion
  121.8 1.1 maximum_bitcast_fusion
  122.9 0.9 pad_maximum_fusion.1
  123.8 6.3 %all-to-all-start.2 = ((f32[64,3,8,128]{3,2,1,0:T(8,128)}), f32[64,3,8,128]{3,2,1,0:T(8,128)S(1)}, u32[]{:S(2)}, u32[]{:S(2)}) async-start(f32[64,3,8,128]{3,2,1,0:T(8,128)} %pad_maximum_fusion.1), calls=%async_computation.2 | async-start | bytes 1572864 | tf_op jit(solution)/shard_map/all_to_all | solution.py:258
  130.2 2.1 constant_dynamic-slice_fusion
  132.2 1.1 copy.268
  133.3 1.1 copy.269
  134.4 1.4 fusion.48
  135.9 17.1 %all-to-all-done.2 = f32[64,3,8,128]{3,2,1,0:T(8,128)S(1)} async-done(((f32[64,3,8,128]{3,2,1,0:T(8,128)}), f32[64,3,8,128]{3,2,1,0:T(8,128)S(1)}, u32[]{:S(2)}, u32[]{:S(2)}) %all-to-all-start.2) | async-done | bytes 786464 | tf_op jit(solution)/shard_map/all_to_all | solution.py:258
  153.1 0.8 fusion.51
  153.8 1.4 copy.249
  155.2 0.7 fusion.83
  155.9 1.3 add_select_fusion
  157.2 0.8 copy.250
  158.2 0.8 copy.251
  158.9 0.8 copy.254
  160.1 18.1 %all_to_all.41 = bf16[64,2,1024]{2,1,0:T(2,128)(2,1)S(1)} all-to-all(bf16[64,2,1024]{2,1,0:T(2,128)(2,1)S(1)} %broadcast_in_dim.189), channel_id=1, replica_groups=mesh['seq'=64,'head'=4] {'seq'}, dimensions={0} | all-to-all | bytes 524288 | tf_op jit(solution)/shard_map/all_to_all | solution.py:101
  178.3 1.1 fusion.90
  180.0 4.8 %all-to-all-start.4 = ((f32[4,128,64]{1,2,0:T(8,128)}), f32[4,128,64]{1,2,0:T(8,128)S(1)}, u32[]{:S(2)}, u32[]{:S(2)}) async-start(f32[4,128,64]{1,2,0:T(8,128)} %broadcast_in_dim.190), calls=%async_computation.4 | async-start | bytes 262144 | tf_op jit(solution)/shard_map/all_to_all | solution.py:111
  184.9 3.2 %all-to-all-done.4 = f32[4,128,64]{1,2,0:T(8,128)S(1)} async-done(((f32[4,128,64]{1,2,0:T(8,128)}), f32[4,128,64]{1,2,0:T(8,128)S(1)}, u32[]{:S(2)}, u32[]{:S(2)}) %all-to-all-start.4) | async-done | bytes 131104 | tf_op jit(solution)/shard_map/all_to_all | solution.py:111
  188.1 1.3 broadcast_in_dim.192
  189.4 6.5 %all-to-all-start.5 = ((bf16[64,128,64]{1,2,0:T(8,128)(2,1)}), bf16[64,128,64]{1,2,0:T(8,128)(2,1)}, u32[]{:S(2)}, u32[]{:S(2)}) async-start(bf16[64,128,64]{1,2,0:T(8,128)(2,1)} %broadcast_in_dim.192), calls=%async_computation.5 | async-start | bytes 2097152 | tf_op jit(solution)/shard_map/all_to_all | solution.py:101
  196.0 27.7 %all-to-all-done.5 = bf16[64,128,64]{1,2,0:T(8,128)(2,1)} async-done(((bf16[64,128,64]{1,2,0:T(8,128)(2,1)}), bf16[64,128,64]{1,2,0:T(8,128)(2,1)}, u32[]{:S(2)}, u32[]{:S(2)}) %all-to-all-start.5) | async-done | bytes 1048608 | tf_op jit(solution)/shard_map/all_to_all | solution.py:101
  223.7 1.8 convert_reduce_fusion
  225.5 2.5 fusion.57
  228.3 34.5 %all_to_all.42 = bf16[64,128,64]{1,2,0:T(8,128)(2,1)S(1)} all-to-all(bf16[64,128,64]{1,2,0:T(8,128)(2,1)S(1)} %broadcast_in_dim.193), channel_id=1, replica_groups=mesh['seq'=64,'head'=4] {'seq'}, dimensions={0} | all-to-all | bytes 2097152 | tf_op jit(solution)/shard_map/all_to_all | solution.py:101
  263.7 6.0 %all-to-all-start.7 = ((f32[4,128,64]{1,2,0:T(8,128)}), f32[4,128,64]{1,2,0:T(8,128)S(1)}, u32[]{:S(2)}, u32[]{:S(2)}) async-start(f32[4,128,64]{1,2,0:T(8,128)} %broadcast_in_dim.194), calls=%async_computation.7 | async-start | bytes 262144 | tf_op jit(solution)/shard_map/all_to_all | solution.py:111
  269.8 3.3 %all-to-all-done.7 = f32[4,128,64]{1,2,0:T(8,128)S(1)} async-done(((f32[4,128,64]{1,2,0:T(8,128)}), f32[4,128,64]{1,2,0:T(8,128)S(1)}, u32[]{:S(2)}, u32[]{:S(2)}) %all-to-all-start.7) | async-done | bytes 131104 | tf_op jit(solution)/shard_map/all_to_all | solution.py:111
  (81 shorter events, 10.4 us)
Async XLA Ops:
  0.0 262.8 %copy-start = (bf16[64,4096]{1,0:T(8,128)(2,1)S(1)}, bf16[64,4096]{1,0:T(8,128)(2,1)}, u32[]{:S(2)}) copy-start(bf16[64,4096]{1,0:T(8,128)(2,1)} %param.25) | copy-start | bytes 1572868
  3.5 3.3 %copy-start.2 = (bf16[2,64,64]{2,1,0:T(8,128)(2,1)S(1)}, bf16[2,64,64]{2,1,0:T(8,128)(2,1)}, u32[]{:S(2)}) copy-start(bf16[2,64,64]{2,1,0:T(8,128)(2,1)} %param.13) | copy-start | bytes 49156
  73.1 7.1 %copy-start.5 = (s32[32]{0:T(128)S(1)}, s32[32]{0:T(128)}, u32[]{:S(2)}) copy-start(s32[32]{0:T(128)} %param.15) | copy-start | bytes 388
  73.1 7.1 %copy-start.1 = (s32[64]{0:T(128)S(1)}, s32[64]{0:T(128)}, u32[]{:S(2)}) copy-start(s32[64]{0:T(128)} %param.14) | copy-start | bytes 772
  73.1 7.9 %copy-start.6 = (s32[32]{0:T(128)S(1)}, s32[32]{0:T(128)}, u32[]{:S(2)}) copy-start(s32[32]{0:T(128)} %param.16) | copy-start | bytes 388
  74.1 28.8 %all-to-all-start.1 = ((bf16[64,128,48]{1,2,0:T(8,128)(2,1)}), bf16[64,128,48]{1,2,0:T(8,128)(2,1)S(1)}, u32[]{:S(2)}, u32[]{:S(2)}) async-start(bf16[64,128,48]{1,2,0:T(8,128)(2,1)} %broadcast_in_dim.175), calls=%async_computation.1 | async-start | bytes 1572864 | tf_op jit(solution)/shard_map/all_to_all | solution.py:101
  80.2 25.5 %copy-start.7 = (f32[8]{0:T(128)S(1)}, f32[8]{0:T(128)}, u32[]{:S(2)}) copy-start(f32[8]{0:T(128)} %param.19) | copy-start | bytes 100
  123.8 29.2 %all-to-all-start.2 = ((f32[64,3,8,128]{3,2,1,0:T(8,128)}), f32[64,3,8,128]{3,2,1,0:T(8,128)S(1)}, u32[]{:S(2)}, u32[]{:S(2)}) async-start(f32[64,3,8,128]{3,2,1,0:T(8,128)} %pad_maximum_fusion.1), calls=%async_computation.2 | async-start | bytes 1572864 | tf_op jit(solution)/shard_map/all_to_all | solution.py:258
  130.2 25.8 %copy-start.3 = (f32[8]{0:T(128)}, f32[8]{0:T(128)S(1)}, u32[]{:S(2)}) copy-start(f32[8]{0:T(128)S(1)} %get-tuple-element.32) | copy-start | bytes 100
  130.2 25.7 %copy-start.4 = (f32[8]{0:T(128)}, f32[8]{0:T(128)S(1)}, u32[]{:S(2)}) copy-start(f32[8]{0:T(128)S(1)} %get-tuple-element.33) | copy-start | bytes 100
  180.0 8.1 %all-to-all-start.4 = ((f32[4,128,64]{1,2,0:T(8,128)}), f32[4,128,64]{1,2,0:T(8,128)S(1)}, u32[]{:S(2)}, u32[]{:S(2)}) async-start(f32[4,128,64]{1,2,0:T(8,128)} %broadcast_in_dim.190), calls=%async_computation.4 | async-start | bytes 262144 | tf_op jit(solution)/shard_map/all_to_all | solution.py:111
  189.4 34.3 %all-to-all-start.5 = ((bf16[64,128,64]{1,2,0:T(8,128)(2,1)}), bf16[64,128,64]{1,2,0:T(8,128)(2,1)}, u32[]{:S(2)}, u32[]{:S(2)}) async-start(bf16[64,128,64]{1,2,0:T(8,128)(2,1)} %broadcast_in_dim.192), calls=%async_computation.5 | async-start | bytes 2097152 | tf_op jit(solution)/shard_map/all_to_all | solution.py:101
  263.7 9.4 %all-to-all-start.7 = ((f32[4,128,64]{1,2,0:T(8,128)}), f32[4,128,64]{1,2,0:T(8,128)S(1)}, u32[]{:S(2)}, u32[]{:S(2)}) async-start(f32[4,128,64]{1,2,0:T(8,128)} %broadcast_in_dim.194), calls=%async_computation.7 | async-start | bytes 262144 | tf_op jit(solution)/shard_map/all_to_all | solution.py:111

commit v11 on v9

--- a/solution.py
+++ b/solution.py
@@ -207,7 +207,10 @@
         return jnp.pad(block, [(0, 0)] * (block.ndim - 1) + [(0, pad_width - block.shape[-1])])
 
     gain_cols = jnp.concatenate(gain_parts, axis=0).T
-    qkv_block = jnp.swapaxes(w_qkv.reshape(local_width, nseq, qkv_chunk), 0, 1)
+    split = head_width // nseq
+    qkv_block = jnp.transpose(w_qkv.reshape(local_width, 3, nseq, split), (2, 0, 1, 3)).reshape(
+        nseq, local_width, qkv_chunk
+    )
     qkv_block = jnp.concatenate(
         [qkv_block, jnp.broadcast_to(gain_cols[None], (nseq,) + gain_cols.shape)], axis=2
     )
@@ -228,11 +231,14 @@
     gains = (pieces[0:2] + pieces[2:4]) + pieces[4:6]
     normed = full_normalize(gathered, gains[0])
     qkv_part = jnp.dot(normed, qkv_cols, preferred_element_type=jnp.float32).astype(jnp.bfloat16)
-    joined = gather_cols(qkv_part, nseq)
-    all_queries = joined[:, :head_width].reshape(nsteps, requests, nheads, head_size)
-    new_keys = joined[:, head_width : 2 * head_width].reshape(nsteps, requests, nheads, head_size)
-    new_values = joined[:, 2 * head_width :].reshape(nsteps, requests, nheads, head_size)
-
+    all_queries = gather_cols(qkv_part[:, :split], nseq).reshape(nsteps, requests, nheads, head_size)
+    kv_part = qkv_part[:, split:].astype(jnp.float32)
+    own_rows = rows // nseq
+    req_blocks = requests // own_rows
+    kv_by_block = kv_part.reshape(nsteps, req_blocks, own_rows, 2 * split)
+    kv_dest = jnp.take(kv_by_block, jnp.arange(nseq) % req_blocks, axis=1)
+    kv_lanes = nsteps * own_rows * 2 * split // nheads
+    kv_dest = jnp.swapaxes(kv_dest, 0, 1).reshape(nseq, nheads, kv_lanes)
     carry_state = (
         jnp.full((nsteps, requests, nheads), floor_score, jnp.float32),
         jnp.zeros((nsteps, requests, nheads), jnp.float32),
@@ -245,12 +251,12 @@
 
     joined_state = tuple(part.reshape((rows,) + part.shape[2:]) for part in final_state)
     run_max, run_sum, run_out = joined_state
-    own_rows = rows // nseq
     stats = jnp.concatenate(
         [
             jnp.swapaxes(run_max.reshape(nseq, own_rows, nheads), 1, 2),
             jnp.swapaxes(run_sum.reshape(nseq, own_rows, nheads), 1, 2),
-            jnp.zeros((nseq, nheads, head_size - 2 * own_rows), jnp.float32),
+            kv_dest,
+            jnp.zeros((nseq, nheads, head_size - 2 * own_rows - kv_lanes), jnp.float32),
         ],
         axis=2,
     )
@@ -267,14 +273,16 @@
     top_out = jnp.sum(part_out * rescale[:, :, :, None], axis=0)
     first_row = lax.axis_index("seq") * own_rows
     my_step = first_row // requests
-    pick = lambda a: lax.dynamic_slice_in_dim(a.reshape(rows, nheads, head_size), first_row, own_rows, 0)
-    my_queries = pick(all_queries)
-    my_keys = []
-    my_values = []
-    for earlier in range(nsteps):
-        shifted = first_row - (my_step - earlier) * requests
-        my_keys.append(lax.dynamic_slice_in_dim(new_keys.reshape(rows, nheads, head_size), shifted, own_rows, 0))
-        my_values.append(lax.dynamic_slice_in_dim(new_values.reshape(rows, nheads, head_size), shifted, own_rows, 0))
+    my_queries = lax.dynamic_slice_in_dim(
+        all_queries.reshape(rows, nheads, head_size), first_row, own_rows, 0
+    )
+    kv_got = packed[:, own_rows, :, 2 * own_rows : 2 * own_rows + kv_lanes]
+    kv_got = kv_got.reshape(nseq, nsteps, own_rows, 2 * split).astype(jnp.bfloat16)
+    kv_got = jnp.transpose(kv_got, (1, 2, 0, 3))
+    key_rows = kv_got[..., :split].reshape(nsteps, own_rows, nheads, head_size)
+    value_rows = kv_got[..., split:].reshape(nsteps, own_rows, nheads, head_size)
+    my_keys = [key_rows[earlier] for earlier in range(nsteps)]
+    my_values = [value_rows[earlier] for earlier in range(nsteps)]
     mine = attend_rows(
         (top_max, top_sum, top_out), my_queries, my_keys, my_values, alibi_slopes, my_step
     )

time: 273 us -> 276 us (1.011)
  blocking collectives: 116 us -> 52.6 us
  waiting for transfers between devices: 80.9 us -> 121 us
  starting transfers between devices: 22.4 us -> 34.4 us
  local copies, waits for them, and re-layouts: 25.2 us -> 32 us
  other arithmetic: 13.4 us -> 19.8 us
    all_to_all x1 -> x0, blocking collectives: 63 us -> none  [on_device(): got = lax.all_to_all(payload, 'seq', 0, 0, tiled=True)]
    all_to_all x0 -> x1, waiting for transfers between devices: none -> 49.4 us  [on_device(): got = lax.all_to_all(payload, 'seq', 0, 0, tiled=True)]
    all_to_all x0 -> x1, starting transfers between devices: none -> 12.2 us  [on_device(): got = lax.all_to_all(payload, 'seq', 0, 0, tiled=True)]
    all_to_all x2, waiting for transfers between devices: 48.6 us -> 37.5 us  [gather_rows(): return lax.all_to_all(copies, 'seq', 0, 0, tiled=True)]
  transfers between devices with their start and end apart: 7 -> 8, of which waited for: 7 -> 8; matrix products, arithmetic and copies ran while one was open for 3% -> 3% of each run, Pallas kernels for 0% -> 0%
where the time goes in v11:
time: 276 us; the launch traced here: 275 us
  waiting for transfers between devices  121 us (44%)
  blocking collectives  52.6 us (19%)
  starting transfers between devices  34.4 us (12%)
  local copies, waits for them, and re-layouts  32 us (12%)
  other arithmetic  19.8 us (7%)
  matrix products  14.8 us (5%)
    all_to_all x2, blocking collectives, gather_rows(): return lax.all_to_all(copies, 'seq', 0, 0, tiled=True)  52.6 us
    all_to_all x1, waiting for transfers between devices, on_device(): got = lax.all_to_all(payload, 'seq', 0, 0, tiled=True)  49.4 us
    all_to_all x2, waiting for transfers between devices, gather_rows(): return lax.all_to_all(copies, 'seq', 0, 0, tiled=True)  37.5 us
    all_to_all x1, waiting for transfers between devices, on_device(): packed = lax.all_to_all(packed, 'seq', 0, 0, tiled=True)  18.8 us
    ppermute x4, waiting for transfers between devices, head_sum(): other = lax.ppermute(part, 'head', [(i, i ^ stride) for i in range(nhead)])  15.3 us
    all_to_all x2, starting transfers between devices, gather_rows(): return lax.all_to_all(copies, 'seq', 0, 0, tiled=True)  12.6 us
    all_to_all x1, starting transfers between devices, on_device(): got = lax.all_to_all(payload, 'seq', 0, 0, tiled=True)  12.2 us
    all_to_all x1, starting transfers between devices, on_device(): packed = lax.all_to_all(packed, 'seq', 0, 0, tiled=True)  6.03 us
  transfers between devices with their start and end apart: 8, of which 8 were waited for; matrix products, arithmetic and copies ran while one was open for 3% of the time, Pallas kernels for 0%

profile of v11, /device:TPU:4, one launch (start us, length us, event | category | flops | bytes accessed | tf_op | source)
XLA Modules:
  0.0 275.0 jit_solution(14963512416521583787)
XLA Ops:
  2.1 1.4 copy.277
  3.8 2.1 reshape.467
  5.8 1.2 copy.279
  7.7 2.1 pad_maximum_fusion
  9.7 12.2 %all-to-all-start = ((bf16[64,256,64]{1,2,0:T(8,128)(2,1)}), bf16[64,256,64]{1,2,0:T(8,128)(2,1)S(1)}, u32[]{:S(2)}, u32[]{:S(2)}) async-start(bf16[64,256,64]{1,2,0:T(8,128)(2,1)} %pad_maximum_fusion), calls=%async_computation | async-start | bytes 4194304 | tf_op jit(solution)/shard_map/all_to_all | solution.py:225
  23.8 49.4 %all-to-all-done = bf16[64,256,64]{1,2,0:T(8,128)(2,1)S(1)} async-done(((bf16[64,256,64]{1,2,0:T(8,128)(2,1)}), bf16[64,256,64]{1,2,0:T(8,128)(2,1)S(1)}, u32[]{:S(2)}, u32[]{:S(2)}) %all-to-all-start) | async-done | bytes 2097184 | tf_op jit(solution)/shard_map/all_to_all | solution.py:225
  74.6 0.8 fusion.28
  76.2 6.1 %all-to-all-start.1 = ((bf16[64,128,16]{1,2,0:T(8,128)(2,1)}), bf16[64,128,16]{1,2,0:T(8,128)(2,1)S(1)}, u32[]{:S(2)}, u32[]{:S(2)}) async-start(bf16[64,128,16]{1,2,0:T(8,128)(2,1)} %broadcast_in_dim.166), calls=%async_computation.1 | async-start | bytes 524288 | tf_op jit(solution)/shard_map/all_to_all | solution.py:101
  83.4 0.8 copy.296
  84.2 9.9 %all-to-all-done.1 = bf16[64,128,16]{1,2,0:T(8,128)(2,1)S(1)} async-done(((bf16[64,128,16]{1,2,0:T(8,128)(2,1)}), bf16[64,128,16]{1,2,0:T(8,128)(2,1)S(1)}, u32[]{:S(2)}, u32[]{:S(2)}) %all-to-all-start.1) | async-done | bytes 262176 | tf_op jit(solution)/shard_map/all_to_all | solution.py:101
  94.3 1.0 copy.281
  95.3 1.6 gather_fusion.1
  97.0 4.5 %fusion.92 = (f32[2,32,8]{0,2,1:T(8,128)S(1)}, f32[2,32,64,8]{2,0,3,1:T(2,128)S(1)}) fusion(f32[8]{0:T(128)S(1)} %copy-done.14, f32[2,32,64]{2,0,1:T(2,128)S(1)} %subtract_convert_fusion, bf16[2,32,8,128]{3,2,0,1:T(8,128)(2,1)S(1)} %select_bitcast_fusion, pred[32,64]{1,0:T(8,128)(4,1)S(1)} %compare_and_fusion, bf16[32,64,1024]{2,1,0:T(8,128)(2,1)} %param.17), kind=kOutput, calls=%fused_computation.173 | convolution fusion | flops 8551936 | bytes 4476960 | tf_op jit(solution)/shard_map/sbhe,bthe->sbth/dot_general | solution.py:38
  103.4 0.8 select_bitcast_fusion.1
  104.4 2.0 fusion.70
  106.4 3.4 %fusion.22 = f32[2,32,8,128]{3,0,2,1:T(2,128)S(1)} fusion(f32[2,32,64,8]{2,0,3,1:T(2,128)S(1)} %get-tuple-element.35, pred[32,64]{1,0:T(8,128)(4,1)} %copy-done.8, f32[2,32,8]{0,2,1:T(8,128)S(1)} %copy.287, bf16[32,64,1024]{2,1,0:T(8,128)(2,1)} %param.18), kind=kOutput, calls=%fused_computation.30 | convolution fusion | flops 8486912 | bytes 4591616 | tf_op jit(solution)/shard_map/sbth,bthe->sbhe/dot_general | solution.py:62
  110.7 1.6 copy.290
  112.3 1.5 fusion.29
  113.8 1.4 copy.291
  115.2 2.0 copy.295
  117.2 1.1 copy.294
  118.6 1.2 maximum_bitcast_fusion
  119.8 0.9 pad_maximum_fusion.1
  120.8 6.0 %all-to-all-start.2 = ((f32[64,3,8,128]{3,2,1,0:T(8,128)}), f32[64,3,8,128]{3,2,1,0:T(8,128)S(1)}, u32[]{:S(2)}, u32[]{:S(2)}) async-start(f32[64,3,8,128]{3,2,1,0:T(8,128)} %pad_maximum_fusion.1), calls=%async_computation.2 | async-start | bytes 1572864 | tf_op jit(solution)/shard_map/all_to_all | solution.py:266
  127.4 1.8 constant_dynamic-slice_fusion
  129.2 1.7 copy.317
  130.9 18.8 %all-to-all-done.2 = f32[64,3,8,128]{3,2,1,0:T(8,128)S(1)} async-done(((f32[64,3,8,128]{3,2,1,0:T(8,128)}), f32[64,3,8,128]{3,2,1,0:T(8,128)S(1)}, u32[]{:S(2)}, u32[]{:S(2)}) %all-to-all-start.2) | async-done | bytes 786464 | tf_op jit(solution)/shard_map/all_to_all | solution.py:266
  149.7 1.4 fusion.49
  151.1 2.0 copy.298
  153.9 0.8 slice_convert_fusion.3
  155.0 0.8 fusion.72
  156.0 0.8 fusion.87
  156.7 0.8 add_select_fusion
  159.3 1.0 fusion.47
  161.2 18.1 %all_to_all.30 = bf16[64,2,1024]{2,1,0:T(2,128)(2,1)S(1)} all-to-all(bf16[64,2,1024]{2,1,0:T(2,128)(2,1)S(1)} %broadcast_in_dim.181), channel_id=1, replica_groups=mesh['seq'=64,'head'=4] {'seq'}, dimensions={0} | all-to-all | bytes 524288 | tf_op jit(solution)/shard_map/all_to_all | solution.py:101
  179.3 1.1 fusion.93
  180.5 1.3 collective-permute-start
  181.7 2.7 collective-permute-done
  185.0 4.9 %collective-permute-done.1 = f32[128,64]{0,1:T(8,128)S(1)} collective-permute-done((f32[128,64]{0,1:T(8,128)S(1)}, f32[128,64]{0,1:T(8,128)S(1)}, u32[]{:S(2)}, u32[]{:S(2)}) %collective-permute-start.1) | collective-permute-done | bytes 32800 | tf_op jit(solution)/shard_map/ppermute | solution.py:113
  189.9 1.3 broadcast_in_dim.182
  191.2 6.5 %all-to-all-start.4 = ((bf16[64,128,64]{1,2,0:T(8,128)(2,1)}), bf16[64,128,64]{1,2,0:T(8,128)(2,1)}, u32[]{:S(2)}, u32[]{:S(2)}) async-start(bf16[64,128,64]{1,2,0:T(8,128)(2,1)} %broadcast_in_dim.182), calls=%async_computation.4 | async-start | bytes 2097152 | tf_op jit(solution)/shard_map/all_to_all | solution.py:101
  197.8 27.7 %all-to-all-done.4 = bf16[64,128,64]{1,2,0:T(8,128)(2,1)} async-done(((bf16[64,128,64]{1,2,0:T(8,128)(2,1)}), bf16[64,128,64]{1,2,0:T(8,128)(2,1)}, u32[]{:S(2)}, u32[]{:S(2)}) %all-to-all-start.4) | async-done | bytes 1048608 | tf_op jit(solution)/shard_map/all_to_all | solution.py:101
  225.5 1.8 convert_reduce_fusion
  227.3 2.5 fusion.55
  230.0 34.5 %all_to_all.31 = bf16[64,128,64]{1,2,0:T(8,128)(2,1)S(1)} all-to-all(bf16[64,128,64]{1,2,0:T(8,128)(2,1)S(1)} %broadcast_in_dim.183), channel_id=1, replica_groups=mesh['seq'=64,'head'=4] {'seq'}, dimensions={0} | all-to-all | bytes 2097152 | tf_op jit(solution)/shard_map/all_to_all | solution.py:101
  264.9 1.3 collective-permute-start.2
  266.1 2.7 collective-permute-done.2
  269.4 4.9 %collective-permute-done.3 = f32[128,64]{0,1:T(8,128)S(1)} collective-permute-done((f32[128,64]{0,1:T(8,128)S(1)}, f32[128,64]{0,1:T(8,128)S(1)}, u32[]{:S(2)}, u32[]{:S(2)}) %collective-permute-start.3) | collective-permute-done | bytes 32800 | tf_op jit(solution)/shard_map/ppermute | solution.py:113
  (123 shorter events, 18.4 us)
Async XLA Ops:
  0.0 264.5 %copy-start = (bf16[64,4096]{1,0:T(8,128)(2,1)S(1)}, bf16[64,4096]{1,0:T(8,128)(2,1)}, u32[]{:S(2)}) copy-start(bf16[64,4096]{1,0:T(8,128)(2,1)} %param.25) | copy-start | bytes 1572868
  0.0 3.7 %copy-start.6 = (bf16[2,64,64]{2,1,0:T(8,128)(2,1)S(1)}, bf16[2,64,64]{2,1,0:T(8,128)(2,1)}, u32[]{:S(2)}) copy-start(bf16[2,64,64]{2,1,0:T(8,128)(2,1)} %param.13) | copy-start | bytes 49156
  9.7 12.3 %copy-start.11 = (s32[32]{0:T(128)S(1)}, s32[32]{0:T(128)}, u32[]{:S(2)}) copy-start(s32[32]{0:T(128)} %param.15) | copy-start | bytes 388
  9.7 12.3 %copy-start.1 = (s32[64]{0:T(128)S(1)}, s32[64]{0:T(128)}, u32[]{:S(2)}) copy-start(s32[64]{0:T(128)} %param.14) | copy-start | bytes 772
  9.7 13.6 %copy-start.13 = (s32[32]{0:T(128)S(1)}, s32[32]{0:T(128)}, u32[]{:S(2)}) copy-start(s32[32]{0:T(128)} %param.16) | copy-start | bytes 388
  9.7 63.4 %all-to-all-start = ((bf16[64,256,64]{1,2,0:T(8,128)(2,1)}), bf16[64,256,64]{1,2,0:T(8,128)(2,1)S(1)}, u32[]{:S(2)}, u32[]{:S(2)}) async-start(bf16[64,256,64]{1,2,0:T(8,128)(2,1)} %pad_maximum_fusion), calls=%async_computation | async-start | bytes 4194304 | tf_op jit(solution)/shard_map/all_to_all | solution.py:225
  22.0 74.9 %copy-start.10 = (pred[32]{0:T(512)(128)(4,1)}, pred[32]{0:T(512)(128)(4,1)S(1)}, u32[]{:S(2)}) copy-start(pred[32]{0:T(512)(128)(4,1)S(1)} %get-tuple-element.20) | copy-start | bytes 100
  22.0 73.3 %copy-start.9 = (s32[1024]{0:T(1024)}, s32[1024]{0:T(1024)S(1)}, u32[]{:S(2)}) copy-start(s32[1024]{0:T(1024)S(1)} %pad_clamp_fusion.1) | copy-start | bytes 12292
  23.5 73.5 %copy-start.8 = (pred[32,64]{1,0:T(8,128)(4,1)}, pred[32,64]{1,0:T(8,128)(4,1)S(1)}, u32[]{:S(2)}) copy-start(pred[32,64]{1,0:T(8,128)(4,1)S(1)} %compare_and_fusion) | copy-start | bytes 6148
  75.5 21.5 %copy-start.14 = (f32[8]{0:T(128)S(1)}, f32[8]{0:T(128)}, u32[]{:S(2)}) copy-start(f32[8]{0:T(128)} %param.19) | copy-start | bytes 100
  76.2 17.9 %all-to-all-start.1 = ((bf16[64,128,16]{1,2,0:T(8,128)(2,1)}), bf16[64,128,16]{1,2,0:T(8,128)(2,1)S(1)}, u32[]{:S(2)}, u32[]{:S(2)}) async-start(bf16[64,128,16]{1,2,0:T(8,128)(2,1)} %broadcast_in_dim.166), calls=%async_computation.1 | async-start | bytes 524288 | tf_op jit(solution)/shard_map/all_to_all | solution.py:101
  94.1 15.8 %copy-start.2 = (bf16[64,128,16]{1,2,0:T(8,128)(2,1)}, bf16[64,128,16]{1,2,0:T(8,128)(2,1)S(1)}, u32[]{:S(2)}) copy-start(bf16[64,128,16]{1,2,0:T(8,128)(2,1)S(1)} %all-to-all-done.1) | copy-start | bytes 786436
  102.0 0.6 copy-start.7
  106.4 3.6 %copy-start.12 = (s32[32]{0:T(128)S(1)}, s32[32]{0:T(128)}, u32[]{:S(2)}) copy-start(s32[32]{0:T(128)} %param.15) | copy-start | bytes 388
  110.0 8.6 %copy-start.3 = (f32[64,8,16]{2,1,0:T(8,128)S(1)}, f32[64,8,16]{2,1,0:T(8,128)}, u32[]{:S(2)}) copy-start(f32[64,8,16]{2,1,0:T(8,128)} %copy.296) | copy-start | bytes 98308
  118.6 8.3 %copy-start.15 = (f32[8]{0:T(128)S(1)}, f32[8]{0:T(128)}, u32[]{:S(2)}) copy-start(f32[8]{0:T(128)} %param.19) | copy-start | bytes 100
  120.8 28.9 %all-to-all-start.2 = ((f32[64,3,8,128]{3,2,1,0:T(8,128)}), f32[64,3,8,128]{3,2,1,0:T(8,128)S(1)}, u32[]{:S(2)}, u32[]{:S(2)}) async-start(f32[64,3,8,128]{3,2,1,0:T(8,128)} %pad_maximum_fusion.1), calls=%async_computation.2 | async-start | bytes 1572864 | tf_op jit(solution)/shard_map/all_to_all | solution.py:266
  149.7 1.4 copy-start.4
  179.2 18.5 %copy-start.5 = (f32[4096]{0:T(1024)S(1)}, f32[4096]{0:T(1024)}, u32[]{:S(2)}) copy-start(f32[4096]{0:T(1024)} %get-tuple-element.9) | copy-start | bytes 49156
  180.5 4.0 %collective-permute-start = (f32[128,64]{0,1:T(8,128)S(1)}, f32[128,64]{0,1:T(8,128)S(1)}, u32[]{:S(2)}, u32[]{:S(2)}) collective-permute-start(f32[128,64]{0,1:T(8,128)S(1)} %fusion.93), channel_id=1, source_target_pairs={{0,1},{1,0},{2,3},{3,2},{4,5},{5,4},{6,7},{7,6},{8,9},{9,8},{10,11... | collective-permute-start | bytes 98312 | tf_op jit(solution)/shard_map/ppermute | solution.py:113
  184.5 5.4 %collective-permute-start.1 = (f32[128,64]{0,1:T(8,128)S(1)}, f32[128,64]{0,1:T(8,128)S(1)}, u32[]{:S(2)}, u32[]{:S(2)}) collective-permute-start(f32[128,64]{0,1:T(8,128)S(1)} %add.192), channel_id=1, source_target_pairs={{0,2},{1,3},{2,0},{3,1},{4,6},{5,7},{6,4},{7,5},{8,10},{9,11},{10,... | collective-permute-start | bytes 98312 | tf_op jit(solution)/shard_map/ppermute | solution.py:113
  191.2 34.3 %all-to-all-start.4 = ((bf16[64,128,64]{1,2,0:T(8,128)(2,1)}), bf16[64,128,64]{1,2,0:T(8,128)(2,1)}, u32[]{:S(2)}, u32[]{:S(2)}) async-start(bf16[64,128,64]{1,2,0:T(8,128)(2,1)} %broadcast_in_dim.182), calls=%async_computation.4 | async-start | bytes 2097152 | tf_op jit(solution)/shard_map/all_to_all | solution.py:101
  264.9 4.0 %collective-permute-start.2 = (f32[128,64]{0,1:T(8,128)S(1)}, f32[128,64]{0,1:T(8,128)S(1)}, u32[]{:S(2)}, u32[]{:S(2)}) collective-permute-start(f32[128,64]{0,1:T(8,128)S(1)} %fusion.94), channel_id=1, source_target_pairs={{0,1},{1,0},{2,3},{3,2},{4,5},{5,4},{6,7},{7,6},{8,9},{9,8},{10,11... | collective-permute-start | bytes 98312 | tf_op jit(solution)/shard_map/ppermute | solution.py:113
  268.9 5.4 %collective-permute-start.3 = (f32[128,64]{0,1:T(8,128)S(1)}, f32[128,64]{0,1:T(8,128)S(1)}, u32[]{:S(2)}, u32[]{:S(2)}) collective-permute-start(f32[128,64]{0,1:T(8,128)S(1)} %add.196), channel_id=1, source_target_pairs={{0,2},{1,3},{2,0},{3,1},{4,6},{5,7},{6,4},{7,5},{8,10},{9,11},{10,... | collective-permute-start | bytes 98312 | tf_op jit(solution)/shard_map/ppermute | solution.py:113

commit v12 on v11

--- a/solution.py
+++ b/solution.py
@@ -237,8 +237,10 @@
     req_blocks = requests // own_rows
     kv_by_block = kv_part.reshape(nsteps, req_blocks, own_rows, 2 * split)
     kv_dest = jnp.take(kv_by_block, jnp.arange(nseq) % req_blocks, axis=1)
-    kv_lanes = nsteps * own_rows * 2 * split // nheads
-    kv_dest = jnp.swapaxes(kv_dest, 0, 1).reshape(nseq, nheads, kv_lanes)
+    kv_got = lax.all_to_all(jnp.swapaxes(kv_dest, 0, 1).astype(jnp.bfloat16), "seq", 0, 0, tiled=True)
+    kv_got = jnp.transpose(kv_got, (1, 2, 0, 3))
+    key_rows = kv_got[..., :split].reshape(nsteps, own_rows, nheads, head_size)
+    value_rows = kv_got[..., split:].reshape(nsteps, own_rows, nheads, head_size)
     carry_state = (
         jnp.full((nsteps, requests, nheads), floor_score, jnp.float32),
         jnp.zeros((nsteps, requests, nheads), jnp.float32),
@@ -255,8 +257,7 @@
         [
             jnp.swapaxes(run_max.reshape(nseq, own_rows, nheads), 1, 2),
             jnp.swapaxes(run_sum.reshape(nseq, own_rows, nheads), 1, 2),
-            kv_dest,
-            jnp.zeros((nseq, nheads, head_size - 2 * own_rows - kv_lanes), jnp.float32),
+            jnp.zeros((nseq, nheads, head_size - 2 * own_rows), jnp.float32),
         ],
         axis=2,
     )
@@ -276,11 +277,6 @@
     my_queries = lax.dynamic_slice_in_dim(
         all_queries.reshape(rows, nheads, head_size), first_row, own_rows, 0
     )
-    kv_got = packed[:, own_rows, :, 2 * own_rows : 2 * own_rows + kv_lanes]
-    kv_got = kv_got.reshape(nseq, nsteps, own_rows, 2 * split).astype(jnp.bfloat16)
-    kv_got = jnp.transpose(kv_got, (1, 2, 0, 3))
-    key_rows = kv_got[..., :split].reshape(nsteps, own_rows, nheads, head_size)
-    value_rows = kv_got[..., split:].reshape(nsteps, own_rows, nheads, head_size)
     my_keys = [key_rows[earlier] for earlier in range(nsteps)]
     my_values = [value_rows[earlier] for earlier in range(nsteps)]
     mine = attend_rows(

time: 276 us -> 274 us (level)
  starting transfers between devices: 34.4 us -> 44.8 us
  local copies, waits for them, and re-layouts: 32 us -> 26 us
  other arithmetic: 19.8 us -> 14.9 us
    all_to_all x0 -> x1, starting transfers between devices: none -> 6.47 us  [on_device(): lax.all_to_all(jnp.swapaxes(kv_dest, 0, 1).astype(jnp.bfloat16), 'seq', 0...]
    all_to_all x1, starting transfers between devices: 6.03 us -> 10.1 us  [on_device(): packed = lax.all_to_all(packed, 'seq', 0, 0, tiled=True)]
  transfers between devices with their start and end apart: 8 -> 9, of which waited for: 8 -> 8; matrix products, arithmetic and copies ran while one was open for 3% -> 11% of each run, Pallas kernels for 0% -> 0%
where the time goes in v12:
time: 274 us; the launch traced here: 273 us
  waiting for transfers between devices  120 us (44%)
  blocking collectives  52.6 us (19%)
  starting transfers between devices  44.8 us (16%)
  local copies, waits for them, and re-layouts  26 us (9%)
  other arithmetic  14.9 us (5%)
  matrix products  14.1 us (5%)
    all_to_all x2, blocking collectives, gather_rows(): return lax.all_to_all(copies, 'seq', 0, 0, tiled=True)  52.6 us
    all_to_all x1, waiting for transfers between devices, on_device(): got = lax.all_to_all(payload, 'seq', 0, 0, tiled=True)  49.4 us
    all_to_all x2, waiting for transfers between devices, gather_rows(): return lax.all_to_all(copies, 'seq', 0, 0, tiled=True)  37.9 us
    all_to_all x1, waiting for transfers between devices, on_device(): packed = lax.all_to_all(packed, 'seq', 0, 0, tiled=True)  17.5 us
    ppermute x4, waiting for transfers between devices, head_sum(): other = lax.ppermute(part, 'head', [(i, i ^ stride) for i in range(nhead)])  15.3 us
    all_to_all x2, starting transfers between devices, gather_rows(): return lax.all_to_all(copies, 'seq', 0, 0, tiled=True)  12.4 us
    all_to_all x1, starting transfers between devices, on_device(): got = lax.all_to_all(payload, 'seq', 0, 0, tiled=True)  12.2 us
    all_to_all x1, starting transfers between devices, on_device(): packed = lax.all_to_all(packed, 'seq', 0, 0, tiled=True)  10.1 us
  transfers between devices with their start and end apart: 9, of which 8 were waited for; matrix products, arithmetic and copies ran while one was open for 11% of the time, Pallas kernels for 0%

profile of v12, /device:TPU:4, one launch (start us, length us, event | category | flops | bytes accessed | tf_op | source)
XLA Modules:
  0.0 273.1 jit_solution(10977934923726983122)
XLA Ops:
  0.0 0.8 fusion.89
  2.1 1.4 copy.297
  3.8 2.1 reshape.463
  5.8 1.2 copy.299
  7.7 2.1 pad_maximum_fusion
  9.7 12.2 %all-to-all-start = ((bf16[64,256,64]{1,2,0:T(8,128)(2,1)}), bf16[64,256,64]{1,2,0:T(8,128)(2,1)S(1)}, u32[]{:S(2)}, u32[]{:S(2)}) async-start(bf16[64,256,64]{1,2,0:T(8,128)(2,1)} %pad_maximum_fusion), calls=%async_computation | async-start | bytes 4194304 | tf_op jit(solution)/shard_map/all_to_all | solution.py:225
  23.7 49.4 %all-to-all-done = bf16[64,256,64]{1,2,0:T(8,128)(2,1)S(1)} async-done(((bf16[64,256,64]{1,2,0:T(8,128)(2,1)}), bf16[64,256,64]{1,2,0:T(8,128)(2,1)S(1)}, u32[]{:S(2)}, u32[]{:S(2)}) %all-to-all-start) | async-done | bytes 2097184 | tf_op jit(solution)/shard_map/all_to_all | solution.py:225
  74.6 0.8 fusion.28
  75.5 0.7 broadcast_in_dim.166
  76.2 5.9 %all-to-all-start.1 = ((bf16[64,128,16]{1,2,0:T(8,128)(2,1)}), bf16[64,128,16]{1,2,0:T(8,128)(2,1)S(1)}, u32[]{:S(2)}, u32[]{:S(2)}) async-start(bf16[64,128,16]{1,2,0:T(8,128)(2,1)} %broadcast_in_dim.166), calls=%async_computation.1 | async-start | bytes 524288 | tf_op jit(solution)/shard_map/all_to_all | solution.py:101
  82.3 0.7 gather_fusion.3
  83.1 0.8 select_convert_fusion
  83.8 10.2 %all-to-all-done.1 = bf16[64,128,16]{1,2,0:T(8,128)(2,1)S(1)} async-done(((bf16[64,128,16]{1,2,0:T(8,128)(2,1)}), bf16[64,128,16]{1,2,0:T(8,128)(2,1)S(1)}, u32[]{:S(2)}, u32[]{:S(2)}) %all-to-all-start.1) | async-done | bytes 262176 | tf_op jit(solution)/shard_map/all_to_all | solution.py:101
  94.1 6.5 %all-to-all-start.3 = ((bf16[64,2,2,32]{3,2,1,0:T(2,128)(2,1)}), bf16[64,2,2,32]{3,2,1,0:T(2,128)(2,1)}, u32[]{:S(2)}, u32[]{:S(2)}) async-start(bf16[64,2,2,32]{3,2,1,0:T(2,128)(2,1)} %select_convert_fusion), calls=%async_computation.3 | async-start | bytes 131072 | tf_op jit(solution)/shard_map/all_to_all | solution.py:240
  100.8 0.9 copy.301
  101.8 1.6 gather_fusion.1
  103.5 5.2 %fusion.92 = (f32[2,32,8]{0,2,1:T(8,128)S(1)}, f32[2,32,64,8]{2,0,3,1:T(2,128)}) fusion(f32[8]{0:T(128)S(1)} %copy-done.14, f32[2,32,64]{2,0,1:T(2,128)S(1)} %subtract_convert_fusion, bf16[2,32,8,128]{3,2,0,1:T(8,128)(2,1)S(1)} %select_bitcast_fusion, pred[32,64]{1,0:T(8,128)(4,1)S(1)} %compare_and_fusion, bf16[32,64,1024]{2,1,0:T(8,128)(2,1)} %param.17), kind=kOutput, calls=%fused_computation.172 | convolution fusion | flops 8551936 | bytes 4476960 | tf_op jit(solution)/shard_map/sbhe,bthe->sbth/dot_general | solution.py:38
  109.3 0.7 gather_fusion.2
  110.4 1.6 fusion.70
  112.0 3.5 %fusion.22 = f32[2,32,8,128]{3,0,2,1:T(2,128)S(1)} fusion(f32[2,32,64,8]{2,0,3,1:T(2,128)} %get-tuple-element.35, pred[32,64]{1,0:T(8,128)(4,1)} %copy-done.5, f32[2,32,8]{0,2,1:T(8,128)S(1)} %copy.307, bf16[32,64,1024]{2,1,0:T(8,128)(2,1)} %param.18), kind=kOutput, calls=%fused_computation.30 | convolution fusion | flops 8486912 | bytes 4591616 | tf_op jit(solution)/shard_map/sbth,bthe->sbhe/dot_general | solution.py:62
  116.6 0.7 copy.311
  117.4 1.3 copy.313
  118.6 1.1 copy.312
  120.0 1.1 maximum_bitcast_fusion
  121.1 0.9 pad_maximum_fusion.1
  122.0 10.1 %all-to-all-start.2 = ((f32[64,3,8,128]{3,2,1,0:T(8,128)}), f32[64,3,8,128]{3,2,1,0:T(8,128)S(1)}, u32[]{:S(2)}, u32[]{:S(2)}) async-start(f32[64,3,8,128]{3,2,1,0:T(8,128)} %pad_maximum_fusion.1), calls=%async_computation.2 | async-start | bytes 1572864 | tf_op jit(solution)/shard_map/all_to_all | solution.py:267
  132.7 0.9 copy.318
  134.4 1.8 constant_dynamic-slice_fusion
  136.2 1.1 copy.335
  137.5 17.5 %all-to-all-done.2 = f32[64,3,8,128]{3,2,1,0:T(8,128)S(1)} async-done(((f32[64,3,8,128]{3,2,1,0:T(8,128)}), f32[64,3,8,128]{3,2,1,0:T(8,128)S(1)}, u32[]{:S(2)}, u32[]{:S(2)}) %all-to-all-start.2) | async-done | bytes 786464 | tf_op jit(solution)/shard_map/all_to_all | solution.py:267
  155.1 0.8 fusion.49
  155.8 1.4 copy.315
  157.3 0.7 add_select_fusion
  159.2 18.1 %all_to_all.35 = bf16[64,2,1024]{2,1,0:T(2,128)(2,1)S(1)} all-to-all(bf16[64,2,1024]{2,1,0:T(2,128)(2,1)S(1)} %broadcast_in_dim.181), channel_id=1, replica_groups=mesh['seq'=64,'head'=4] {'seq'}, dimensions={0} | all-to-all | bytes 524288 | tf_op jit(solution)/shard_map/all_to_all | solution.py:101
  177.4 1.1 fusion.93
  178.5 1.3 collective-permute-start
  179.8 2.7 collective-permute-done
  183.0 4.9 %collective-permute-done.1 = f32[128,64]{0,1:T(8,128)S(1)} collective-permute-done((f32[128,64]{0,1:T(8,128)S(1)}, f32[128,64]{0,1:T(8,128)S(1)}, u32[]{:S(2)}, u32[]{:S(2)}) %collective-permute-start.1) | collective-permute-done | bytes 32800 | tf_op jit(solution)/shard_map/ppermute | solution.py:113
  187.9 1.3 broadcast_in_dim.182
  189.2 6.5 %all-to-all-start.5 = ((bf16[64,128,64]{1,2,0:T(8,128)(2,1)}), bf16[64,128,64]{1,2,0:T(8,128)(2,1)}, u32[]{:S(2)}, u32[]{:S(2)}) async-start(bf16[64,128,64]{1,2,0:T(8,128)(2,1)} %broadcast_in_dim.182), calls=%async_computation.5 | async-start | bytes 2097152 | tf_op jit(solution)/shard_map/all_to_all | solution.py:101
  195.8 27.7 %all-to-all-done.5 = bf16[64,128,64]{1,2,0:T(8,128)(2,1)} async-done(((bf16[64,128,64]{1,2,0:T(8,128)(2,1)}), bf16[64,128,64]{1,2,0:T(8,128)(2,1)}, u32[]{:S(2)}, u32[]{:S(2)}) %all-to-all-start.5) | async-done | bytes 1048608 | tf_op jit(solution)/shard_map/all_to_all | solution.py:101
  223.5 1.8 convert_reduce_fusion
  225.3 2.5 fusion.55
  228.0 34.5 %all_to_all.36 = bf16[64,128,64]{1,2,0:T(8,128)(2,1)S(1)} all-to-all(bf16[64,128,64]{1,2,0:T(8,128)(2,1)S(1)} %broadcast_in_dim.183), channel_id=1, replica_groups=mesh['seq'=64,'head'=4] {'seq'}, dimensions={0} | all-to-all | bytes 2097152 | tf_op jit(solution)/shard_map/all_to_all | solution.py:101
  262.9 1.3 collective-permute-start.2
  264.2 2.7 collective-permute-done.2
  267.4 4.9 %collective-permute-done.3 = f32[128,64]{0,1:T(8,128)S(1)} collective-permute-done((f32[128,64]{0,1:T(8,128)S(1)}, f32[128,64]{0,1:T(8,128)S(1)}, u32[]{:S(2)}, u32[]{:S(2)}) %collective-permute-start.3) | collective-permute-done | bytes 32800 | tf_op jit(solution)/shard_map/ppermute | solution.py:113
  272.3 0.7 copy.332
  (122 shorter events, 12.7 us)
Async XLA Ops:
  0.0 262.6 %copy-start = (bf16[64,4096]{1,0:T(8,128)(2,1)S(1)}, bf16[64,4096]{1,0:T(8,128)(2,1)}, u32[]{:S(2)}) copy-start(bf16[64,4096]{1,0:T(8,128)(2,1)} %param.25) | copy-start | bytes 1572868
  0.0 3.7 %copy-start.4 = (bf16[2,64,64]{2,1,0:T(8,128)(2,1)S(1)}, bf16[2,64,64]{2,1,0:T(8,128)(2,1)}, u32[]{:S(2)}) copy-start(bf16[2,64,64]{2,1,0:T(8,128)(2,1)} %param.13) | copy-start | bytes 49156
  9.7 12.3 %copy-start.11 = (s32[32]{0:T(128)S(1)}, s32[32]{0:T(128)}, u32[]{:S(2)}) copy-start(s32[32]{0:T(128)} %param.15) | copy-start | bytes 388
  9.7 12.3 %copy-start.1 = (s32[64]{0:T(128)S(1)}, s32[64]{0:T(128)}, u32[]{:S(2)}) copy-start(s32[64]{0:T(128)} %param.14) | copy-start | bytes 772
  9.7 13.6 %copy-start.13 = (s32[32]{0:T(128)S(1)}, s32[32]{0:T(128)}, u32[]{:S(2)}) copy-start(s32[32]{0:T(128)} %param.16) | copy-start | bytes 388
  9.7 63.4 %all-to-all-start = ((bf16[64,256,64]{1,2,0:T(8,128)(2,1)}), bf16[64,256,64]{1,2,0:T(8,128)(2,1)S(1)}, u32[]{:S(2)}, u32[]{:S(2)}) async-start(bf16[64,256,64]{1,2,0:T(8,128)(2,1)} %pad_maximum_fusion), calls=%async_computation | async-start | bytes 4194304 | tf_op jit(solution)/shard_map/all_to_all | solution.py:225
  22.0 81.3 %copy-start.7 = (pred[32]{0:T(512)(128)(4,1)}, pred[32]{0:T(512)(128)(4,1)S(1)}, u32[]{:S(2)}) copy-start(pred[32]{0:T(512)(128)(4,1)S(1)} %get-tuple-element.20) | copy-start | bytes 100
  22.0 79.7 %copy-start.6 = (s32[1024]{0:T(1024)}, s32[1024]{0:T(1024)S(1)}, u32[]{:S(2)}) copy-start(s32[1024]{0:T(1024)S(1)} %pad_clamp_fusion.1) | copy-start | bytes 12292
  23.5 79.9 %copy-start.5 = (pred[32,64]{1,0:T(8,128)(4,1)}, pred[32,64]{1,0:T(8,128)(4,1)S(1)}, u32[]{:S(2)}) copy-start(pred[32,64]{1,0:T(8,128)(4,1)S(1)} %compare_and_fusion) | copy-start | bytes 6148
  75.5 28.0 %copy-start.14 = (f32[8]{0:T(128)S(1)}, f32[8]{0:T(128)}, u32[]{:S(2)}) copy-start(f32[8]{0:T(128)} %param.19) | copy-start | bytes 100
  76.2 17.9 %all-to-all-start.1 = ((bf16[64,128,16]{1,2,0:T(8,128)(2,1)}), bf16[64,128,16]{1,2,0:T(8,128)(2,1)S(1)}, u32[]{:S(2)}, u32[]{:S(2)}) async-start(bf16[64,128,16]{1,2,0:T(8,128)(2,1)} %broadcast_in_dim.166), calls=%async_computation.1 | async-start | bytes 524288 | tf_op jit(solution)/shard_map/all_to_all | solution.py:101
  94.1 21.5 %copy-start.2 = (bf16[64,128,16]{1,2,0:T(8,128)(2,1)}, bf16[64,128,16]{1,2,0:T(8,128)(2,1)S(1)}, u32[]{:S(2)}) copy-start(bf16[64,128,16]{1,2,0:T(8,128)(2,1)S(1)} %all-to-all-done.1) | copy-start | bytes 786436
  94.1 28.0 %all-to-all-start.3 = ((bf16[64,2,2,32]{3,2,1,0:T(2,128)(2,1)}), bf16[64,2,2,32]{3,2,1,0:T(2,128)(2,1)}, u32[]{:S(2)}, u32[]{:S(2)}) async-start(bf16[64,2,2,32]{3,2,1,0:T(2,128)(2,1)} %select_convert_fusion), calls=%async_computation.3 | async-start | bytes 131072 | tf_op jit(solution)/shard_map/all_to_all | solution.py:240
  103.5 6.6 %copy-start.8 = (pred[32]{0:T(512)(128)(4,1)S(1)}, pred[32]{0:T(512)(128)(4,1)}, u32[]{:S(2)}) copy-start(pred[32]{0:T(512)(128)(4,1)} %copy-done.7) | copy-start | bytes 100
  112.0 3.6 %copy-start.12 = (s32[32]{0:T(128)S(1)}, s32[32]{0:T(128)}, u32[]{:S(2)}) copy-start(s32[32]{0:T(128)} %param.15) | copy-start | bytes 388
  120.0 12.2 %copy-start.15 = (f32[8]{0:T(128)S(1)}, f32[8]{0:T(128)}, u32[]{:S(2)}) copy-start(f32[8]{0:T(128)} %param.19) | copy-start | bytes 100
  122.0 33.0 %all-to-all-start.2 = ((f32[64,3,8,128]{3,2,1,0:T(8,128)}), f32[64,3,8,128]{3,2,1,0:T(8,128)S(1)}, u32[]{:S(2)}, u32[]{:S(2)}) async-start(f32[64,3,8,128]{3,2,1,0:T(8,128)} %pad_maximum_fusion.1), calls=%async_computation.2 | async-start | bytes 1572864 | tf_op jit(solution)/shard_map/all_to_all | solution.py:267
  133.9 23.3 %copy-start.9 = (f32[8]{0:T(128)S(1)}, f32[8]{0:T(128)}, u32[]{:S(2)}) copy-start(f32[8]{0:T(128)} %get-tuple-element.29) | copy-start | bytes 100
  133.9 23.3 %copy-start.10 = (f32[8]{0:T(128)S(1)}, f32[8]{0:T(128)}, u32[]{:S(2)}) copy-start(f32[8]{0:T(128)} %get-tuple-element.30) | copy-start | bytes 100
  177.3 18.5 %copy-start.3 = (f32[4096]{0:T(1024)S(1)}, f32[4096]{0:T(1024)}, u32[]{:S(2)}) copy-start(f32[4096]{0:T(1024)} %get-tuple-element.9) | copy-start | bytes 49156
  178.5 4.0 %collective-permute-start = (f32[128,64]{0,1:T(8,128)S(1)}, f32[128,64]{0,1:T(8,128)S(1)}, u32[]{:S(2)}, u32[]{:S(2)}) collective-permute-start(f32[128,64]{0,1:T(8,128)S(1)} %fusion.93), channel_id=1, source_target_pairs={{0,1},{1,0},{2,3},{3,2},{4,5},{5,4},{6,7},{7,6},{8,9},{9,8},{10,11... | collective-permute-start | bytes 98312 | tf_op jit(solution)/shard_map/ppermute | solution.py:113
  182.5 5.4 %collective-permute-start.1 = (f32[128,64]{0,1:T(8,128)S(1)}, f32[128,64]{0,1:T(8,128)S(1)}, u32[]{:S(2)}, u32[]{:S(2)}) collective-permute-start(f32[128,64]{0,1:T(8,128)S(1)} %add.192), channel_id=1, source_target_pairs={{0,2},{1,3},{2,0},{3,1},{4,6},{5,7},{6,4},{7,5},{8,10},{9,11},{10,... | collective-permute-start | bytes 98312 | tf_op jit(solution)/shard_map/ppermute | solution.py:113
  189.2 34.3 %all-to-all-start.5 = ((bf16[64,128,64]{1,2,0:T(8,128)(2,1)}), bf16[64,128,64]{1,2,0:T(8,128)(2,1)}, u32[]{:S(2)}, u32[]{:S(2)}) async-start(bf16[64,128,64]{1,2,0:T(8,128)(2,1)} %broadcast_in_dim.182), calls=%async_computation.5 | async-start | bytes 2097152 | tf_op jit(solution)/shard_map/all_to_all | solution.py:101
  262.9 4.0 %collective-permute-start.2 = (f32[128,64]{0,1:T(8,128)S(1)}, f32[128,64]{0,1:T(8,128)S(1)}, u32[]{:S(2)}, u32[]{:S(2)}) collective-permute-start(f32[128,64]{0,1:T(8,128)S(1)} %fusion.94), channel_id=1, source_target_pairs={{0,1},{1,0},{2,3},{3,2},{4,5},{5,4},{6,7},{7,6},{8,9},{9,8},{10,11... | collective-permute-start | bytes 98312 | tf_op jit(solution)/shard_map/ppermute | solution.py:113
  266.9 5.4 %collective-permute-start.3 = (f32[128,64]{0,1:T(8,128)S(1)}, f32[128,64]{0,1:T(8,128)S(1)}, u32[]{:S(2)}, u32[]{:S(2)}) collective-permute-start(f32[128,64]{0,1:T(8,128)S(1)} %add.196), channel_id=1, source_target_pairs={{0,2},{1,3},{2,0},{3,1},{4,6},{5,7},{6,4},{7,5},{8,10},{9,11},{10,... | collective-permute-start | bytes 98312 | tf_op jit(solution)/shard_map/ppermute | solution.py:113

commit v13 on v12

--- a/solution.py
+++ b/solution.py
@@ -231,13 +231,19 @@
     gains = (pieces[0:2] + pieces[2:4]) + pieces[4:6]
     normed = full_normalize(gathered, gains[0])
     qkv_part = jnp.dot(normed, qkv_cols, preferred_element_type=jnp.float32).astype(jnp.bfloat16)
-    all_queries = gather_cols(qkv_part[:, :split], nseq).reshape(nsteps, requests, nheads, head_size)
     kv_part = qkv_part[:, split:].astype(jnp.float32)
     own_rows = rows // nseq
     req_blocks = requests // own_rows
     kv_by_block = kv_part.reshape(nsteps, req_blocks, own_rows, 2 * split)
     kv_dest = jnp.take(kv_by_block, jnp.arange(nseq) % req_blocks, axis=1)
-    kv_got = lax.all_to_all(jnp.swapaxes(kv_dest, 0, 1).astype(jnp.bfloat16), "seq", 0, 0, tiled=True)
+    q_part = qkv_part[:, :split]
+    kv_flat = jnp.swapaxes(kv_dest, 0, 1).astype(jnp.bfloat16).reshape(nseq, -1, split)
+    q_payload = jnp.concatenate(
+        [jnp.broadcast_to(q_part[None], (nseq,) + q_part.shape), kv_flat], axis=1
+    )
+    q_got = lax.all_to_all(q_payload, "seq", 0, 0, tiled=True)
+    all_queries = jnp.moveaxis(q_got[:, :rows], 0, -2).reshape(nsteps, requests, nheads, head_size)
+    kv_got = q_got[:, rows:].reshape(nseq, nsteps, own_rows, 2 * split)
     kv_got = jnp.transpose(kv_got, (1, 2, 0, 3))
     key_rows = kv_got[..., :split].reshape(nsteps, own_rows, nheads, head_size)
     value_rows = kv_got[..., split:].reshape(nsteps, own_rows, nheads, head_size)

time: 274 us -> 276 us (level)
  starting transfers between devices: 44.8 us -> 34.9 us
  other arithmetic: 14.9 us -> 22.1 us
  local copies, waits for them, and re-layouts: 26 us -> 29.8 us
    all_to_all x1, waiting for transfers between devices: 0.01 us -> 14.8 us  [on_device(): q_got = lax.all_to_all(q_payload, 'seq', 0, 0, tiled=True)]
    all_to_all x2 -> x1, waiting for transfers between devices: 37.9 us -> 27.7 us  [gather_rows(): return lax.all_to_all(copies, 'seq', 0, 0, tiled=True)]
    all_to_all x2 -> x1, starting transfers between devices: 12.4 us -> 6.51 us  [gather_rows(): return lax.all_to_all(copies, 'seq', 0, 0, tiled=True)]
    slice x1 -> x4, local copies, waits for them, and re-layouts: 0.01 us -> 3.77 us  [the longest x2 2.9 us: on_device(): kv_got = q_got[:, rows:].reshape(nseq, nsteps, own_rows, 2 * split)]
    all_to_all x1, starting transfers between devices: 10.1 us -> 6.53 us  [on_device(): packed = lax.all_to_all(packed, 'seq', 0, 0, tiled=True)]
    all_to_all x1, waiting for transfers between devices: 17.5 us -> 14.2 us  [on_device(): packed = lax.all_to_all(packed, 'seq', 0, 0, tiled=True)]
  transfers between devices with their start and end apart: 9 -> 8, of which waited for: 8 -> 8; matrix products, arithmetic and copies ran while one was open for 11% -> 5% of each run, Pallas kernels for 0% -> 0%
where the time goes in v13:
time: 276 us; the launch traced here: 275 us
  waiting for transfers between devices  121 us (44%)
  blocking collectives  52.6 us (19%)
  starting transfers between devices  34.9 us (13%)
  local copies, waits for them, and re-layouts  29.8 us (11%)
  other arithmetic  22.1 us (8%)
  matrix products  14.2 us (5%)
    all_to_all x2, blocking collectives, gather_rows(): return lax.all_to_all(copies, 'seq', 0, 0, tiled=True)  52.6 us
    all_to_all x1, waiting for transfers between devices, on_device(): got = lax.all_to_all(payload, 'seq', 0, 0, tiled=True)  49.1 us
    all_to_all x1, waiting for transfers between devices, gather_rows(): return lax.all_to_all(copies, 'seq', 0, 0, tiled=True)  27.7 us
    ppermute x4, waiting for transfers between devices, head_sum(): other = lax.ppermute(part, 'head', [(i, i ^ stride) for i in range(nhead)])  15.3 us
    all_to_all x1, waiting for transfers between devices, on_device(): q_got = lax.all_to_all(q_payload, 'seq', 0, 0, tiled=True)  14.8 us
    all_to_all x1, waiting for transfers between devices, on_device(): packed = lax.all_to_all(packed, 'seq', 0, 0, tiled=True)  14.2 us
    all_to_all x1, starting transfers between devices, on_device(): got = lax.all_to_all(payload, 'seq', 0, 0, tiled=True)  12.2 us
    all_to_all x1, starting transfers between devices, on_device(): packed = lax.all_to_all(packed, 'seq', 0, 0, tiled=True)  6.53 us
  transfers between devices with their start and end apart: 8, of which 8 were waited for; matrix products, arithmetic and copies ran while one was open for 5% of the time, Pallas kernels for 0%

profile of v13, /device:TPU:4, one launch (start us, length us, event | category | flops | bytes accessed | tf_op | source)
XLA Modules:
  0.0 275.1 jit_solution(2898130649353317148)
XLA Ops:
  2.1 1.4 copy.316
  3.8 2.1 reshape.472
  5.8 1.2 copy.318
  7.7 2.1 pad_maximum_fusion
  9.7 12.2 %all-to-all-start = ((bf16[64,256,64]{1,2,0:T(8,128)(2,1)}), bf16[64,256,64]{1,2,0:T(8,128)(2,1)S(1)}, u32[]{:S(2)}, u32[]{:S(2)}) async-start(bf16[64,256,64]{1,2,0:T(8,128)(2,1)} %pad_maximum_fusion), calls=%async_computation | async-start | bytes 4194304 | tf_op jit(solution)/shard_map/all_to_all | solution.py:225
  24.0 49.1 %all-to-all-done = bf16[64,256,64]{1,2,0:T(8,128)(2,1)S(1)} async-done(((bf16[64,256,64]{1,2,0:T(8,128)(2,1)}), bf16[64,256,64]{1,2,0:T(8,128)(2,1)S(1)}, u32[]{:S(2)}, u32[]{:S(2)}) %all-to-all-start) | async-done | bytes 2097184 | tf_op jit(solution)/shard_map/all_to_all | solution.py:225
  74.6 0.8 fusion.28
  76.8 0.9 pad_maximum_fusion.2
  77.7 6.1 %all-to-all-start.1 = ((bf16[64,136,16]{1,2,0:T(8,128)(2,1)}), bf16[64,136,16]{1,2,0:T(8,128)(2,1)S(1)}, u32[]{:S(2)}, u32[]{:S(2)}) async-start(bf16[64,136,16]{1,2,0:T(8,128)(2,1)} %pad_maximum_fusion.2), calls=%async_computation.1 | async-start | bytes 1048576 | tf_op jit(solution)/shard_map/all_to_all | solution.py:244
  85.9 14.8 %all-to-all-done.1 = bf16[64,136,16]{1,2,0:T(8,128)(2,1)S(1)} async-done(((bf16[64,136,16]{1,2,0:T(8,128)(2,1)}), bf16[64,136,16]{1,2,0:T(8,128)(2,1)S(1)}, u32[]{:S(2)}, u32[]{:S(2)}) %all-to-all-start.1) | async-done | bytes 278560 | tf_op jit(solution)/shard_map/all_to_all | solution.py:244
  100.7 0.9 fusion.92
  101.5 1.0 reshape.476
  102.6 1.4 copy.323
  105.4 4.6 %fusion.93 = (f32[2,32,8]{0,2,1:T(8,128)S(1)}, f32[2,32,64,8]{2,0,3,1:T(2,128)S(1)}) fusion(f32[8]{0:T(128)} %param.19, f32[2,32,64]{2,0,1:T(2,128)} %subtract_convert_fusion, bf16[2,32,8,128]{3,2,0,1:T(8,128)(2,1)S(1)} %select_bitcast_fusion, pred[32,64]{1,0:T(8,128)(4,1)} %compare_and_fusion, bf16[32,64,1024]{2,1,0:T(8,128)(2,1)} %param.17), kind=kOutput, calls=%fused_computation.175 | convolution fusion | flops 8551936 | bytes 4476960 | tf_op jit(solution)/shard_map/sbhe,bthe->sbth/dot_general | solution.py:38
  110.3 0.8 select_reduce_fusion
  113.0 2.0 fusion.70
  115.0 3.4 %fusion.22 = f32[2,32,8,128]{3,0,2,1:T(2,128)S(1)} fusion(f32[2,32,64,8]{2,0,3,1:T(2,128)S(1)} %get-tuple-element.37, pred[32,64]{1,0:T(8,128)(4,1)} %compare_and_fusion, f32[2,32,8]{0,2,1:T(8,128)S(1)} %copy.329, bf16[32,64,1024]{2,1,0:T(8,128)(2,1)} %param.18), kind=kOutput, calls=%fused_computation.30 | convolution fusion | flops 8486912 | bytes 4591616 | tf_op jit(solution)/shard_map/sbth,bthe->sbhe/dot_general | solution.py:62
  119.0 0.9 copy.359
  120.0 1.0 copy.332
  121.0 0.9 fusion.29
  122.5 1.2 copy.334
  123.6 1.2 broadcast_add_fusion
  124.9 1.1 maximum_bitcast_fusion
  126.0 0.9 pad_maximum_fusion.1
  126.9 6.5 %all-to-all-start.2 = ((f32[64,3,8,128]{3,2,1,0:T(8,128)}), f32[64,3,8,128]{3,2,1,0:T(8,128)S(1)}, u32[]{:S(2)}, u32[]{:S(2)}) async-start(f32[64,3,8,128]{3,2,1,0:T(8,128)} %pad_maximum_fusion.1), calls=%async_computation.2 | async-start | bytes 1572864 | tf_op jit(solution)/shard_map/all_to_all | solution.py:273
  134.1 1.8 constant_dynamic-slice_fusion
  135.9 1.7 copy.356
  137.5 1.7 slice.113
  139.2 1.2 copy.339
  140.8 0.8 fusion.72
  142.1 14.2 %all-to-all-done.2 = f32[64,3,8,128]{3,2,1,0:T(8,128)S(1)} async-done(((f32[64,3,8,128]{3,2,1,0:T(8,128)}), f32[64,3,8,128]{3,2,1,0:T(8,128)S(1)}, u32[]{:S(2)}, u32[]{:S(2)}) %all-to-all-start.2) | async-done | bytes 786464 | tf_op jit(solution)/shard_map/all_to_all | solution.py:273
  156.4 0.8 fusion.49
  157.1 1.4 copy.337
  158.5 0.8 fusion.87
  161.3 18.1 %all_to_all.30 = bf16[64,2,1024]{2,1,0:T(2,128)(2,1)S(1)} all-to-all(bf16[64,2,1024]{2,1,0:T(2,128)(2,1)S(1)} %broadcast_in_dim.181), channel_id=1, replica_groups=mesh['seq'=64,'head'=4] {'seq'}, dimensions={0} | all-to-all | bytes 524288 | tf_op jit(solution)/shard_map/all_to_all | solution.py:101
  179.4 1.1 fusion.94
  180.5 1.3 collective-permute-start
  181.8 2.7 collective-permute-done
  185.0 4.9 %collective-permute-done.1 = f32[128,64]{0,1:T(8,128)S(1)} collective-permute-done((f32[128,64]{0,1:T(8,128)S(1)}, f32[128,64]{0,1:T(8,128)S(1)}, u32[]{:S(2)}, u32[]{:S(2)}) %collective-permute-start.1) | collective-permute-done | bytes 32800 | tf_op jit(solution)/shard_map/ppermute | solution.py:113
  190.0 1.3 broadcast_in_dim.182
  191.3 6.5 %all-to-all-start.4 = ((bf16[64,128,64]{1,2,0:T(8,128)(2,1)}), bf16[64,128,64]{1,2,0:T(8,128)(2,1)}, u32[]{:S(2)}, u32[]{:S(2)}) async-start(bf16[64,128,64]{1,2,0:T(8,128)(2,1)} %broadcast_in_dim.182), calls=%async_computation.4 | async-start | bytes 2097152 | tf_op jit(solution)/shard_map/all_to_all | solution.py:101
  197.9 27.7 %all-to-all-done.4 = bf16[64,128,64]{1,2,0:T(8,128)(2,1)} async-done(((bf16[64,128,64]{1,2,0:T(8,128)(2,1)}), bf16[64,128,64]{1,2,0:T(8,128)(2,1)}, u32[]{:S(2)}, u32[]{:S(2)}) %all-to-all-start.4) | async-done | bytes 1048608 | tf_op jit(solution)/shard_map/all_to_all | solution.py:101
  225.5 1.8 convert_reduce_fusion
  227.3 2.5 fusion.55
  230.1 34.5 %all_to_all.31 = bf16[64,128,64]{1,2,0:T(8,128)(2,1)S(1)} all-to-all(bf16[64,128,64]{1,2,0:T(8,128)(2,1)S(1)} %broadcast_in_dim.183), channel_id=1, replica_groups=mesh['seq'=64,'head'=4] {'seq'}, dimensions={0} | all-to-all | bytes 2097152 | tf_op jit(solution)/shard_map/all_to_all | solution.py:101
  264.9 1.3 collective-permute-start.2
  266.2 2.7 collective-permute-done.2
  269.4 4.9 %collective-permute-done.3 = f32[128,64]{0,1:T(8,128)S(1)} collective-permute-done((f32[128,64]{0,1:T(8,128)S(1)}, f32[128,64]{0,1:T(8,128)S(1)}, u32[]{:S(2)}, u32[]{:S(2)}) %collective-permute-start.3) | collective-permute-done | bytes 32800 | tf_op jit(solution)/shard_map/ppermute | solution.py:113
  (115 shorter events, 20.4 us)
Async XLA Ops:
  0.0 264.6 %copy-start = (bf16[64,4096]{1,0:T(8,128)(2,1)S(1)}, bf16[64,4096]{1,0:T(8,128)(2,1)}, u32[]{:S(2)}) copy-start(bf16[64,4096]{1,0:T(8,128)(2,1)} %param.25) | copy-start | bytes 1572868
  0.0 3.7 %copy-start.4 = (bf16[2,64,64]{2,1,0:T(8,128)(2,1)S(1)}, bf16[2,64,64]{2,1,0:T(8,128)(2,1)}, u32[]{:S(2)}) copy-start(bf16[2,64,64]{2,1,0:T(8,128)(2,1)} %param.13) | copy-start | bytes 49156
  9.7 12.3 %copy-start.7 = (s32[32]{0:T(128)S(1)}, s32[32]{0:T(128)}, u32[]{:S(2)}) copy-start(s32[32]{0:T(128)} %param.15) | copy-start | bytes 388
  9.7 12.8 %copy-start.1 = (s32[64]{0:T(128)S(1)}, s32[64]{0:T(128)}, u32[]{:S(2)}) copy-start(s32[64]{0:T(128)} %param.14) | copy-start | bytes 772
  9.7 13.5 %copy-start.9 = (s32[32]{0:T(128)S(1)}, s32[32]{0:T(128)}, u32[]{:S(2)}) copy-start(s32[32]{0:T(128)} %param.16) | copy-start | bytes 388
  9.7 63.4 %all-to-all-start = ((bf16[64,256,64]{1,2,0:T(8,128)(2,1)}), bf16[64,256,64]{1,2,0:T(8,128)(2,1)S(1)}, u32[]{:S(2)}, u32[]{:S(2)}) async-start(bf16[64,256,64]{1,2,0:T(8,128)(2,1)} %pad_maximum_fusion), calls=%async_computation | async-start | bytes 4194304 | tf_op jit(solution)/shard_map/all_to_all | solution.py:225
  22.5 50.8 %copy-start.6 = (s32[1024]{0:T(1024)}, s32[1024]{0:T(1024)S(1)}, u32[]{:S(2)}) copy-start(s32[1024]{0:T(1024)S(1)} %pad_clamp_fusion.1) | copy-start | bytes 12292
  77.7 22.9 %all-to-all-start.1 = ((bf16[64,136,16]{1,2,0:T(8,128)(2,1)}), bf16[64,136,16]{1,2,0:T(8,128)(2,1)S(1)}, u32[]{:S(2)}, u32[]{:S(2)}) async-start(bf16[64,136,16]{1,2,0:T(8,128)(2,1)} %pad_maximum_fusion.2), calls=%async_computation.1 | async-start | bytes 1048576 | tf_op jit(solution)/shard_map/all_to_all | solution.py:244
  100.7 9.3 %copy-start.2 = (bf16[64,136,16]{1,2,0:T(8,128)(2,1)}, bf16[64,136,16]{1,2,0:T(8,128)(2,1)S(1)}, u32[]{:S(2)}) copy-start(bf16[64,136,16]{1,2,0:T(8,128)(2,1)S(1)} %all-to-all-done.1) | copy-start | bytes 835588
  111.1 1.0 copy-start.5
  115.0 3.5 %copy-start.8 = (s32[32]{0:T(128)S(1)}, s32[32]{0:T(128)}, u32[]{:S(2)}) copy-start(s32[32]{0:T(128)} %param.15) | copy-start | bytes 388
  124.9 8.6 %copy-start.10 = (f32[8]{0:T(128)S(1)}, f32[8]{0:T(128)}, u32[]{:S(2)}) copy-start(f32[8]{0:T(128)} %param.19) | copy-start | bytes 100
  126.9 29.4 %all-to-all-start.2 = ((f32[64,3,8,128]{3,2,1,0:T(8,128)}), f32[64,3,8,128]{3,2,1,0:T(8,128)S(1)}, u32[]{:S(2)}, u32[]{:S(2)}) async-start(f32[64,3,8,128]{3,2,1,0:T(8,128)} %pad_maximum_fusion.1), calls=%async_computation.2 | async-start | bytes 1572864 | tf_op jit(solution)/shard_map/all_to_all | solution.py:273
  179.3 18.5 %copy-start.3 = (f32[4096]{0:T(1024)S(1)}, f32[4096]{0:T(1024)}, u32[]{:S(2)}) copy-start(f32[4096]{0:T(1024)} %get-tuple-element.9) | copy-start | bytes 49156
  180.5 4.0 %collective-permute-start = (f32[128,64]{0,1:T(8,128)S(1)}, f32[128,64]{0,1:T(8,128)S(1)}, u32[]{:S(2)}, u32[]{:S(2)}) collective-permute-start(f32[128,64]{0,1:T(8,128)S(1)} %fusion.94), channel_id=1, source_target_pairs={{0,1},{1,0},{2,3},{3,2},{4,5},{5,4},{6,7},{7,6},{8,9},{9,8},{10,11... | collective-permute-start | bytes 98312 | tf_op jit(solution)/shard_map/ppermute | solution.py:113
  184.5 5.4 %collective-permute-start.1 = (f32[128,64]{0,1:T(8,128)S(1)}, f32[128,64]{0,1:T(8,128)S(1)}, u32[]{:S(2)}, u32[]{:S(2)}) collective-permute-start(f32[128,64]{0,1:T(8,128)S(1)} %add.192), channel_id=1, source_target_pairs={{0,2},{1,3},{2,0},{3,1},{4,6},{5,7},{6,4},{7,5},{8,10},{9,11},{10,... | collective-permute-start | bytes 98312 | tf_op jit(solution)/shard_map/ppermute | solution.py:113
  191.3 34.3 %all-to-all-start.4 = ((bf16[64,128,64]{1,2,0:T(8,128)(2,1)}), bf16[64,128,64]{1,2,0:T(8,128)(2,1)}, u32[]{:S(2)}, u32[]{:S(2)}) async-start(bf16[64,128,64]{1,2,0:T(8,128)(2,1)} %broadcast_in_dim.182), calls=%async_computation.4 | async-start | bytes 2097152 | tf_op jit(solution)/shard_map/all_to_all | solution.py:101
  264.9 4.0 %collective-permute-start.2 = (f32[128,64]{0,1:T(8,128)S(1)}, f32[128,64]{0,1:T(8,128)S(1)}, u32[]{:S(2)}, u32[]{:S(2)}) collective-permute-start(f32[128,64]{0,1:T(8,128)S(1)} %fusion.95), channel_id=1, source_target_pairs={{0,1},{1,0},{2,3},{3,2},{4,5},{5,4},{6,7},{7,6},{8,9},{9,8},{10,11... | collective-permute-start | bytes 98312 | tf_op jit(solution)/shard_map/ppermute | solution.py:113
  268.9 5.4 %collective-permute-start.3 = (f32[128,64]{0,1:T(8,128)S(1)}, f32[128,64]{0,1:T(8,128)S(1)}, u32[]{:S(2)}, u32[]{:S(2)}) collective-permute-start(f32[128,64]{0,1:T(8,128)S(1)} %add.196), channel_id=1, source_target_pairs={{0,2},{1,3},{2,0},{3,1},{4,6},{5,7},{6,4},{7,5},{8,10},{9,11},{10,... | collective-permute-start | bytes 98312 | tf_op jit(solution)/shard_map/ppermute | solution.py:113
